TPU v7x, 512 devices: a whole 4x8x8 slice. The times are simulated.
512 devices in a mesh: group: 16 (over x_lo, z), row: 32 (over x_hi, y, core).
Axes of the slice: x: 4 (x_hi: 2, x_lo: 2; x = x_hi * 2 + x_lo), y: 8, z: 8, core: 2. Of those that a mesh axis runs over, the one named last changes fastest.
Arguments:
- features: float32 [98304, 2048], P('row', 'group'), may hold values from -6 to 6
- feature_id: int32 [2048], P('group'), may hold values from 0 to 2047, each once
- feature_shift: float32 [2048], replicated, may hold values from -3 to 3
- feature_scale: float32 [2048], replicated, may hold values from 0.25 to 2
- proj_weight: bfloat16 [2048, 256], P('group'), may hold values from -0.5 to 0.5
- row_slot: int32 [32, 3072], P('row'), may hold values from 0 to 3071, each once within a row
- down_weight: bfloat16 [2, 4096, 128], P(None, 'row'), may hold values from -0.09375 to 0.09375
- up_weight: bfloat16 [2, 4096, 128], P(None, 'row'), may hold values from -0.5 to 0.5
- cross_bias: float32 [2, 4096], replicated, may hold values from -3 to 3
- head_weight: float32 [4096], replicated, may hold values from -0.09375 to 0.09375
- labels: int32 [98304], P(('group', 'row')), may hold values 0 or 1
Outputs:
- logits: float32 [98304], P(('group', 'row'))
- grad_down: float32 [2, 4096, 128], P(None, 'row')
- grad_up: float32 [2, 4096, 128], P(None, 'row')
- grad_bias: float32 [2, 4096], replicated
- grad_proj: float32 [2048, 256], P('group')
Inputs may be any that keep to these rules, and one draw needn't show every extreme that they name: Each row of row_slot holds every number 0 .. 3071 once. feature_id holds every number 0 .. 2047 once.
All inputs are finite; a program needn't handle non-finite values. No bound on the sum of `labels` on one device may be relied on, other than what follows from the above.
Results may differ from a plain program's by a relative error of at most 0.02.
Values may be sent and summed in bfloat16 or wider, within the bound.
No kernel may reach another device: no remote copies, remote signals or barrier semaphores. Data moves between devices by JAX's collectives and lax.ppermute only.
A program may use at most 64 MiB of HBM per device.

v0:
```python
import jax
import jax.numpy as jnp
from jax import lax
from jax.sharding import PartitionSpec as P


def column_table(feature_id, lookup_table):
    columns = jnp.arange(lookup_table.shape[0], dtype=jnp.int32)
    picker = (feature_id[:, None] == columns[None, :]).astype(jnp.float32)
    return jnp.dot(picker, lookup_table, precision=lax.Precision.HIGHEST)


def body(
    features,
    feature_id,
    feature_shift,
    feature_scale,
    proj_weight,
    row_slot,
    down_weight,
    up_weight,
    cross_bias,
    head_weight,
    labels,
):
    layers = down_weight.shape[0]
    groups = lax.axis_size("group")
    row_count = labels.shape[0]
    feature_stats = column_table(feature_id, jnp.stack([feature_shift, feature_scale], axis=1))
    normed = ((features - feature_stats[:, 0][None, :]) * feature_stats[:, 1][None, :]).astype(
        jnp.bfloat16
    )
    ordered = jnp.zeros_like(normed).at[row_slot[0]].set(normed)
    projected = jnp.dot(ordered, proj_weight, preferred_element_type=jnp.float32).astype(
        jnp.bfloat16
    )
    first = lax.all_to_all(projected, "group", split_axis=0, concat_axis=1, tiled=True)
    first_wide = first.astype(jnp.float32)
    crossed = first
    stored = []
    for layer_index in range(layers):
        down_full, up_full = (
            lax.all_gather(down_weight[layer_index], "row", axis=0, tiled=True),
            lax.all_gather(up_weight[layer_index], "row", axis=0, tiled=True),
        )
        hidden = jnp.dot(crossed, down_full, preferred_element_type=jnp.float32).astype(
            jnp.bfloat16
        )
        mixture = lax.dot_general(
            hidden, up_full, (((1,), (1,)), ((), ())), preferred_element_type=jnp.float32
        )
        mixture = mixture + cross_bias[layer_index][None, :]
        stored.append((crossed, hidden, mixture, down_full, up_full))
        crossed = (first_wide * mixture + crossed.astype(jnp.float32)).astype(jnp.bfloat16)
    logits = jnp.sum(crossed.astype(jnp.float32) * head_weight[None, :], axis=1)
    total_rows = row_count * groups * lax.axis_size("row")
    loss_scale = 2.0 * (crossed.shape[1] / total_rows) ** 0.5
    logit_grad = (jax.nn.sigmoid(logits) - labels.astype(jnp.float32)) * loss_scale
    back = (logit_grad[:, None] * head_weight[None, :]).astype(jnp.bfloat16)
    first_grad = jnp.zeros(first.shape, jnp.float32)
    up_parts = [None] * layers
    down_parts = [None] * layers
    bias_terms = [None] * layers
    for layer_index in reversed(range(layers)):
        crossed_in, hidden, mixture, down_full, up_full = stored[layer_index]
        back_wide = back.astype(jnp.float32)
        first_grad = first_grad + back_wide * mixture
        mix_grad = (back_wide * first_wide).astype(jnp.bfloat16)
        up_term = lax.dot_general(
            mix_grad, hidden, (((0,), (0,)), ((), ())), preferred_element_type=jnp.float32
        )
        bias_terms[layer_index] = jnp.sum(mix_grad.astype(jnp.float32), axis=0)
        hidden_grad = jnp.dot(mix_grad, up_full, preferred_element_type=jnp.float32).astype(
            jnp.bfloat16
        )
        down_term = lax.dot_general(
            crossed_in, hidden_grad, (((0,), (0,)), ((), ())), preferred_element_type=jnp.float32
        )
        through = lax.dot_general(
            hidden_grad, down_full, (((1,), (1,)), ((), ())), preferred_element_type=jnp.float32
        )
        back = (back_wide + through).astype(jnp.bfloat16)
        up_parts[layer_index] = up_term
        down_parts[layer_index] = down_term
    up_rows, down_rows = (
        lax.psum_scatter(
            jnp.stack(up_parts).astype(jnp.bfloat16), "row", scatter_dimension=1, tiled=True
        ).astype(jnp.float32),
        lax.psum_scatter(
            jnp.stack(down_parts).astype(jnp.bfloat16), "row", scatter_dimension=1, tiled=True
        ).astype(jnp.float32),
    )
    first_grad = (first_grad + back.astype(jnp.float32)).astype(jnp.bfloat16)
    owner_grad = lax.all_to_all(first_grad, "group", split_axis=1, concat_axis=0, tiled=True)
    proj_term = lax.dot_general(
        ordered, owner_grad, (((0,), (0,)), ((), ())), preferred_element_type=jnp.float32
    )
    grad_proj, bias_rows = (
        lax.psum(proj_term.astype(jnp.bfloat16), "row").astype(jnp.float32),
        lax.psum(jnp.stack(bias_terms).astype(jnp.bfloat16), "row").astype(jnp.float32),
    )
    grad_up, grad_down, grad_bias = (
        lax.psum(up_rows.astype(jnp.bfloat16), "group").astype(jnp.float32),
        lax.psum(down_rows.astype(jnp.bfloat16), "group").astype(jnp.float32),
        lax.psum(bias_rows.astype(jnp.bfloat16), "group").astype(jnp.float32),
    )
    return (logits, grad_down, grad_up, grad_bias, grad_proj)


def solution(mesh):
    in_specs = (
        P("row", "group"),
        P("group"),
        P(),
        P(),
        P("group", None),
        P("row", None),
        P(None, "row", None),
        P(None, "row", None),
        P(),
        P(),
        P(("group", "row")),
    )
    out_specs = (
        P(("group", "row")),
        P(None, "row", None),
        P(None, "row", None),
        P(),
        P("group", None),
    )
    return jax.shard_map(body, mesh=mesh, in_specs=in_specs, out_specs=out_specs, check_vma=False)
```

profile of v0, /device:TPU:40, one launch (start us, length us, event | category | flops | bytes accessed | tf_op | source)
XLA Modules:
  0.0 1006.8 jit_solution(14008433392692285830)
XLA Ops:
  13.0 8.9 scatter_custom_fusion
  21.9 1.7 convolution_convert_fusion.4
  23.6 11.5 %all-to-all-start = ((bf16[16,192,256]{2,1,0:T(8,128)(2,1)}), bf16[16,192,256]{2,1,0:T(8,128)(2,1)S(1)}, u32[]{:S(2)}, u32[]{:S(2)}) async-start(bf16[16,192,256]{2,1,0:T(8,128)(2,1)} %bitcast.88), calls=%async_computation | async-start | bytes 3145728 | tf_op jit(solution)/shard_map/all_to_all | solution.py:37
  35.8 37.5 %all-to-all-done = bf16[16,192,256]{2,1,0:T(8,128)(2,1)S(1)} async-done(((bf16[16,192,256]{2,1,0:T(8,128)(2,1)}), bf16[16,192,256]{2,1,0:T(8,128)(2,1)S(1)}, u32[]{:S(2)}, u32[]{:S(2)}) %all-to-all-start) | async-done | bytes 1572896 | tf_op jit(solution)/shard_map/all_to_all | solution.py:37
  73.5 23.1 %all-gather.9.cloned.1.call-done = bf16[1,4096,128]{2,1,0:T(8,128)(2,1)} async-done(((bf16[1,128,128]{2,1,0:T(8,128)(2,1)}), bf16[1,4096,128]{2,1,0:T(8,128)(2,1)}) %all-gather.9.cloned.1.call-update) | async-done | bytes 1048592 | tf_op jit(solution)/shard_map/all_gather | solution.py:43
  96.5 1.8 convolution_convert_fusion.9
  98.3 82.0 %all-gather.11.cloned.1.call-done = bf16[1,4096,128]{2,1,0:T(8,128)(2,1)} async-done(((bf16[1,128,128]{2,1,0:T(8,128)(2,1)}), bf16[1,4096,128]{2,1,0:T(8,128)(2,1)}) %all-gather.11.cloned.1.call-update) | async-done | bytes 1048592 | tf_op jit(solution)/shard_map/all_gather | solution.py:44
  180.4 3.5 fusion.11
  183.9 80.4 %all-gather.13.cloned.1.call-done = bf16[1,4096,128]{2,1,0:T(8,128)(2,1)} async-done(((bf16[1,128,128]{2,1,0:T(8,128)(2,1)}), bf16[1,4096,128]{2,1,0:T(8,128)(2,1)}) %all-gather.13.cloned.1.call-update) | async-done | bytes 1048592 | tf_op jit(solution)/shard_map/all_gather | solution.py:43
  264.3 1.8 convolution_convert_fusion.8
  266.1 82.0 %all-gather.15.cloned.1.call-done = bf16[1,4096,128]{2,1,0:T(8,128)(2,1)} async-done(((bf16[1,128,128]{2,1,0:T(8,128)(2,1)}), bf16[1,4096,128]{2,1,0:T(8,128)(2,1)}) %all-gather.15.cloned.1.call-update) | async-done | bytes 1048592 | tf_op jit(solution)/shard_map/all_gather | solution.py:44
  348.0 3.9 multiply_reduce_fusion
  353.9 2.5 fusion.38
  359.3 4.9 fusion.5
  365.5 7.6 all-to-all-start.1
  375.0 1.5 pad_maximum_fusion.1
  376.6 35.0 %all-to-all-done.1 = bf16[192,16,256]{2,0,1:T(8,128)(2,1)} async-done(((bf16[192,16,256]{2,0,1:T(8,128)(2,1)}), bf16[192,16,256]{2,0,1:T(8,128)(2,1)}, u32[]{:S(2)}, u32[]{:S(2)}) %all-to-all-start.1) | async-done | bytes 1572896 | tf_op jit(solution)/shard_map/all_to_all | solution.py:94
  411.6 2.5 convolution_convert_fusion.5
  414.8 69.3 %reduce-scatter.3.cloned.1.call-done = bf16[2,128,128]{2,1,0:T(8,128)(2,1)} async-done(((bf16[2,4096,128]{2,1,0:T(8,128)(2,1)}), bf16[2,128,128]{2,1,0:T(8,128)(2,1)}) %reduce-scatter.3.cloned.1.call-update) | async-done | bytes 65552 | tf_op jit(solution)/shard_map/reduce_scatter | solution.py:89
  484.1 131.0 %reduce-scatter.5.cloned.1.call-done = bf16[2,128,128]{2,1,0:T(8,128)(2,1)} async-done(((bf16[2,4096,128]{2,1,0:T(8,128)(2,1)}), bf16[2,128,128]{2,1,0:T(8,128)(2,1)}) %reduce-scatter.5.cloned.1.call-update) | async-done | bytes 65552 | tf_op jit(solution)/shard_map/reduce_scatter | solution.py:86
  615.2 113.0 %psum.37 = bf16[2,4096]{1,0:T(2,128)(2,1)S(1)} all-reduce(bf16[2,4096]{1,0:T(2,128)(2,1)S(1)} %pad_maximum_fusion.2), channel_id=1, replica_groups=mesh['group'=16,'row'=32] {'row'}, use_global_device_ids=true, to_apply=%region_8.0 | all-reduce | flops 8192 | bytes 32768 | tf_op jit(solution)/shard_map/psum | solution.py:100
  728.2 63.2 %psum.38 = bf16[2,4096]{1,0:T(2,128)(2,1)S(1)} all-reduce(bf16[2,4096]{1,0:T(2,128)(2,1)S(1)} %psum.37), channel_id=1, replica_groups=mesh['group'=16,'row'=32] {'group'}, use_global_device_ids=true, to_apply=%region_9.0 | all-reduce | flops 8192 | bytes 32768 | tf_op jit(solution)/shard_map/psum | solution.py:105
  792.0 58.7 %all-reduce.4.cloned.1.call-done = bf16[128,256]{1,0:T(8,128)(2,1)} async-done(((bf16[128,256]{1,0:T(8,128)(2,1)}), bf16[128,256]{1,0:T(8,128)(2,1)}) %all-reduce.4.cloned.1.call-update) | async-done | bytes 65552 | tf_op jit(solution)/shard_map/psum | solution.py:99
  852.2 144.8 %all-reduce.6.cloned.1.call-done = (bf16[2,128,128]{2,1,0:T(8,128)(2,1)}, bf16[2,128,128]{2,1,0:T(8,128)(2,1)}) async-done(((bf16[2,128,128]{2,1,0:T(8,128)(2,1)}, bf16[2,128,128]{2,1,0:T(8,128)(2,1)}), (bf16[2,128,128]{2,1,0:T(8,128)(2,1)}, bf16[2,128,128]{2,1,0:T(8,128)(2,1)})) %all-reduce.6.cloned.1.call-update) | async-done | bytes 131088 | tf_op jit(solution)/shard_map/psum | solution.py:104
  (65 shorter events, 20.4 us)
Async XLA Ops:
  7.2 14.7 %copy-start = (bf16[128,256]{1,0:T(8,128)(2,1)S(1)}, bf16[128,256]{1,0:T(8,128)(2,1)}, u32[]{:S(2)}) copy-start(bf16[128,256]{1,0:T(8,128)(2,1)} %param.15) | copy-start | bytes 196612
  7.2 89.4 %all-gather.9.cloned.1.call-start = ((), (), s32[]{:S(2)}) async-start(), calls=%async_computation.7 | async-start | bytes 1081344 | tf_op jit(solution)/shard_map/all_gather | solution.py:43
  8.7 171.7 %all-gather.11.cloned.1.call-start = ((), (), s32[]{:S(2)}) async-start(), calls=%async_computation.8 | async-start | bytes 1081344 | tf_op jit(solution)/shard_map/all_gather | solution.py:44
  10.1 254.1 %all-gather.13.cloned.1.call-start = ((), (), s32[]{:S(2)}) async-start(), calls=%async_computation.9 | async-start | bytes 1081344 | tf_op jit(solution)/shard_map/all_gather | solution.py:43
  21.9 1.7 copy-start.3
  23.6 12.1 %copy-start.9 = (f32[2,4096]{1,0:T(2,128)S(1)}, f32[2,4096]{1,0:T(2,128)}, u32[]{:S(2)}) copy-start(f32[2,4096]{1,0:T(2,128)} %param.19) | copy-start | bytes 98308
  23.6 49.6 %all-to-all-start = ((bf16[16,192,256]{2,1,0:T(8,128)(2,1)}), bf16[16,192,256]{2,1,0:T(8,128)(2,1)S(1)}, u32[]{:S(2)}, u32[]{:S(2)}) async-start(bf16[16,192,256]{2,1,0:T(8,128)(2,1)} %bitcast.88), calls=%async_computation | async-start | bytes 3145728 | tf_op jit(solution)/shard_map/all_to_all | solution.py:37
  35.1 312.9 %all-gather.15.cloned.1.call-start = ((), (), s32[]{:S(2)}) async-start(), calls=%async_computation.10 | async-start | bytes 1081344 | tf_op jit(solution)/shard_map/all_gather | solution.py:44
  35.7 448.4 %reduce-scatter.3.cloned.1.call-start = ((), (), s32[]{:S(2)}) async-start(), calls=%async_computation.4 | async-start | bytes 2162688 | tf_op jit(solution)/shard_map/reduce_scatter | solution.py:89
  73.3 25.1 %copy-start.1 = (bf16[16,192,256]{2,1,0:T(8,128)(2,1)}, bf16[16,192,256]{2,1,0:T(8,128)(2,1)S(1)}, u32[]{:S(2)}) copy-start(bf16[16,192,256]{2,1,0:T(8,128)(2,1)S(1)} %all-to-all-done) | copy-start | bytes 4718596
  183.9 164.1 %copy-start.8 = (f32[4096]{0:T(1024)S(1)}, f32[4096]{0:T(1024)}, u32[]{:S(2)}) copy-start(f32[4096]{0:T(1024)} %param.20) | copy-start | bytes 49156
  348.0 3.9 copy-start.11
  348.0 3.9 copy-start.7
  351.9 1.5 copy-start.10
  352.7 1.2 copy-start.6
  353.9 2.5 copy-start.5
  365.5 46.1 %all-to-all-start.1 = ((bf16[192,16,256]{2,0,1:T(8,128)(2,1)}), bf16[192,16,256]{2,0,1:T(8,128)(2,1)}, u32[]{:S(2)}, u32[]{:S(2)}) async-start(bf16[192,16,256]{2,0,1:T(8,128)(2,1)} %bitcast.87), calls=%async_computation.3 | async-start | bytes 3145728 | tf_op jit(solution)/shard_map/all_to_all | solution.py:94
  373.2 242.0 %reduce-scatter.5.cloned.1.call-start = ((), (), s32[]{:S(2)}) async-start(), calls=%async_computation.5 | async-start | bytes 2162688 | tf_op jit(solution)/shard_map/reduce_scatter | solution.py:86
  376.5 35.1 %copy-start.4 = (bf16[3072,128]{1,0:T(8,128)(2,1)S(1)}, bf16[3072,128]{1,0:T(8,128)(2,1)}, u32[]{:S(2)}) copy-start(bf16[3072,128]{1,0:T(8,128)(2,1)} %copy-done.3) | copy-start | bytes 2359300
  376.5 37.7 %copy-start.2 = (bf16[16,192,256]{2,1,0:T(8,128)(2,1)S(1)}, bf16[16,192,256]{2,1,0:T(8,128)(2,1)}, u32[]{:S(2)}) copy-start(bf16[16,192,256]{2,1,0:T(8,128)(2,1)} %copy-done.1) | copy-start | bytes 4718596
  376.6 474.2 %all-reduce.4.cloned.1.call-start = ((), (), s32[]{:S(2)}) async-start(), calls=%async_computation.6 | async-start | bytes 131072 | tf_op jit(solution)/shard_map/psum | solution.py:99
  414.2 582.8 %all-reduce.6.cloned.1.call-start = ((), (), s32[]{:S(2)}) async-start(), calls=%async_computation.11 | async-start | bytes 262144 | tf_op jit(solution)/shard_map/psum | solution.py:104
Sparse Core Ops, SparseCore 0:
  11.9 84.5 all-gather.8
  100.5 79.8 all-gather.10
  184.3 79.9 all-gather.12
  268.1 79.9 all-gather.14
  359.4 124.6 reduce-scatter.2
  489.4 125.6 reduce-scatter.4
  618.6 232.0 all-reduce.3
  853.9 143.0 all-reduce.5
where the time goes:
time: 1010 us
  waiting for transfers between devices  745 us (74%)
  blocking collectives  176 us (17%)
  matrix products  28.5 us (3%)
  starting transfers between devices  19.6 us (2%)
  other arithmetic  18.4 us (2%)
  between operations  14.4 us (1%)
    all_gather x2, waiting for transfers between devices, body(): lax.all_gather(up_weight[layer_index], 'row', axis=0, tiled=True)  164 us
    psum x1, waiting for transfers between devices, body(): lax.psum(down_rows.astype(jnp.bfloat16), 'group').astype(jnp.float32)  145 us
    reduce_scatter x1, waiting for transfers between devices, body(): lax.psum_scatter(jnp.stack(up_parts).astype(jnp.bfloat16), 'row', scatter...  131 us
    psum x1, blocking collectives, body(): lax.psum(jnp.stack(bias_terms).astype(jnp.bfloat16), 'row')  113 us
    all_gather x2, waiting for transfers between devices, body(): lax.all_gather(down_weight[layer_index], 'row', axis=0, tiled=True)  103 us
    reduce_scatter x1, waiting for transfers between devices, body(): lax.psum_scatter(jnp.stack(down_parts).astype(jnp.bfloat16), 'row', scatt...  69.3 us
    psum x1, blocking collectives, body(): lax.psum(bias_rows.astype(jnp.bfloat16), 'group').astype(jnp.float32)  63.2 us
    psum x1, waiting for transfers between devices, body(): lax.psum(proj_term.astype(jnp.bfloat16), 'row').astype(jnp.float32)  58.7 us
  transfers between devices with their start and end apart: 10, of which 10 were waited for; matrix products, arithmetic and copies ran while one was open for 4% of the time, Pallas kernels for 0%

commit v1 on v0

--- a/solution.py
+++ b/solution.py
@@ -8,6 +8,22 @@
     columns = jnp.arange(lookup_table.shape[0], dtype=jnp.int32)
     picker = (feature_id[:, None] == columns[None, :]).astype(jnp.float32)
     return jnp.dot(picker, lookup_table, precision=lax.Precision.HIGHEST)
+
+
+def exchange_sum(partial, axis, count):
+    pieces = partial.reshape(count, -1)
+    mine = jnp.sum(lax.all_to_all(pieces, axis, 0, 0, tiled=True), axis=0)
+    spread = jnp.broadcast_to(mine[None], pieces.shape)
+    return lax.all_to_all(spread, axis, 0, 0, tiled=True).reshape(partial.shape)
+
+
+def group_all_reduce(rows, groups):
+    stacked, height, width = rows.shape
+    pieces = rows.reshape(stacked, groups, height // groups, width).transpose(1, 0, 2, 3)
+    mine = jnp.sum(lax.all_to_all(pieces, "group", 0, 0, tiled=True), axis=0)
+    spread = jnp.broadcast_to(mine[None], pieces.shape)
+    gathered = lax.all_to_all(spread, "group", 0, 0, tiled=True)
+    return gathered.transpose(1, 0, 2, 3).reshape(rows.shape)
 
 
 def body(
@@ -38,11 +54,11 @@
     first_wide = first.astype(jnp.float32)
     crossed = first
     stored = []
+    weights_full = lax.all_gather(
+        jnp.concatenate([down_weight, up_weight], axis=0), "row", axis=1, tiled=True
+    )
     for layer_index in range(layers):
-        down_full, up_full = (
-            lax.all_gather(down_weight[layer_index], "row", axis=0, tiled=True),
-            lax.all_gather(up_weight[layer_index], "row", axis=0, tiled=True),
-        )
+        down_full, up_full = weights_full[layer_index], weights_full[layers + layer_index]
         hidden = jnp.dot(crossed, down_full, preferred_element_type=jnp.float32).astype(
             jnp.bfloat16
         )
@@ -82,28 +98,19 @@
         back = (back_wide + through).astype(jnp.bfloat16)
         up_parts[layer_index] = up_term
         down_parts[layer_index] = down_term
-    up_rows, down_rows = (
-        lax.psum_scatter(
-            jnp.stack(up_parts).astype(jnp.bfloat16), "row", scatter_dimension=1, tiled=True
-        ).astype(jnp.float32),
-        lax.psum_scatter(
-            jnp.stack(down_parts).astype(jnp.bfloat16), "row", scatter_dimension=1, tiled=True
-        ).astype(jnp.float32),
+    weight_rows = lax.psum_scatter(
+        jnp.stack(up_parts + down_parts).astype(jnp.bfloat16), "row", scatter_dimension=1, tiled=True
     )
+    weight_sums = group_all_reduce(weight_rows.astype(jnp.float32), groups)
+    grad_up, grad_down = weight_sums[:layers], weight_sums[layers:]
     first_grad = (first_grad + back.astype(jnp.float32)).astype(jnp.bfloat16)
     owner_grad = lax.all_to_all(first_grad, "group", split_axis=1, concat_axis=0, tiled=True)
     proj_term = lax.dot_general(
         ordered, owner_grad, (((0,), (0,)), ((), ())), preferred_element_type=jnp.float32
     )
-    grad_proj, bias_rows = (
-        lax.psum(proj_term.astype(jnp.bfloat16), "row").astype(jnp.float32),
-        lax.psum(jnp.stack(bias_terms).astype(jnp.bfloat16), "row").astype(jnp.float32),
-    )
-    grad_up, grad_down, grad_bias = (
-        lax.psum(up_rows.astype(jnp.bfloat16), "group").astype(jnp.float32),
-        lax.psum(down_rows.astype(jnp.bfloat16), "group").astype(jnp.float32),
-        lax.psum(bias_rows.astype(jnp.bfloat16), "group").astype(jnp.float32),
-    )
+    grad_proj = exchange_sum(proj_term, "row", lax.axis_size("row"))
+    bias_all = jnp.stack(bias_terms)
+    grad_bias = exchange_sum(bias_all, ("group", "row"), groups * lax.axis_size("row"))
     return (logits, grad_down, grad_up, grad_bias, grad_proj)
 
 

time: 1010 us -> 330 us (0.33)
  the two profiles are of different devices: /device:TPU:40 before, /device:TPU:2 now
where the time goes in v1:
time: 330 us; the launch traced here: 329 us
  waiting for transfers between devices  196 us (59%)
  starting transfers between devices  68.8 us (21%)
  matrix products  23.2 us (7%)
  other arithmetic  18 us (5%)
  between operations  14.3 us (4%)
  local copies, waits for them, and re-layouts  8.4 us (3%)
    all_gather x1, waiting for transfers between devices, body(): lax.all_gather(jnp.concatenate([down_weight, up_weight], axis=0), 'row',...  38.7 us
    all_to_all x1, waiting for transfers between devices, body(): lax.all_to_all(first_grad, 'group', split_axis=1, concat_axis=0, tiled=True)  36.3 us
    all_to_all x1, waiting for transfers between devices, body(): lax.all_to_all(projected, 'group', split_axis=0, concat_axis=1, tiled=True)  36.1 us
    reduce_scatter x1, waiting for transfers between devices, body(): lax.psum_scatter(jnp.stack(up_parts + down_parts).astype(jnp.bfloat16), '...  33.2 us
    all_to_all x2, waiting for transfers between devices, exchange_sum(): return lax.all_to_all(spread, axis, 0, 0, tiled=True).reshape(partial.shape)  28.7 us
    all_to_all x2, starting transfers between devices, exchange_sum(): mine = jnp.sum(lax.all_to_all(pieces, axis, 0, 0, tiled=True), axis=0)  19.2 us
    all_to_all x2, starting transfers between devices, exchange_sum(): return lax.all_to_all(spread, axis, 0, 0, tiled=True).reshape(partial.shape)  17.1 us
    all_to_all x1, starting transfers between devices, body(): lax.all_to_all(projected, 'group', split_axis=0, concat_axis=1, tiled=True)  11.8 us
  transfers between devices with their start and end apart: 10, of which 9 were waited for; matrix products, arithmetic and copies ran while one was open for 8% of the time, Pallas kernels for 0%

profile of v1, /device:TPU:2, one launch (start us, length us, event | category | flops | bytes accessed | tf_op | source)
XLA Modules:
  0.0 329.1 jit_solution(3709292654171521705)
XLA Ops:
  10.9 8.9 %scatter_custom_fusion = bf16[3072,128]{1,0:T(8,128)(2,1)S(1)} fusion(s32[3072]{0:T(1024)S(1)} %bitcast.116, f32[3072,128]{1,0:T(8,128)} %param.11, f32[128]{0:T(128)S(1)} %get-tuple-element.14, f32[128]{0:T(128)S(1)} %get-tuple-element.13, bf16[]{:T(256)} %constant.0.clone.1), kind=kCustom, calls=%fused_computation.53 | custom fusion | flops 1179648 | bytes 2360322 | tf_op jit(solution)/shard_map/scatter | solution.py:49
  21.6 11.8 %all-to-all-start = ((bf16[16,192,256]{2,1,0:T(8,128)(2,1)}), bf16[16,192,256]{2,1,0:T(8,128)(2,1)S(1)}, u32[]{:S(2)}, u32[]{:S(2)}) async-start(bf16[16,192,256]{2,1,0:T(8,128)(2,1)} %bitcast.106), calls=%async_computation | async-start | bytes 3145728 | tf_op jit(solution)/shard_map/all_to_all | solution.py:53
  33.6 36.1 %all-to-all-done = bf16[16,192,256]{2,1,0:T(8,128)(2,1)S(1)} async-done(((bf16[16,192,256]{2,1,0:T(8,128)(2,1)}), bf16[16,192,256]{2,1,0:T(8,128)(2,1)S(1)}, u32[]{:S(2)}, u32[]{:S(2)}) %all-to-all-start) | async-done | bytes 1572896 | tf_op jit(solution)/shard_map/all_to_all | solution.py:53
  70.0 38.7 %all-gather.2.cloned.1.call-done = bf16[4,4096,128]{2,1,0:T(8,128)(2,1)} async-done(((bf16[4,128,128]{2,1,0:T(8,128)(2,1)}), bf16[4,4096,128]{2,1,0:T(8,128)(2,1)}) %all-gather.2.cloned.1.call-update) | async-done | bytes 4194320 | tf_op jit(solution)/shard_map/all_gather | solution.py:57
  108.7 1.8 convolution_convert_fusion.8
  110.5 3.7 %fusion.11 = (bf16[192,4096]{1,0:T(8,128)(2,1)S(1)}, f32[192,4096]{1,0:T(8,128)}) fusion(bf16[192,4096]{1,0:T(8,128)(2,1)S(1)} %bitcast.98, f32[4096]{0:T(1024)S(1)} %bitcast.114, bf16[192,128]{1,0:T(8,128)(2,1)S(1)} %convolution_convert_fusion.8, bf16[4,4096,128]{2,1,0:T(8,128)(2,1)} %all-gather.2.cloned.1.call-done), kind=kOutput, calls=%fused_computation.28 | convolution fusion | flops 205258752 | bytes 7405568 | tf_op jit(solution)/shard_map/dot_general | solution.py:65
  114.7 2.7 multiply_reduce_fusion
  120.5 2.5 convert_reduce_fusion.1
  125.2 2.2 pad_maximum_fusion
  128.3 14.8 %all-to-all-start.3 = ((f32[512,1,16]{2,1,0:T(1,128)}), f32[512,1,16]{2,1,0:T(1,128)S(1)}, u32[]{:S(2)}, u32[]{:S(2)}) async-start(f32[512,1,16]{2,1,0:T(1,128)} %bitcast.109), calls=%async_computation.4 | async-start | bytes 524288 | tf_op jit(solution)/shard_map/all_to_all | solution.py:15
  143.1 4.2 %fusion.5 = bf16[192,4096]{1,0:T(8,128)(2,1)S(1)} fusion(f32[192,4096]{1,0:T(8,128)} %get-tuple-element.19, bf16[192,128]{1,0:T(8,128)(2,1)S(1)} %convolution_convert_fusion.5, f32[192,4096]{1,0:T(8,128)} %get-tuple-element.18, f32[192,4096]{1,0:T(8,128)S(1)} %copy-done.1, f32[192]{0:T(256)S(1)} %fusion.29, f32[4096]{0:T(1024)S(1)} %copy-done.5, ...), kind=kOutput, calls=%fused_computation.15 | convolution fusion | flops 209977344 | bytes 12124928 | tf_op jit(solution)/shard_map/dot_general | solution.py:95
  148.7 10.5 %all-to-all-done.3 = f32[512,1,16]{2,1,0:T(1,128)S(1)} async-done(((f32[512,1,16]{2,1,0:T(1,128)}), f32[512,1,16]{2,1,0:T(1,128)S(1)}, u32[]{:S(2)}, u32[]{:S(2)}) %all-to-all-start.3) | async-done | bytes 32800 | tf_op jit(solution)/shard_map/all_to_all | solution.py:15
  159.2 5.8 %all-to-all-start.5 = ((bf16[192,16,256]{2,0,1:T(8,128)(2,1)}), bf16[192,16,256]{2,0,1:T(8,128)(2,1)S(1)}, u32[]{:S(2)}, u32[]{:S(2)}) async-start(bf16[192,16,256]{2,0,1:T(8,128)(2,1)} %bitcast.105), calls=%async_computation.6 | async-start | bytes 3145728 | tf_op jit(solution)/shard_map/all_to_all | solution.py:107
  165.5 36.3 %all-to-all-done.5 = bf16[192,16,256]{2,0,1:T(8,128)(2,1)S(1)} async-done(((bf16[192,16,256]{2,0,1:T(8,128)(2,1)}), bf16[192,16,256]{2,0,1:T(8,128)(2,1)S(1)}, u32[]{:S(2)}, u32[]{:S(2)}) %all-to-all-start.5) | async-done | bytes 1572896 | tf_op jit(solution)/shard_map/all_to_all | solution.py:107
  202.6 10.1 %all-to-all-start.4 = ((f32[512,1,16]{2,1,0:T(1,128)}), f32[512,1,16]{2,1,0:T(1,128)S(1)}, u32[]{:S(2)}, u32[]{:S(2)}) async-start(f32[512,1,16]{2,1,0:T(1,128)} %broadcast_in_dim.10), calls=%async_computation.5 | async-start | bytes 524288 | tf_op jit(solution)/shard_map/all_to_all | solution.py:17
  214.0 16.7 %all-to-all-done.4 = f32[512,1,16]{2,1,0:T(1,128)S(1)} async-done(((f32[512,1,16]{2,1,0:T(1,128)}), f32[512,1,16]{2,1,0:T(1,128)S(1)}, u32[]{:S(2)}, u32[]{:S(2)}) %all-to-all-start.4) | async-done | bytes 32800 | tf_op jit(solution)/shard_map/all_to_all | solution.py:17
  230.7 4.4 %all-to-all-start.6 = ((f32[32,1,1024]{2,1,0:T(1,128)}), f32[32,1,1024]{2,1,0:T(1,128)S(1)}, u32[]{:S(2)}, u32[]{:S(2)}) async-start(f32[32,1,1024]{2,1,0:T(1,128)} %all_to_all.70), calls=%async_computation.7 | async-start | bytes 262144 | tf_op jit(solution)/shard_map/all_to_all | solution.py:15
  235.1 33.2 %reduce-scatter.2.cloned.1.call-done = bf16[4,128,128]{2,1,0:T(8,128)(2,1)} async-done(((bf16[4,4096,128]{2,1,0:T(8,128)(2,1)}), bf16[4,128,128]{2,1,0:T(8,128)(2,1)}) %reduce-scatter.2.cloned.1.call-update) | async-done | bytes 131088 | tf_op jit(solution)/shard_map/reduce_scatter | solution.py:101
  269.9 8.9 %all-to-all-start.1 = ((f32[16,4,8,128]{3,2,1,0:T(8,128)}), f32[16,4,8,128]{3,2,1,0:T(8,128)S(1)}, u32[]{:S(2)}, u32[]{:S(2)}) async-start(f32[16,4,8,128]{3,2,1,0:T(8,128)} %copy_bitcast_fusion.2), calls=%async_computation.2 | async-start | bytes 524288 | tf_op jit(solution)/shard_map/all_to_all | solution.py:23
  278.9 7.9 %all-to-all-done.1 = f32[16,4,8,128]{3,2,1,0:T(8,128)S(1)} async-done(((f32[16,4,8,128]{3,2,1,0:T(8,128)}), f32[16,4,8,128]{3,2,1,0:T(8,128)S(1)}, u32[]{:S(2)}, u32[]{:S(2)}) %all-to-all-start.1) | async-done | bytes 262176 | tf_op jit(solution)/shard_map/all_to_all | solution.py:23
  287.5 7.0 %all-to-all-start.7 = ((f32[32,1,1024]{2,1,0:T(1,128)}), f32[32,1,1024]{2,1,0:T(1,128)S(1)}, u32[]{:S(2)}, u32[]{:S(2)}) async-start(f32[32,1,1024]{2,1,0:T(1,128)} %broadcast_in_dim.11), calls=%async_computation.8 | async-start | bytes 262144 | tf_op jit(solution)/shard_map/all_to_all | solution.py:17
  294.5 11.9 %all-to-all-done.7 = f32[32,1,1024]{2,1,0:T(1,128)S(1)} async-done(((f32[32,1,1024]{2,1,0:T(1,128)}), f32[32,1,1024]{2,1,0:T(1,128)S(1)}, u32[]{:S(2)}, u32[]{:S(2)}) %all-to-all-start.7) | async-done | bytes 131104 | tf_op jit(solution)/shard_map/all_to_all | solution.py:17
  307.2 5.8 %all-to-all-start.2 = ((f32[16,4,8,128]{3,2,1,0:T(8,128)}), f32[16,4,8,128]{3,2,1,0:T(8,128)S(1)}, u32[]{:S(2)}, u32[]{:S(2)}) async-start(f32[16,4,8,128]{3,2,1,0:T(8,128)} %broadcast_in_dim.9), calls=%async_computation.3 | async-start | bytes 524288 | tf_op jit(solution)/shard_map/all_to_all | solution.py:25
  316.5 5.0 %all-to-all-done.2 = f32[16,4,8,128]{3,2,1,0:T(8,128)S(1)} async-done(((f32[16,4,8,128]{3,2,1,0:T(8,128)}), f32[16,4,8,128]{3,2,1,0:T(8,128)S(1)}, u32[]{:S(2)}, u32[]{:S(2)}) %all-to-all-start.2) | async-done | bytes 262176 | tf_op jit(solution)/shard_map/all_to_all | solution.py:25
  (61 shorter events, 24.0 us)
Async XLA Ops:
  7.2 12.7 %copy-start = (bf16[128,256]{1,0:T(8,128)(2,1)S(1)}, bf16[128,256]{1,0:T(8,128)(2,1)}, u32[]{:S(2)}) copy-start(bf16[128,256]{1,0:T(8,128)(2,1)} %param.15) | copy-start | bytes 196612
  7.2 101.5 %all-gather.2.cloned.1.call-start = ((), (), s32[]{:S(2)}) async-start(), calls=%async_computation.9 | async-start | bytes 4325376 | tf_op jit(solution)/shard_map/all_gather | solution.py:57
  19.8 50.0 %copy-start.2 = (bf16[3072,128]{1,0:T(8,128)(2,1)}, bf16[3072,128]{1,0:T(8,128)(2,1)S(1)}, u32[]{:S(2)}) copy-start(bf16[3072,128]{1,0:T(8,128)(2,1)S(1)} %scatter_custom_fusion) | copy-start | bytes 2359300
  19.8 13.7 %copy-start.5 = (f32[4096]{0:T(1024)S(1)}, f32[4096]{0:T(1024)}, u32[]{:S(2)}) copy-start(f32[4096]{0:T(1024)} %param.20) | copy-start | bytes 49156
  19.8 13.8 %copy-start.6 = (f32[2,4096]{1,0:T(2,128)S(1)}, f32[2,4096]{1,0:T(2,128)}, u32[]{:S(2)}) copy-start(f32[2,4096]{1,0:T(2,128)} %param.19) | copy-start | bytes 98308
  21.6 48.2 %all-to-all-start = ((bf16[16,192,256]{2,1,0:T(8,128)(2,1)}), bf16[16,192,256]{2,1,0:T(8,128)(2,1)S(1)}, u32[]{:S(2)}, u32[]{:S(2)}) async-start(bf16[16,192,256]{2,1,0:T(8,128)(2,1)} %bitcast.106), calls=%async_computation | async-start | bytes 3145728 | tf_op jit(solution)/shard_map/all_to_all | solution.py:53
  33.4 234.9 %reduce-scatter.2.cloned.1.call-start = ((), (), s32[]{:S(2)}) async-start(), calls=%async_computation.10 | async-start | bytes 4325376 | tf_op jit(solution)/shard_map/reduce_scatter | solution.py:101
  110.5 3.7 %copy-start.4 = (bf16[4,4096,128]{2,1,0:T(8,128)(2,1)S(1)}, bf16[4,4096,128]{2,1,0:T(8,128)(2,1)}, u32[]{:S(2)}) copy-start(bf16[4,4096,128]{2,1,0:T(8,128)(2,1)} %all-gather.2.cloned.1.call-done) | copy-start | bytes 12582916
  114.7 2.7 copy-start.8
  117.4 1.6 copy-start.7
  127.4 15.8 %copy-start.1 = (f32[192,4096]{1,0:T(8,128)S(1)}, f32[192,4096]{1,0:T(8,128)}, u32[]{:S(2)}) copy-start(f32[192,4096]{1,0:T(8,128)} %get-tuple-element.16) | copy-start | bytes 9437188
  128.3 30.9 %all-to-all-start.3 = ((f32[512,1,16]{2,1,0:T(1,128)}), f32[512,1,16]{2,1,0:T(1,128)S(1)}, u32[]{:S(2)}, u32[]{:S(2)}) async-start(f32[512,1,16]{2,1,0:T(1,128)} %bitcast.109), calls=%async_computation.4 | async-start | bytes 524288 | tf_op jit(solution)/shard_map/all_to_all | solution.py:15
  147.4 65.4 %copy-start.3 = (bf16[3072,128]{1,0:T(8,128)(2,1)S(1)}, bf16[3072,128]{1,0:T(8,128)(2,1)}, u32[]{:S(2)}) copy-start(bf16[3072,128]{1,0:T(8,128)(2,1)} %copy-done.2) | copy-start | bytes 2359300
  159.2 42.7 %all-to-all-start.5 = ((bf16[192,16,256]{2,0,1:T(8,128)(2,1)}), bf16[192,16,256]{2,0,1:T(8,128)(2,1)S(1)}, u32[]{:S(2)}, u32[]{:S(2)}) async-start(bf16[192,16,256]{2,0,1:T(8,128)(2,1)} %bitcast.105), calls=%async_computation.6 | async-start | bytes 3145728 | tf_op jit(solution)/shard_map/all_to_all | solution.py:107
  202.6 28.1 %all-to-all-start.4 = ((f32[512,1,16]{2,1,0:T(1,128)}), f32[512,1,16]{2,1,0:T(1,128)S(1)}, u32[]{:S(2)}, u32[]{:S(2)}) async-start(f32[512,1,16]{2,1,0:T(1,128)} %broadcast_in_dim.10), calls=%async_computation.5 | async-start | bytes 524288 | tf_op jit(solution)/shard_map/all_to_all | solution.py:17
  230.7 39.2 %all-to-all-start.6 = ((f32[32,1,1024]{2,1,0:T(1,128)}), f32[32,1,1024]{2,1,0:T(1,128)S(1)}, u32[]{:S(2)}, u32[]{:S(2)}) async-start(f32[32,1,1024]{2,1,0:T(1,128)} %all_to_all.70), calls=%async_computation.7 | async-start | bytes 262144 | tf_op jit(solution)/shard_map/all_to_all | solution.py:15
  269.9 16.8 %all-to-all-start.1 = ((f32[16,4,8,128]{3,2,1,0:T(8,128)}), f32[16,4,8,128]{3,2,1,0:T(8,128)S(1)}, u32[]{:S(2)}, u32[]{:S(2)}) async-start(f32[16,4,8,128]{3,2,1,0:T(8,128)} %copy_bitcast_fusion.2), calls=%async_computation.2 | async-start | bytes 524288 | tf_op jit(solution)/shard_map/all_to_all | solution.py:23
  287.5 18.9 %all-to-all-start.7 = ((f32[32,1,1024]{2,1,0:T(1,128)}), f32[32,1,1024]{2,1,0:T(1,128)S(1)}, u32[]{:S(2)}, u32[]{:S(2)}) async-start(f32[32,1,1024]{2,1,0:T(1,128)} %broadcast_in_dim.11), calls=%async_computation.8 | async-start | bytes 262144 | tf_op jit(solution)/shard_map/all_to_all | solution.py:17
  307.2 14.4 %all-to-all-start.2 = ((f32[16,4,8,128]{3,2,1,0:T(8,128)}), f32[16,4,8,128]{3,2,1,0:T(8,128)S(1)}, u32[]{:S(2)}, u32[]{:S(2)}) async-start(f32[16,4,8,128]{3,2,1,0:T(8,128)} %broadcast_in_dim.9), calls=%async_computation.3 | async-start | bytes 524288 | tf_op jit(solution)/shard_map/all_to_all | solution.py:25
Sparse Core Ops, SparseCore 0:
  12.0 96.6 all-gather.1
  127.5 140.7 reduce-scatter.1

commit v2 on v1

--- a/solution.py
+++ b/solution.py
@@ -8,22 +8,6 @@
     columns = jnp.arange(lookup_table.shape[0], dtype=jnp.int32)
     picker = (feature_id[:, None] == columns[None, :]).astype(jnp.float32)
     return jnp.dot(picker, lookup_table, precision=lax.Precision.HIGHEST)
-
-
-def exchange_sum(partial, axis, count):
-    pieces = partial.reshape(count, -1)
-    mine = jnp.sum(lax.all_to_all(pieces, axis, 0, 0, tiled=True), axis=0)
-    spread = jnp.broadcast_to(mine[None], pieces.shape)
-    return lax.all_to_all(spread, axis, 0, 0, tiled=True).reshape(partial.shape)
-
-
-def group_all_reduce(rows, groups):
-    stacked, height, width = rows.shape
-    pieces = rows.reshape(stacked, groups, height // groups, width).transpose(1, 0, 2, 3)
-    mine = jnp.sum(lax.all_to_all(pieces, "group", 0, 0, tiled=True), axis=0)
-    spread = jnp.broadcast_to(mine[None], pieces.shape)
-    gathered = lax.all_to_all(spread, "group", 0, 0, tiled=True)
-    return gathered.transpose(1, 0, 2, 3).reshape(rows.shape)
 
 
 def body(
@@ -98,19 +82,48 @@
         back = (back_wide + through).astype(jnp.bfloat16)
         up_parts[layer_index] = up_term
         down_parts[layer_index] = down_term
-    weight_rows = lax.psum_scatter(
-        jnp.stack(up_parts + down_parts).astype(jnp.bfloat16), "row", scatter_dimension=1, tiled=True
+    row_count_axis = lax.axis_size("row")
+    width = first.shape[1]
+    rank = up_parts[0].shape[1]
+    block_rows = width // row_count_axis
+    piece = block_rows // groups
+    bias_all = jnp.stack(bias_terms)
+    bias_slab = jnp.zeros((row_count_axis, block_rows, rank), jnp.float32)
+    bias_slab = bias_slab.at[:, :layers, :].set(
+        bias_all.reshape(layers, row_count_axis, block_rows).transpose(1, 0, 2)
     )
-    weight_sums = group_all_reduce(weight_rows.astype(jnp.float32), groups)
-    grad_up, grad_down = weight_sums[:layers], weight_sums[layers:]
+    slabs = jnp.concatenate([jnp.stack(up_parts + down_parts), bias_slab.reshape(1, width, rank)])
+    count = slabs.shape[0]
+    slabs = slabs.astype(jnp.bfloat16).reshape(count, row_count_axis, groups, piece, rank)
+    slabs = slabs.transpose(0, 2, 1, 3, 4).reshape(count, width, rank)
+    group_part = lax.psum_scatter(slabs, "group", scatter_dimension=1, tiled=True)
+    row_pieces = group_part.reshape(count, row_count_axis, piece, rank).transpose(1, 0, 2, 3)
+    mine = jnp.sum(
+        lax.all_to_all(row_pieces.astype(jnp.float32), "row", 0, 0, tiled=True), axis=0
+    )
+    spread = jnp.broadcast_to(mine[None], (groups,) + mine.shape)
+    gathered = lax.all_to_all(spread, "group", 0, 0, tiled=True)
+    blocks = gathered.transpose(1, 0, 2, 3).reshape(count, block_rows, rank)
+    grad_up, grad_down = blocks[:layers], blocks[layers : 2 * layers]
+    bias_rows = blocks[2 * layers, :layers, :]
     first_grad = (first_grad + back.astype(jnp.float32)).astype(jnp.bfloat16)
     owner_grad = lax.all_to_all(first_grad, "group", split_axis=1, concat_axis=0, tiled=True)
     proj_term = lax.dot_general(
         ordered, owner_grad, (((0,), (0,)), ((), ())), preferred_element_type=jnp.float32
     )
-    grad_proj = exchange_sum(proj_term, "row", lax.axis_size("row"))
-    bias_all = jnp.stack(bias_terms)
-    grad_bias = exchange_sum(bias_all, ("group", "row"), groups * lax.axis_size("row"))
+    proj_pieces = proj_term.reshape(row_count_axis, -1)
+    proj_mine = jnp.sum(lax.all_to_all(proj_pieces, "row", 0, 0, tiled=True), axis=0)
+    last = jnp.concatenate([proj_mine, bias_rows.reshape(-1)])
+    last_all = lax.all_to_all(
+        jnp.broadcast_to(last[None], (row_count_axis,) + last.shape), "row", 0, 0, tiled=True
+    )
+    grad_proj = last_all[:, : proj_mine.shape[0]].reshape(proj_term.shape)
+    grad_bias = (
+        last_all[:, proj_mine.shape[0] :]
+        .reshape(row_count_axis, layers, block_rows)
+        .transpose(1, 0, 2)
+        .reshape(layers, width)
+    )
     return (logits, grad_down, grad_up, grad_bias, grad_proj)
 
 

time: 330 us -> 351 us (1.064)
  waiting for transfers between devices: 196 us -> 224 us
  starting transfers between devices: 68.8 us -> 42.7 us
  local copies, waits for them, and re-layouts: 8.4 us -> 24 us
  matrix products: 23.2 us -> 29.3 us
    reduce_scatter x1, waiting for transfers between devices: 33.2 us -> 97 us  [body(): lax.psum_scatter(slabs, 'group', scatter_dimension=1, tiled=True)]
    all_to_all x1, waiting for transfers between devices: 36.3 us -> 0.01 us  [body(): lax.all_to_all(first_grad, 'group', split_axis=1, concat_axis=0, tiled=True)]
    all_to_all x6 -> x4, starting transfers between devices: 50.9 us -> 21.8 us  [the longest x1 8.74 us: body(): lax.all_to_all(row_pieces.astype(jnp.float32), 'row', 0, 0, tiled=True)]
    transpose x0 -> x1, local copies, waits for them, and re-layouts: none -> 6.24 us  [body(): slabs = slabs.transpose(0, 2, 1, 3, 4).reshape(count, width, rank)]
    unnamed x19 -> x30, local copies, waits for them, and re-layouts: 0.07 us -> 5.39 us
    dot_general x0 -> x2, local copies, waits for them, and re-layouts: none -> 5.12 us  [the longest x1 2.67 us: body(): lax.dot_general(crossed_in, hidden_grad, (((0,), (0,)), ((), ())), prefer...]
    all_to_all x6 -> x4, waiting for transfers between devices: 52.1 us -> 54.6 us  [the longest x1 21 us: body(): lax.all_to_all(row_pieces.astype(jnp.float32), 'row', 0, 0, tiled=True)]
  transfers between devices with their start and end apart: 10 -> 8, of which waited for: 9 -> 7; matrix products, arithmetic and copies ran while one was open for 8% -> 7% of each run, Pallas kernels for 0% -> 0%
where the time goes in v2:
time: 351 us; the launch traced here: 350 us
  waiting for transfers between devices  224 us (64%)
  starting transfers between devices  42.7 us (12%)
  matrix products  29.3 us (8%)
  local copies, waits for them, and re-layouts  24 us (7%)
  other arithmetic  16 us (5%)
  between operations  14.3 us (4%)
    reduce_scatter x1, waiting for transfers between devices, body(): lax.psum_scatter(slabs, 'group', scatter_dimension=1, tiled=True)  97 us
    all_to_all x1, waiting for transfers between devices, body(): lax.all_to_all(projected, 'group', split_axis=0, concat_axis=1, tiled=True)  36.3 us
    all_gather x1, waiting for transfers between devices, body(): lax.all_gather(jnp.concatenate([down_weight, up_weight], axis=0), 'row',...  36 us
    all_to_all x1, waiting for transfers between devices, body(): lax.all_to_all(row_pieces.astype(jnp.float32), 'row', 0, 0, tiled=True)  21 us
    all_to_all x1, waiting for transfers between devices, body(): lax.all_to_all(jnp.broadcast_to(last[None], (row_count_axis,) + last.shap...  11.9 us
    all_to_all x1, waiting for transfers between devices, body(): lax.all_to_all(proj_pieces, 'row', 0, 0, tiled=True)  11.9 us
    all_to_all x1, starting transfers between devices, body(): lax.all_to_all(projected, 'group', split_axis=0, concat_axis=1, tiled=True)  11.8 us
    all_to_all x1, waiting for transfers between devices, body(): gathered = lax.all_to_all(spread, 'group', 0, 0, tiled=True)  9.76 us
  transfers between devices with their start and end apart: 8, of which 7 were waited for; matrix products, arithmetic and copies ran while one was open for 7% of the time, Pallas kernels for 0%

profile of v2, /device:TPU:2, one launch (start us, length us, event | category | flops | bytes accessed | tf_op | source)
XLA Modules:
  0.0 350.3 jit_solution(194929365157466082)
XLA Ops:
  10.9 8.9 %scatter_custom_fusion = bf16[3072,128]{1,0:T(8,128)(2,1)S(1)} fusion(s32[3072]{0:T(1024)S(1)} %bitcast.154, f32[3072,128]{1,0:T(8,128)} %param.13, f32[128]{0:T(128)S(1)} %get-tuple-element.26, f32[128]{0:T(128)S(1)} %get-tuple-element.25, bf16[]{:T(256)} %constant.33.clone.1), kind=kCustom, calls=%fused_computation.51 | custom fusion | flops 1179648 | bytes 2360322 | tf_op jit(solution)/shard_map/scatter | solution.py:33
  21.6 11.8 %all-to-all-start = ((bf16[16,192,256]{2,1,0:T(8,128)(2,1)}), bf16[16,192,256]{2,1,0:T(8,128)(2,1)S(1)}, u32[]{:S(2)}, u32[]{:S(2)}) async-start(bf16[16,192,256]{2,1,0:T(8,128)(2,1)} %bitcast.6), calls=%async_computation | async-start | bytes 3145728 | tf_op jit(solution)/shard_map/all_to_all | solution.py:37
  33.5 36.3 %all-to-all-done = bf16[16,192,256]{2,1,0:T(8,128)(2,1)S(1)} async-done(((bf16[16,192,256]{2,1,0:T(8,128)(2,1)}), bf16[16,192,256]{2,1,0:T(8,128)(2,1)S(1)}, u32[]{:S(2)}, u32[]{:S(2)}) %all-to-all-start) | async-done | bytes 1572896 | tf_op jit(solution)/shard_map/all_to_all | solution.py:37
  70.0 2.7 copy.40
  72.7 36.0 %all-gather.2.cloned.1.call-done = bf16[4,4096,128]{2,1,0:T(8,128)(2,1)} async-done(((bf16[4,128,128]{2,1,0:T(8,128)(2,1)}), bf16[4,4096,128]{2,1,0:T(8,128)(2,1)}) %all-gather.2.cloned.1.call-update) | async-done | bytes 4194320 | tf_op jit(solution)/shard_map/all_gather | solution.py:41
  110.4 3.7 %fusion.7 = (bf16[192,4096]{1,0:T(8,128)(2,1)S(1)}, f32[192,4096]{1,0:T(8,128)}) fusion(bf16[192,4096]{1,0:T(8,128)(2,1)S(1)} %bitcast.131, f32[4096]{0:T(1024)S(1)} %bitcast.151, bf16[192,128]{1,0:T(8,128)(2,1)S(1)} %convolution_convert_fusion.8, bf16[4,4096,128]{2,1,0:T(8,128)(2,1)} %all-gather.2.cloned.1.call-done), kind=kOutput, calls=%fused_computation.21 | convolution fusion | flops 205258752 | bytes 7405568 | tf_op jit(solution)/shard_map/dot_general | solution.py:49
  114.7 2.6 multiply_reduce_fusion
  122.2 2.5 fusion.33
  127.8 2.4 copy.39
  130.8 3.4 fusion.14
  134.2 2.3 convolution_convert_fusion.5
  140.7 6.2 %copy.42 = bf16[5,16,32,8,128]{4,3,2,1,0:T(8,128)(2,1)} copy(bf16[5,16,32,8,128]{4,3,1,2,0:T(8,128)(2,1)} %bitcast.139) | data formatting | bytes 10485760 | tf_op jit(solution)/shard_map/transpose | solution.py:98
  146.9 1.9 copy-done.1
  148.8 4.0 %fusion.5 = bf16[192,4096]{1,0:T(8,128)(2,1)S(1)} fusion(f32[192,4096]{1,0:T(8,128)} %get-tuple-element.31, bf16[192,128]{1,0:T(8,128)(2,1)S(1)} %convolution_convert_fusion.5, f32[192,4096]{1,0:T(8,128)} %get-tuple-element.30, f32[192,4096]{1,0:T(8,128)S(1)} %copy-done.1, f32[192]{0:T(256)S(1)} %fusion.31, f32[4096]{0:T(1024)S(1)} %copy-done.9, ...), kind=kOutput, calls=%fused_computation.15 | convolution fusion | flops 209977344 | bytes 12124928 | tf_op jit(solution)/shard_map/dot_general | solution.py:79
  154.1 9.0 %all-to-all-start.3 = ((bf16[192,16,256]{2,0,1:T(8,128)(2,1)}), bf16[192,16,256]{2,0,1:T(8,128)(2,1)S(1)}, u32[]{:S(2)}, u32[]{:S(2)}) async-start(bf16[192,16,256]{2,0,1:T(8,128)(2,1)} %bitcast.141), calls=%async_computation.4 | async-start | bytes 3145728 | tf_op jit(solution)/shard_map/all_to_all | solution.py:110
  163.1 97.0 %reduce-scatter.2.cloned.1.call-done = bf16[5,256,128]{2,1,0:T(8,128)(2,1)} async-done(((bf16[5,4096,128]{2,1,0:T(8,128)(2,1)}), bf16[5,256,128]{2,1,0:T(8,128)(2,1)}) %reduce-scatter.2.cloned.1.call-update) | async-done | bytes 327696 | tf_op jit(solution)/shard_map/reduce_scatter | solution.py:99
  262.0 8.7 %all-to-all-start.1 = ((f32[32,5,8,128]{3,2,1,0:T(8,128)}), f32[32,5,8,128]{3,2,1,0:T(8,128)S(1)}, u32[]{:S(2)}, u32[]{:S(2)}) async-start(f32[32,5,8,128]{3,2,1,0:T(8,128)} %copy_bitcast_fusion.1), calls=%async_computation.2 | async-start | bytes 1310720 | tf_op jit(solution)/shard_map/all_to_all | solution.py:102
  272.0 21.0 %all-to-all-done.1 = f32[32,5,8,128]{3,2,1,0:T(8,128)S(1)} async-done(((f32[32,5,8,128]{3,2,1,0:T(8,128)}), f32[32,5,8,128]{3,2,1,0:T(8,128)S(1)}, u32[]{:S(2)}, u32[]{:S(2)}) %all-to-all-start.1) | async-done | bytes 655392 | tf_op jit(solution)/shard_map/all_to_all | solution.py:102
  293.0 3.9 %all-to-all-start.4 = ((f32[32,1,1024]{2,1,0:T(1,128)}), f32[32,1,1024]{2,1,0:T(1,128)S(1)}, u32[]{:S(2)}, u32[]{:S(2)}) async-start(f32[32,1,1024]{2,1,0:T(1,128)} %all_to_all.60), calls=%async_computation.5 | async-start | bytes 262144 | tf_op jit(solution)/shard_map/all_to_all | solution.py:115
  296.9 11.9 %all-to-all-done.4 = f32[32,1,1024]{2,1,0:T(1,128)S(1)} async-done(((f32[32,1,1024]{2,1,0:T(1,128)}), f32[32,1,1024]{2,1,0:T(1,128)S(1)}, u32[]{:S(2)}, u32[]{:S(2)}) %all-to-all-start.4) | async-done | bytes 131104 | tf_op jit(solution)/shard_map/all_to_all | solution.py:115
  309.5 5.4 %all-to-all-start.2 = ((f32[16,5,8,128]{3,2,1,0:T(8,128)}), f32[16,5,8,128]{3,2,1,0:T(8,128)S(1)}, u32[]{:S(2)}, u32[]{:S(2)}) async-start(f32[16,5,8,128]{3,2,1,0:T(8,128)} %broadcast_in_dim.7), calls=%async_computation.3 | async-start | bytes 655360 | tf_op jit(solution)/shard_map/all_to_all | solution.py:105
  315.0 9.8 %all-to-all-done.2 = f32[16,5,8,128]{3,2,1,0:T(8,128)S(1)} async-done(((f32[16,5,8,128]{3,2,1,0:T(8,128)}), f32[16,5,8,128]{3,2,1,0:T(8,128)S(1)}, u32[]{:S(2)}, u32[]{:S(2)}) %all-to-all-start.2) | async-done | bytes 327712 | tf_op jit(solution)/shard_map/all_to_all | solution.py:105
  325.6 3.9 %all-to-all-start.5 = ((f32[32,1,1280]{2,1,0:T(1,128)}), f32[32,1,1280]{2,1,0:T(1,128)S(1)}, u32[]{:S(2)}, u32[]{:S(2)}) async-start(f32[32,1,1280]{2,1,0:T(1,128)} %broadcast_in_dim.8), calls=%async_computation.6 | async-start | bytes 327680 | tf_op jit(solution)/shard_map/all_to_all | solution.py:117
  330.2 11.9 %all-to-all-done.5 = f32[32,1,1280]{2,1,0:T(1,128)S(1)} async-done(((f32[32,1,1280]{2,1,0:T(1,128)}), f32[32,1,1280]{2,1,0:T(1,128)S(1)}, u32[]{:S(2)}, u32[]{:S(2)}) %all-to-all-start.5) | async-done | bytes 163872 | tf_op jit(solution)/shard_map/all_to_all | solution.py:117
  (72 shorter events, 28.8 us)
Async XLA Ops:
  7.2 12.7 %copy-start = (bf16[128,256]{1,0:T(8,128)(2,1)S(1)}, bf16[128,256]{1,0:T(8,128)(2,1)}, u32[]{:S(2)}) copy-start(bf16[128,256]{1,0:T(8,128)(2,1)} %param.17) | copy-start | bytes 196612
  7.2 101.5 %all-gather.2.cloned.1.call-start = ((), (), s32[]{:S(2)}) async-start(), calls=%async_computation.7 | async-start | bytes 4325376 | tf_op jit(solution)/shard_map/all_gather | solution.py:41
  19.8 1.8 copy-start.3
  19.8 13.6 %copy-start.9 = (f32[4096]{0:T(1024)S(1)}, f32[4096]{0:T(1024)}, u32[]{:S(2)}) copy-start(f32[4096]{0:T(1024)} %param.22) | copy-start | bytes 49156
  19.8 13.6 %copy-start.10 = (f32[2,4096]{1,0:T(2,128)S(1)}, f32[2,4096]{1,0:T(2,128)}, u32[]{:S(2)}) copy-start(f32[2,4096]{1,0:T(2,128)} %param.21) | copy-start | bytes 98308
  21.6 48.2 %all-to-all-start = ((bf16[16,192,256]{2,1,0:T(8,128)(2,1)}), bf16[16,192,256]{2,1,0:T(8,128)(2,1)S(1)}, u32[]{:S(2)}, u32[]{:S(2)}) async-start(bf16[16,192,256]{2,1,0:T(8,128)(2,1)} %bitcast.6), calls=%async_computation | async-start | bytes 3145728 | tf_op jit(solution)/shard_map/all_to_all | solution.py:37
  33.4 226.7 %reduce-scatter.2.cloned.1.call-start = ((), (), s32[]{:S(2)}) async-start(), calls=%async_computation.8 | async-start | bytes 5570560 | tf_op jit(solution)/shard_map/reduce_scatter | solution.py:99
  110.4 3.7 %copy-start.7 = (bf16[4,4096,128]{2,1,0:T(8,128)(2,1)S(1)}, bf16[4,4096,128]{2,1,0:T(8,128)(2,1)}, u32[]{:S(2)}) copy-start(bf16[4,4096,128]{2,1,0:T(8,128)(2,1)} %all-gather.2.cloned.1.call-done) | copy-start | bytes 12582916
  114.7 2.6 copy-start.12
  117.3 2.3 copy-start.11
  124.6 1.2 copy-start.6
  124.6 3.1 copy-start.5
  130.7 5.9 %copy-start.2 = (bf16[4096,192]{1,0:T(8,128)(2,1)S(1)}, bf16[4096,192]{1,0:T(8,128)(2,1)}, u32[]{:S(2)}) copy-start(bf16[4096,192]{1,0:T(8,128)(2,1)} %copy.40) | copy-start | bytes 4718596
  134.2 4.1 %copy-start.8 = (bf16[4096,128]{1,0:T(8,128)(2,1)S(1)}, bf16[4096,128]{1,0:T(8,128)(2,1)}, u32[]{:S(2)}) copy-start(bf16[4096,128]{1,0:T(8,128)(2,1)} %convolution_convert_fusion) | copy-start | bytes 3145732
  146.9 1.9 copy-start.1
  154.1 116.6 %copy-start.4 = (bf16[3072,128]{1,0:T(8,128)(2,1)S(1)}, bf16[3072,128]{1,0:T(8,128)(2,1)}, u32[]{:S(2)}) copy-start(bf16[3072,128]{1,0:T(8,128)(2,1)} %copy-done.3) | copy-start | bytes 2359300
  154.1 107.8 %all-to-all-start.3 = ((bf16[192,16,256]{2,0,1:T(8,128)(2,1)}), bf16[192,16,256]{2,0,1:T(8,128)(2,1)S(1)}, u32[]{:S(2)}, u32[]{:S(2)}) async-start(bf16[192,16,256]{2,0,1:T(8,128)(2,1)} %bitcast.141), calls=%async_computation.4 | async-start | bytes 3145728 | tf_op jit(solution)/shard_map/all_to_all | solution.py:110
  262.0 31.0 %all-to-all-start.1 = ((f32[32,5,8,128]{3,2,1,0:T(8,128)}), f32[32,5,8,128]{3,2,1,0:T(8,128)S(1)}, u32[]{:S(2)}, u32[]{:S(2)}) async-start(f32[32,5,8,128]{3,2,1,0:T(8,128)} %copy_bitcast_fusion.1), calls=%async_computation.2 | async-start | bytes 1310720 | tf_op jit(solution)/shard_map/all_to_all | solution.py:102
  293.0 15.8 %all-to-all-start.4 = ((f32[32,1,1024]{2,1,0:T(1,128)}), f32[32,1,1024]{2,1,0:T(1,128)S(1)}, u32[]{:S(2)}, u32[]{:S(2)}) async-start(f32[32,1,1024]{2,1,0:T(1,128)} %all_to_all.60), calls=%async_computation.5 | async-start | bytes 262144 | tf_op jit(solution)/shard_map/all_to_all | solution.py:115
  309.5 15.2 %all-to-all-start.2 = ((f32[16,5,8,128]{3,2,1,0:T(8,128)}), f32[16,5,8,128]{3,2,1,0:T(8,128)S(1)}, u32[]{:S(2)}, u32[]{:S(2)}) async-start(f32[16,5,8,128]{3,2,1,0:T(8,128)} %broadcast_in_dim.7), calls=%async_computation.3 | async-start | bytes 655360 | tf_op jit(solution)/shard_map/all_to_all | solution.py:105
  325.6 16.5 %all-to-all-start.5 = ((f32[32,1,1280]{2,1,0:T(1,128)}), f32[32,1,1280]{2,1,0:T(1,128)S(1)}, u32[]{:S(2)}, u32[]{:S(2)}) async-start(f32[32,1,1280]{2,1,0:T(1,128)} %broadcast_in_dim.8), calls=%async_computation.6 | async-start | bytes 327680 | tf_op jit(solution)/shard_map/all_to_all | solution.py:117
Sparse Core Ops, SparseCore 0:
  12.0 96.6 all-gather.1
  147.1 113.0 reduce-scatter.1

commit v3 on v1

--- a/solution.py
+++ b/solution.py
@@ -15,15 +15,6 @@
     mine = jnp.sum(lax.all_to_all(pieces, axis, 0, 0, tiled=True), axis=0)
     spread = jnp.broadcast_to(mine[None], pieces.shape)
     return lax.all_to_all(spread, axis, 0, 0, tiled=True).reshape(partial.shape)
-
-
-def group_all_reduce(rows, groups):
-    stacked, height, width = rows.shape
-    pieces = rows.reshape(stacked, groups, height // groups, width).transpose(1, 0, 2, 3)
-    mine = jnp.sum(lax.all_to_all(pieces, "group", 0, 0, tiled=True), axis=0)
-    spread = jnp.broadcast_to(mine[None], pieces.shape)
-    gathered = lax.all_to_all(spread, "group", 0, 0, tiled=True)
-    return gathered.transpose(1, 0, 2, 3).reshape(rows.shape)
 
 
 def body(
@@ -98,19 +89,30 @@
         back = (back_wide + through).astype(jnp.bfloat16)
         up_parts[layer_index] = up_term
         down_parts[layer_index] = down_term
-    weight_rows = lax.psum_scatter(
-        jnp.stack(up_parts + down_parts).astype(jnp.bfloat16), "row", scatter_dimension=1, tiled=True
-    )
-    weight_sums = group_all_reduce(weight_rows.astype(jnp.float32), groups)
-    grad_up, grad_down = weight_sums[:layers], weight_sums[layers:]
+    row_count_axis = lax.axis_size("row")
+    width = first.shape[1]
+    rank = up_parts[0].shape[1]
+    block_rows = width // row_count_axis
+    piece = block_rows // groups
+    slabs = jnp.stack(up_parts + down_parts).astype(jnp.bfloat16)
+    count = slabs.shape[0]
+    slabs = slabs.reshape(count, row_count_axis, groups, piece, rank).transpose(0, 2, 1, 3, 4)
+    slabs = slabs.reshape(count, width, rank)
+    group_part = lax.psum_scatter(slabs, "group", scatter_dimension=1, tiled=True)
     first_grad = (first_grad + back.astype(jnp.float32)).astype(jnp.bfloat16)
     owner_grad = lax.all_to_all(first_grad, "group", split_axis=1, concat_axis=0, tiled=True)
     proj_term = lax.dot_general(
         ordered, owner_grad, (((0,), (0,)), ((), ())), preferred_element_type=jnp.float32
     )
-    grad_proj = exchange_sum(proj_term, "row", lax.axis_size("row"))
-    bias_all = jnp.stack(bias_terms)
-    grad_bias = exchange_sum(bias_all, ("group", "row"), groups * lax.axis_size("row"))
+    grad_proj = exchange_sum(proj_term, "row", row_count_axis)
+    grad_bias = exchange_sum(jnp.stack(bias_terms), ("group", "row"), groups * row_count_axis)
+    group_part, grad_proj, grad_bias = lax.optimization_barrier((group_part, grad_proj, grad_bias))
+    row_pieces = group_part.reshape(count, row_count_axis, piece, rank).transpose(1, 0, 2, 3)
+    mine = jnp.sum(lax.all_to_all(row_pieces, "row", 0, 0, tiled=True).astype(jnp.float32), axis=0)
+    spread = jnp.broadcast_to(mine[None], (groups,) + mine.shape)
+    gathered = lax.all_to_all(spread, "group", 0, 0, tiled=True)
+    blocks = gathered.transpose(1, 0, 2, 3).reshape(count, block_rows, rank)
+    grad_up, grad_down = blocks[:layers], blocks[layers:]
     return (logits, grad_down, grad_up, grad_bias, grad_proj)
 
 

time: 330 us -> 333 us (level)
  blocking collectives: 0 us -> 31.7 us
  waiting for transfers between devices: 196 us -> 175 us
  starting transfers between devices: 68.8 us -> 50.7 us
  local copies, waits for them, and re-layouts: 8.4 us -> 19.3 us
    reduce_scatter x1, waiting for transfers between devices: 33.2 us -> 0.01 us  [body(): lax.psum_scatter(slabs, 'group', scatter_dimension=1, tiled=True)]
    all_to_all x0 -> x2, blocking collectives: none -> 31.7 us  [the longest x1 17.7 us: body(): lax.all_to_all(row_pieces, 'row', 0, 0, tiled=True).astype(jnp.float32)]
    all_to_all x2, waiting for transfers between devices: 10.5 us -> 26.2 us  [exchange_sum(): mine = jnp.sum(lax.all_to_all(pieces, axis, 0, 0, tiled=True), axis=0)]
    all_to_all x1, waiting for transfers between devices: 36.3 us -> 51.3 us  [body(): lax.all_to_all(first_grad, 'group', split_axis=1, concat_axis=0, tiled=True)]
    all_to_all x2 -> x0, starting transfers between devices: 14.6 us -> none  [the longest x1 8.85 us: group_all_reduce(): mine = jnp.sum(lax.all_to_all(pieces, 'group', 0, 0, tiled=True), axis=0)]
    all_to_all x2 -> x0, waiting for transfers between devices: 12.9 us -> none  [the longest x1 7.9 us: group_all_reduce(): mine = jnp.sum(lax.all_to_all(pieces, 'group', 0, 0, tiled=True), axis=0)]
    dot_general x0 -> x2, local copies, waits for them, and re-layouts: none -> 5.61 us  [the longest x1 3.15 us: body(): lax.dot_general(mix_grad, hidden, (((0,), (0,)), ((), ())), preferred_ele...]
    transpose x0 -> x2, local copies, waits for them, and re-layouts: none -> 4.13 us  [the longest x1 3.13 us: body(): slabs.reshape(count, row_count_axis, groups, piece, rank)]
  transfers between devices with their start and end apart: 10 -> 8, of which waited for: 9 -> 7; matrix products, arithmetic and copies ran while one was open for 8% -> 8% of each run, Pallas kernels for 0% -> 0%
where the time goes in v3:
time: 333 us; the launch traced here: 332 us
  waiting for transfers between devices  175 us (53%)
  starting transfers between devices  50.7 us (15%)
  blocking collectives  31.7 us (10%)
  matrix products  23.8 us (7%)
  local copies, waits for them, and re-layouts  19.3 us (6%)
  other arithmetic  16.9 us (5%)
  between operations  14.4 us (4%)
    all_to_all x1, waiting for transfers between devices, body(): lax.all_to_all(first_grad, 'group', split_axis=1, concat_axis=0, tiled=True)  51.3 us
    all_gather x1, waiting for transfers between devices, body(): lax.all_gather(jnp.concatenate([down_weight, up_weight], axis=0), 'row',...  36.2 us
    all_to_all x1, waiting for transfers between devices, body(): lax.all_to_all(projected, 'group', split_axis=0, concat_axis=1, tiled=True)  36.1 us
    all_to_all x2, waiting for transfers between devices, exchange_sum(): mine = jnp.sum(lax.all_to_all(pieces, axis, 0, 0, tiled=True), axis=0)  26.2 us
    all_to_all x2, waiting for transfers between devices, exchange_sum(): return lax.all_to_all(spread, axis, 0, 0, tiled=True).reshape(partial.shape)  25.4 us
    all_to_all x1, blocking collectives, body(): lax.all_to_all(row_pieces, 'row', 0, 0, tiled=True).astype(jnp.float32)  17.7 us
    all_to_all x2, starting transfers between devices, exchange_sum(): mine = jnp.sum(lax.all_to_all(pieces, axis, 0, 0, tiled=True), axis=0)  16.3 us
    all_to_all x1, blocking collectives, body(): gathered = lax.all_to_all(spread, 'group', 0, 0, tiled=True)  14 us
  transfers between devices with their start and end apart: 8, of which 7 were waited for; matrix products, arithmetic and copies ran while one was open for 8% of the time, Pallas kernels for 0%

profile of v3, /device:TPU:2, one launch (start us, length us, event | category | flops | bytes accessed | tf_op | source)
XLA Modules:
  0.0 332.0 jit_solution(16017245443222324255)
XLA Ops:
  10.9 8.9 %scatter_custom_fusion = bf16[3072,128]{1,0:T(8,128)(2,1)S(1)} fusion(s32[3072]{0:T(1024)S(1)} %bitcast.133, f32[3072,128]{1,0:T(8,128)} %param.11, f32[128]{0:T(128)S(1)} %get-tuple-element.21, f32[128]{0:T(128)S(1)} %get-tuple-element.20, bf16[]{:T(256)} %constant.0.clone.1), kind=kCustom, calls=%fused_computation.50 | custom fusion | flops 1179648 | bytes 2360322 | tf_op jit(solution)/shard_map/scatter | solution.py:40
  21.6 11.8 %all-to-all-start = ((bf16[16,192,256]{2,1,0:T(8,128)(2,1)}), bf16[16,192,256]{2,1,0:T(8,128)(2,1)S(1)}, u32[]{:S(2)}, u32[]{:S(2)}) async-start(bf16[16,192,256]{2,1,0:T(8,128)(2,1)} %bitcast.122), calls=%async_computation | async-start | bytes 3145728 | tf_op jit(solution)/shard_map/all_to_all | solution.py:44
  33.7 36.1 %all-to-all-done = bf16[16,192,256]{2,1,0:T(8,128)(2,1)S(1)} async-done(((bf16[16,192,256]{2,1,0:T(8,128)(2,1)}), bf16[16,192,256]{2,1,0:T(8,128)(2,1)S(1)}, u32[]{:S(2)}, u32[]{:S(2)}) %all-to-all-start) | async-done | bytes 1572896 | tf_op jit(solution)/shard_map/all_to_all | solution.py:44
  70.0 2.5 copy.36
  72.5 36.2 %all-gather.2.cloned.1.call-done = bf16[4,4096,128]{2,1,0:T(8,128)(2,1)} async-done(((bf16[4,128,128]{2,1,0:T(8,128)(2,1)}), bf16[4,4096,128]{2,1,0:T(8,128)(2,1)}) %all-gather.2.cloned.1.call-update) | async-done | bytes 4194320 | tf_op jit(solution)/shard_map/all_gather | solution.py:48
  110.4 3.8 %fusion.7 = (bf16[192,4096]{1,0:T(8,128)(2,1)S(1)}, f32[192,4096]{1,0:T(8,128)}) fusion(bf16[192,4096]{1,0:T(8,128)(2,1)S(1)} %bitcast.113, f32[4096]{0:T(1024)S(1)} %bitcast.131, bf16[192,128]{1,0:T(8,128)(2,1)S(1)} %convolution_convert_fusion.8, bf16[4,4096,128]{2,1,0:T(8,128)(2,1)} %all-gather.2.cloned.1.call-done), kind=kOutput, calls=%fused_computation.22 | convolution fusion | flops 205258752 | bytes 7405568 | tf_op jit(solution)/shard_map/dot_general | solution.py:56
  114.8 2.7 multiply_reduce_fusion
  120.3 2.1 convert_reduce_fusion.1
  124.2 3.1 copy.35
  128.1 2.3 convolution_convert_fusion.5
  131.8 3.1 copy.37
  136.8 4.0 %fusion.5 = bf16[192,4096]{1,0:T(8,128)(2,1)S(1)} fusion(f32[192,4096]{1,0:T(8,128)S(1)} %copy-done.2, bf16[192,128]{1,0:T(8,128)(2,1)S(1)} %convolution_convert_fusion.5, f32[192,4096]{1,0:T(8,128)} %get-tuple-element.25, f32[192,4096]{1,0:T(8,128)} %get-tuple-element.23, f32[192]{0:T(256)S(1)} %fusion.27, f32[4096]{0:T(1024)S(1)} %copy-done.9, ...), kind=kOutput, calls=%fused_computation.15 | convolution fusion | flops 209977344 | bytes 12124928 | tf_op jit(solution)/shard_map/dot_general | solution.py:86
  142.2 8.9 %all-to-all-start.1 = ((bf16[192,16,256]{2,0,1:T(8,128)(2,1)}), bf16[192,16,256]{2,0,1:T(8,128)(2,1)S(1)}, u32[]{:S(2)}, u32[]{:S(2)}) async-start(bf16[192,16,256]{2,0,1:T(8,128)(2,1)} %bitcast.121), calls=%async_computation.2 | async-start | bytes 3145728 | tf_op jit(solution)/shard_map/all_to_all | solution.py:103
  151.9 51.3 %all-to-all-done.1 = bf16[192,16,256]{2,0,1:T(8,128)(2,1)S(1)} async-done(((bf16[192,16,256]{2,0,1:T(8,128)(2,1)}), bf16[192,16,256]{2,0,1:T(8,128)(2,1)S(1)}, u32[]{:S(2)}, u32[]{:S(2)}) %all-to-all-start.1) | async-done | bytes 1572896 | tf_op jit(solution)/shard_map/all_to_all | solution.py:103
  203.2 12.1 %all-to-all-start.4 = ((f32[512,1,16]{2,1,0:T(1,128)}), f32[512,1,16]{2,1,0:T(1,128)S(1)}, u32[]{:S(2)}, u32[]{:S(2)}) async-start(f32[512,1,16]{2,1,0:T(1,128)} %bitcast.31), calls=%async_computation.5 | async-start | bytes 524288 | tf_op jit(solution)/shard_map/all_to_all | solution.py:15
  216.5 14.8 %all-to-all-done.4 = f32[512,1,16]{2,1,0:T(1,128)S(1)} async-done(((f32[512,1,16]{2,1,0:T(1,128)}), f32[512,1,16]{2,1,0:T(1,128)S(1)}, u32[]{:S(2)}, u32[]{:S(2)}) %all-to-all-start.4) | async-done | bytes 32800 | tf_op jit(solution)/shard_map/all_to_all | solution.py:15
  231.3 4.2 %all-to-all-start.2 = ((f32[32,1,1024]{2,1,0:T(1,128)}), f32[32,1,1024]{2,1,0:T(1,128)S(1)}, u32[]{:S(2)}, u32[]{:S(2)}) async-start(f32[32,1,1024]{2,1,0:T(1,128)} %all_to_all.70), calls=%async_computation.3 | async-start | bytes 262144 | tf_op jit(solution)/shard_map/all_to_all | solution.py:15
  236.0 11.4 %all-to-all-done.2 = f32[32,1,1024]{2,1,0:T(1,128)S(1)} async-done(((f32[32,1,1024]{2,1,0:T(1,128)}), f32[32,1,1024]{2,1,0:T(1,128)S(1)}, u32[]{:S(2)}, u32[]{:S(2)}) %all-to-all-start.2) | async-done | bytes 131104 | tf_op jit(solution)/shard_map/all_to_all | solution.py:15
  248.3 9.4 %all-to-all-start.5 = ((f32[512,1,16]{2,1,0:T(1,128)}), f32[512,1,16]{2,1,0:T(1,128)S(1)}, u32[]{:S(2)}, u32[]{:S(2)}) async-start(f32[512,1,16]{2,1,0:T(1,128)} %broadcast_in_dim.10), calls=%async_computation.6 | async-start | bytes 524288 | tf_op jit(solution)/shard_map/all_to_all | solution.py:17
  257.8 16.0 %all-to-all-done.5 = f32[512,1,16]{2,1,0:T(1,128)S(1)} async-done(((f32[512,1,16]{2,1,0:T(1,128)}), f32[512,1,16]{2,1,0:T(1,128)S(1)}, u32[]{:S(2)}, u32[]{:S(2)}) %all-to-all-start.5) | async-done | bytes 32800 | tf_op jit(solution)/shard_map/all_to_all | solution.py:17
  274.5 4.2 %all-to-all-start.3 = ((f32[32,1,1024]{2,1,0:T(1,128)}), f32[32,1,1024]{2,1,0:T(1,128)S(1)}, u32[]{:S(2)}, u32[]{:S(2)}) async-start(f32[32,1,1024]{2,1,0:T(1,128)} %broadcast_in_dim.9), calls=%async_computation.4 | async-start | bytes 262144 | tf_op jit(solution)/shard_map/all_to_all | solution.py:17
  281.3 9.4 %all-to-all-done.3 = f32[32,1,1024]{2,1,0:T(1,128)S(1)} async-done(((f32[32,1,1024]{2,1,0:T(1,128)}), f32[32,1,1024]{2,1,0:T(1,128)S(1)}, u32[]{:S(2)}, u32[]{:S(2)}) %all-to-all-start.3) | async-done | bytes 131104 | tf_op jit(solution)/shard_map/all_to_all | solution.py:17
  292.7 17.7 %all_to_all.79 = bf16[32,4,8,128]{3,2,1,0:T(8,128)(2,1)S(1)} all-to-all(bf16[32,4,8,128]{3,2,1,0:T(8,128)(2,1)S(1)} %copy_bitcast_fusion.2), channel_id=1, replica_groups=mesh['group'=16,'row'=32] {'row'}, dimensions={0} | all-to-all | bytes 524288 | tf_op jit(solution)/shard_map/all_to_all | solution.py:111
  310.4 14.0 %all_to_all.80 = f32[16,4,8,128]{3,2,1,0:T(8,128)S(1)} all-to-all(f32[16,4,8,128]{3,2,1,0:T(8,128)S(1)} %broadcast_in_dim.11), channel_id=1, replica_groups=mesh['group'=16,'row'=32] {'group'}, dimensions={0} | all-to-all | bytes 524288 | tf_op jit(solution)/shard_map/all_to_all | solution.py:113
  (71 shorter events, 27.7 us)
Async XLA Ops:
  7.2 12.7 %copy-start = (bf16[128,256]{1,0:T(8,128)(2,1)S(1)}, bf16[128,256]{1,0:T(8,128)(2,1)}, u32[]{:S(2)}) copy-start(bf16[128,256]{1,0:T(8,128)(2,1)} %param.15) | copy-start | bytes 196612
  7.2 101.5 %all-gather.2.cloned.1.call-start = ((), (), s32[]{:S(2)}) async-start(), calls=%async_computation.9 | async-start | bytes 4325376 | tf_op jit(solution)/shard_map/all_gather | solution.py:48
  19.8 50.0 %copy-start.4 = (bf16[3072,128]{1,0:T(8,128)(2,1)}, bf16[3072,128]{1,0:T(8,128)(2,1)S(1)}, u32[]{:S(2)}) copy-start(bf16[3072,128]{1,0:T(8,128)(2,1)S(1)} %scatter_custom_fusion) | copy-start | bytes 2359300
  19.8 13.8 %copy-start.9 = (f32[4096]{0:T(1024)S(1)}, f32[4096]{0:T(1024)}, u32[]{:S(2)}) copy-start(f32[4096]{0:T(1024)} %param.20) | copy-start | bytes 49156
  19.8 13.8 %copy-start.10 = (f32[2,4096]{1,0:T(2,128)S(1)}, f32[2,4096]{1,0:T(2,128)}, u32[]{:S(2)}) copy-start(f32[2,4096]{1,0:T(2,128)} %param.19) | copy-start | bytes 98308
  21.6 48.2 %all-to-all-start = ((bf16[16,192,256]{2,1,0:T(8,128)(2,1)}), bf16[16,192,256]{2,1,0:T(8,128)(2,1)S(1)}, u32[]{:S(2)}, u32[]{:S(2)}) async-start(bf16[16,192,256]{2,1,0:T(8,128)(2,1)} %bitcast.122), calls=%async_computation | async-start | bytes 3145728 | tf_op jit(solution)/shard_map/all_to_all | solution.py:44
  33.4 258.3 %reduce-scatter.2.cloned.1.call-start = ((), (), s32[]{:S(2)}) async-start(), calls=%async_computation.10 | async-start | bytes 4456448 | tf_op jit(solution)/shard_map/reduce_scatter | solution.py:101
  110.4 3.8 %copy-start.7 = (bf16[4,4096,128]{2,1,0:T(8,128)(2,1)S(1)}, bf16[4,4096,128]{2,1,0:T(8,128)(2,1)}, u32[]{:S(2)}) copy-start(bf16[4,4096,128]{2,1,0:T(8,128)(2,1)} %all-gather.2.cloned.1.call-done) | copy-start | bytes 12582916
  114.8 2.7 copy-start.12
  117.5 0.9 copy-start.11
  120.3 2.2 copy-start.1
  122.5 1.8 copy-start.6
  127.4 3.1 copy-start.3
  128.1 3.1 copy-start.8
  134.9 1.9 copy-start.2
  140.8 74.5 %copy-start.5 = (bf16[3072,128]{1,0:T(8,128)(2,1)S(1)}, bf16[3072,128]{1,0:T(8,128)(2,1)}, u32[]{:S(2)}) copy-start(bf16[3072,128]{1,0:T(8,128)(2,1)} %copy-done.4) | copy-start | bytes 2359300
  142.2 61.1 %all-to-all-start.1 = ((bf16[192,16,256]{2,0,1:T(8,128)(2,1)}), bf16[192,16,256]{2,0,1:T(8,128)(2,1)S(1)}, u32[]{:S(2)}, u32[]{:S(2)}) async-start(bf16[192,16,256]{2,0,1:T(8,128)(2,1)} %bitcast.121), calls=%async_computation.2 | async-start | bytes 3145728 | tf_op jit(solution)/shard_map/all_to_all | solution.py:103
  203.2 28.1 %all-to-all-start.4 = ((f32[512,1,16]{2,1,0:T(1,128)}), f32[512,1,16]{2,1,0:T(1,128)S(1)}, u32[]{:S(2)}, u32[]{:S(2)}) async-start(f32[512,1,16]{2,1,0:T(1,128)} %bitcast.31), calls=%async_computation.5 | async-start | bytes 524288 | tf_op jit(solution)/shard_map/all_to_all | solution.py:15
  231.3 16.1 %all-to-all-start.2 = ((f32[32,1,1024]{2,1,0:T(1,128)}), f32[32,1,1024]{2,1,0:T(1,128)S(1)}, u32[]{:S(2)}, u32[]{:S(2)}) async-start(f32[32,1,1024]{2,1,0:T(1,128)} %all_to_all.70), calls=%async_computation.3 | async-start | bytes 262144 | tf_op jit(solution)/shard_map/all_to_all | solution.py:15
  248.3 25.5 %all-to-all-start.5 = ((f32[512,1,16]{2,1,0:T(1,128)}), f32[512,1,16]{2,1,0:T(1,128)S(1)}, u32[]{:S(2)}, u32[]{:S(2)}) async-start(f32[512,1,16]{2,1,0:T(1,128)} %broadcast_in_dim.10), calls=%async_computation.6 | async-start | bytes 524288 | tf_op jit(solution)/shard_map/all_to_all | solution.py:17
  274.5 16.2 %all-to-all-start.3 = ((f32[32,1,1024]{2,1,0:T(1,128)}), f32[32,1,1024]{2,1,0:T(1,128)S(1)}, u32[]{:S(2)}, u32[]{:S(2)}) async-start(f32[32,1,1024]{2,1,0:T(1,128)} %broadcast_in_dim.9), calls=%async_computation.4 | async-start | bytes 262144 | tf_op jit(solution)/shard_map/all_to_all | solution.py:17
Sparse Core Ops, SparseCore 0:
  12.0 96.5 all-gather.1
  135.1 111.8 reduce-scatter.1

commit v4 on v2

--- a/solution.py
+++ b/solution.py
@@ -88,24 +88,15 @@
     block_rows = width // row_count_axis
     piece = block_rows // groups
     bias_all = jnp.stack(bias_terms)
-    bias_slab = jnp.zeros((row_count_axis, block_rows, rank), jnp.float32)
-    bias_slab = bias_slab.at[:, :layers, :].set(
-        bias_all.reshape(layers, row_count_axis, block_rows).transpose(1, 0, 2)
-    )
-    slabs = jnp.concatenate([jnp.stack(up_parts + down_parts), bias_slab.reshape(1, width, rank)])
+    bias_slab = jnp.pad(
+        bias_all.reshape(layers, row_count_axis, block_rows).transpose(1, 0, 2),
+        ((0, 0), (0, block_rows - layers), (0, rank - block_rows)),
+    ).reshape(1, width, rank)
+    slabs = jnp.concatenate([jnp.stack(up_parts + down_parts), bias_slab]).astype(jnp.bfloat16)
     count = slabs.shape[0]
-    slabs = slabs.astype(jnp.bfloat16).reshape(count, row_count_axis, groups, piece, rank)
-    slabs = slabs.transpose(0, 2, 1, 3, 4).reshape(count, width, rank)
+    slabs = slabs.reshape(count, row_count_axis, groups, piece, rank).transpose(0, 2, 1, 3, 4)
+    slabs = slabs.reshape(count, width, rank)
     group_part = lax.psum_scatter(slabs, "group", scatter_dimension=1, tiled=True)
-    row_pieces = group_part.reshape(count, row_count_axis, piece, rank).transpose(1, 0, 2, 3)
-    mine = jnp.sum(
-        lax.all_to_all(row_pieces.astype(jnp.float32), "row", 0, 0, tiled=True), axis=0
-    )
-    spread = jnp.broadcast_to(mine[None], (groups,) + mine.shape)
-    gathered = lax.all_to_all(spread, "group", 0, 0, tiled=True)
-    blocks = gathered.transpose(1, 0, 2, 3).reshape(count, block_rows, rank)
-    grad_up, grad_down = blocks[:layers], blocks[layers : 2 * layers]
-    bias_rows = blocks[2 * layers, :layers, :]
     first_grad = (first_grad + back.astype(jnp.float32)).astype(jnp.bfloat16)
     owner_grad = lax.all_to_all(first_grad, "group", split_axis=1, concat_axis=0, tiled=True)
     proj_term = lax.dot_general(
@@ -113,6 +104,14 @@
     )
     proj_pieces = proj_term.reshape(row_count_axis, -1)
     proj_mine = jnp.sum(lax.all_to_all(proj_pieces, "row", 0, 0, tiled=True), axis=0)
+    group_part, proj_mine = lax.optimization_barrier((group_part, proj_mine))
+    row_pieces = group_part.reshape(count, row_count_axis, piece, rank).transpose(1, 0, 2, 3)
+    mine = jnp.sum(lax.all_to_all(row_pieces, "row", 0, 0, tiled=True).astype(jnp.float32), axis=0)
+    spread = jnp.broadcast_to(mine[None], (groups,) + mine.shape)
+    gathered = lax.all_to_all(spread, "group", 0, 0, tiled=True)
+    blocks = gathered.transpose(1, 0, 2, 3).reshape(count, block_rows, rank)
+    grad_up, grad_down = blocks[:layers], blocks[layers : 2 * layers]
+    bias_rows = blocks[2 * layers, :layers, :]
     last = jnp.concatenate([proj_mine, bias_rows.reshape(-1)])
     last_all = lax.all_to_all(
         jnp.broadcast_to(last[None], (row_count_axis,) + last.shape), "row", 0, 0, tiled=True

time: 351 us -> 326 us (0.929)
  the two profiles are of different devices: /device:TPU:2 before, /device:TPU:1 now
where the time goes in v4:
time: 326 us
  blocking collectives  122 us (37%)
  waiting for transfers between devices  103 us (32%)
  matrix products  29.2 us (9%)
  local copies, waits for them, and re-layouts  22.4 us (7%)
  starting transfers between devices  19.8 us (6%)
  between operations  14.4 us (4%)
  other arithmetic  14.2 us (4%)
    all_to_all x1, blocking collectives, body(): lax.all_to_all(first_grad, 'group', split_axis=1, concat_axis=0, tiled=True)  62 us
    all_gather x1, waiting for transfers between devices, body(): lax.all_gather(jnp.concatenate([down_weight, up_weight], axis=0), 'row',...  38.3 us
    all_to_all x1, waiting for transfers between devices, body(): lax.all_to_all(projected, 'group', split_axis=0, concat_axis=1, tiled=True)  36.1 us
    all_to_all x1, blocking collectives, body(): lax.all_to_all(row_pieces, 'row', 0, 0, tiled=True).astype(jnp.float32)  29.6 us
    all_to_all x1, blocking collectives, body(): lax.all_to_all(proj_pieces, 'row', 0, 0, tiled=True)  19.2 us
    reduce_scatter x1, waiting for transfers between devices, body(): lax.psum_scatter(slabs, 'group', scatter_dimension=1, tiled=True)  18.4 us
    all_to_all x1, starting transfers between devices, body(): lax.all_to_all(projected, 'group', split_axis=0, concat_axis=1, tiled=True)  11.9 us
    all_to_all x1, blocking collectives, body(): gathered = lax.all_to_all(spread, 'group', 0, 0, tiled=True)  11.6 us
  transfers between devices with their start and end apart: 4, of which 4 were waited for; matrix products, arithmetic and copies ran while one was open for 6% of the time, Pallas kernels for 0%

profile of v4, /device:TPU:1, one launch (start us, length us, event | category | flops | bytes accessed | tf_op | source)
XLA Modules:
  0.0 325.7 jit_solution(17141510417800995065)
XLA Ops:
  10.9 8.9 %scatter_custom_fusion = bf16[3072,128]{1,0:T(8,128)(2,1)S(1)} fusion(s32[3072]{0:T(1024)S(1)} %bitcast.153, f32[3072,128]{1,0:T(8,128)} %param.11, f32[128]{0:T(128)S(1)} %get-tuple-element.18, f32[128]{0:T(128)S(1)} %get-tuple-element.17, bf16[]{:T(256)} %constant.6.clone.1), kind=kCustom, calls=%fused_computation.51 | custom fusion | flops 1179648 | bytes 2360322 | tf_op jit(solution)/shard_map/scatter | solution.py:33
  21.6 11.9 %all-to-all-start = ((bf16[16,192,256]{2,1,0:T(8,128)(2,1)}), bf16[16,192,256]{2,1,0:T(8,128)(2,1)S(1)}, u32[]{:S(2)}, u32[]{:S(2)}) async-start(bf16[16,192,256]{2,1,0:T(8,128)(2,1)} %bitcast.6), calls=%async_computation | async-start | bytes 3145728 | tf_op jit(solution)/shard_map/all_to_all | solution.py:37
  33.6 36.1 %all-to-all-done = bf16[16,192,256]{2,1,0:T(8,128)(2,1)S(1)} async-done(((bf16[16,192,256]{2,1,0:T(8,128)(2,1)}), bf16[16,192,256]{2,1,0:T(8,128)(2,1)S(1)}, u32[]{:S(2)}, u32[]{:S(2)}) %all-to-all-start) | async-done | bytes 1572896 | tf_op jit(solution)/shard_map/all_to_all | solution.py:37
  69.9 2.6 copy.40
  72.5 38.3 %all-gather.2.cloned.1.call-done = bf16[4,4096,128]{2,1,0:T(8,128)(2,1)} async-done(((bf16[4,128,128]{2,1,0:T(8,128)(2,1)}), bf16[4,4096,128]{2,1,0:T(8,128)(2,1)}) %all-gather.2.cloned.1.call-update) | async-done | bytes 4194320 | tf_op jit(solution)/shard_map/all_gather | solution.py:41
  110.8 1.8 convolution_convert_fusion.8
  112.6 3.7 %fusion.7 = (bf16[192,4096]{1,0:T(8,128)(2,1)S(1)}, f32[192,4096]{1,0:T(8,128)}) fusion(bf16[192,4096]{1,0:T(8,128)(2,1)S(1)} %bitcast.130, f32[4096]{0:T(1024)S(1)} %bitcast.150, bf16[192,128]{1,0:T(8,128)(2,1)S(1)} %convolution_convert_fusion.8, bf16[4,4096,128]{2,1,0:T(8,128)(2,1)} %all-gather.2.cloned.1.call-done), kind=kOutput, calls=%fused_computation.21 | convolution fusion | flops 205258752 | bytes 7405568 | tf_op jit(solution)/shard_map/dot_general | solution.py:49
  116.9 2.6 multiply_reduce_fusion
  122.5 1.7 convolution_convert_fusion
  124.3 2.5 fusion.33
  129.8 2.4 copy.39
  132.8 3.4 %fusion.14 = bf16[5,32,16,8,128]{4,3,2,1,0:T(8,128)(2,1)} fusion(bf16[5,32,16,8,128]{4,3,2,1,0:T(8,128)(2,1)} %constant_dynamic-update-slice_fusion.1, bf16[32,16,8,192]{3,2,1,0:T(8,128)(2,1)} %bitcast.137, bf16[192,128]{1,0:T(8,128)(2,1)S(1)} %convolution_convert_fusion.7), kind=kOutput, calls=%fused_computation.36 | convolution fusion | flops 201850880 | bytes 3194880 | tf_op jit(solution)/shard_map/dot_general | solution.py:69
  136.3 2.3 convolution_convert_fusion.5
  138.6 1.7 fusion.16
  142.7 6.2 %copy.42 = bf16[5,16,32,8,128]{4,3,2,1,0:T(8,128)(2,1)} copy(bf16[5,16,32,8,128]{4,3,1,2,0:T(8,128)(2,1)} %bitcast.138) | data formatting | bytes 10485760 | tf_op jit(solution)/shard_map/transpose | solution.py:97
  149.0 1.9 copy-done.1
  150.8 4.0 %fusion.5 = bf16[192,4096]{1,0:T(8,128)(2,1)S(1)} fusion(f32[192,4096]{1,0:T(8,128)} %get-tuple-element.23, bf16[192,128]{1,0:T(8,128)(2,1)S(1)} %convolution_convert_fusion.5, f32[192,4096]{1,0:T(8,128)} %get-tuple-element.22, f32[192,4096]{1,0:T(8,128)S(1)} %copy-done.1, f32[192]{0:T(256)S(1)} %fusion.31, f32[4096]{0:T(1024)S(1)} %copy-done.9, ...), kind=kOutput, calls=%fused_computation.15 | convolution fusion | flops 209977344 | bytes 12124928 | tf_op jit(solution)/shard_map/dot_general | solution.py:79
  155.0 62.0 %all_to_all.67 = bf16[192,16,256]{2,0,1:T(8,128)(2,1)S(1)} all-to-all(bf16[192,16,256]{2,0,1:T(8,128)(2,1)S(1)} %bitcast.141), channel_id=1, replica_groups=mesh['group'=16,'row'=32] {'group'}, dimensions={1} | all-to-all | bytes 3145728 | tf_op jit(solution)/shard_map/all_to_all | solution.py:101
  217.6 19.2 %all_to_all.68 = f32[32,1,1024]{2,1,0:T(1,128)S(1)} all-to-all(f32[32,1,1024]{2,1,0:T(1,128)S(1)} %all_to_all.60), channel_id=1, replica_groups=mesh['group'=16,'row'=32] {'row'}, dimensions={0} | all-to-all | bytes 262144 | tf_op jit(solution)/shard_map/all_to_all | solution.py:106
  236.9 18.4 %reduce-scatter.2.cloned.1.call-done = bf16[5,256,128]{2,1,0:T(8,128)(2,1)} async-done(((bf16[5,4096,128]{2,1,0:T(8,128)(2,1)}), bf16[5,256,128]{2,1,0:T(8,128)(2,1)}) %reduce-scatter.2.cloned.1.call-update) | async-done | bytes 327696 | tf_op jit(solution)/shard_map/reduce_scatter | solution.py:99
  256.4 29.6 %all_to_all.69 = bf16[32,5,8,128]{3,2,1,0:T(8,128)(2,1)S(1)} all-to-all(bf16[32,5,8,128]{3,2,1,0:T(8,128)(2,1)S(1)} %copy_bitcast_fusion.1), channel_id=1, replica_groups=mesh['group'=16,'row'=32] {'row'}, dimensions={0} | all-to-all | bytes 655360 | tf_op jit(solution)/shard_map/all_to_all | solution.py:109
  286.1 11.6 %all_to_all.70 = f32[16,5,8,128]{3,2,1,0:T(8,128)S(1)} all-to-all(f32[16,5,8,128]{3,2,1,0:T(8,128)S(1)} %broadcast_in_dim.7), channel_id=1, replica_groups=mesh['group'=16,'row'=32] {'group'}, dimensions={0} | all-to-all | bytes 655360 | tf_op jit(solution)/shard_map/all_to_all | solution.py:111
  298.5 7.8 %all-to-all-start.5 = ((f32[32,1,1280]{2,1,0:T(1,128)}), f32[32,1,1280]{2,1,0:T(1,128)S(1)}, u32[]{:S(2)}, u32[]{:S(2)}) async-start(f32[32,1,1280]{2,1,0:T(1,128)} %broadcast_in_dim.8), calls=%async_computation.6 | async-start | bytes 327680 | tf_op jit(solution)/shard_map/all_to_all | solution.py:116
  307.0 10.5 %all-to-all-done.5 = f32[32,1,1280]{2,1,0:T(1,128)S(1)} async-done(((f32[32,1,1280]{2,1,0:T(1,128)}), f32[32,1,1280]{2,1,0:T(1,128)S(1)}, u32[]{:S(2)}, u32[]{:S(2)}) %all-to-all-start.5) | async-done | bytes 163872 | tf_op jit(solution)/shard_map/all_to_all | solution.py:116
  (68 shorter events, 20.1 us)
Async XLA Ops:
  7.2 12.7 %copy-start = (bf16[128,256]{1,0:T(8,128)(2,1)S(1)}, bf16[128,256]{1,0:T(8,128)(2,1)}, u32[]{:S(2)}) copy-start(bf16[128,256]{1,0:T(8,128)(2,1)} %param.15) | copy-start | bytes 196612
  7.2 103.7 %all-gather.2.cloned.1.call-start = ((), (), s32[]{:S(2)}) async-start(), calls=%async_computation.7 | async-start | bytes 4325376 | tf_op jit(solution)/shard_map/all_gather | solution.py:41
  19.8 1.7 copy-start.3
  19.8 13.7 %copy-start.9 = (f32[4096]{0:T(1024)S(1)}, f32[4096]{0:T(1024)}, u32[]{:S(2)}) copy-start(f32[4096]{0:T(1024)} %param.20) | copy-start | bytes 49156
  19.8 13.7 %copy-start.10 = (f32[2,4096]{1,0:T(2,128)S(1)}, f32[2,4096]{1,0:T(2,128)}, u32[]{:S(2)}) copy-start(f32[2,4096]{1,0:T(2,128)} %param.19) | copy-start | bytes 98308
  21.6 48.1 %all-to-all-start = ((bf16[16,192,256]{2,1,0:T(8,128)(2,1)}), bf16[16,192,256]{2,1,0:T(8,128)(2,1)S(1)}, u32[]{:S(2)}, u32[]{:S(2)}) async-start(bf16[16,192,256]{2,1,0:T(8,128)(2,1)} %bitcast.6), calls=%async_computation | async-start | bytes 3145728 | tf_op jit(solution)/shard_map/all_to_all | solution.py:37
  33.5 221.9 %reduce-scatter.2.cloned.1.call-start = ((), (), s32[]{:S(2)}) async-start(), calls=%async_computation.8 | async-start | bytes 5570560 | tf_op jit(solution)/shard_map/reduce_scatter | solution.py:99
  112.6 3.7 %copy-start.7 = (bf16[4,4096,128]{2,1,0:T(8,128)(2,1)S(1)}, bf16[4,4096,128]{2,1,0:T(8,128)(2,1)}, u32[]{:S(2)}) copy-start(bf16[4,4096,128]{2,1,0:T(8,128)(2,1)} %all-gather.2.cloned.1.call-done) | copy-start | bytes 12582916
  116.9 2.6 copy-start.12
  119.5 2.3 copy-start.11
  126.7 1.3 copy-start.6
  126.7 3.1 copy-start.5
  132.8 5.8 %copy-start.2 = (bf16[4096,192]{1,0:T(8,128)(2,1)S(1)}, bf16[4096,192]{1,0:T(8,128)(2,1)}, u32[]{:S(2)}) copy-start(bf16[4096,192]{1,0:T(8,128)(2,1)} %copy.40) | copy-start | bytes 4718596
  136.3 4.1 %copy-start.8 = (bf16[4096,128]{1,0:T(8,128)(2,1)S(1)}, bf16[4096,128]{1,0:T(8,128)(2,1)}, u32[]{:S(2)}) copy-start(bf16[4096,128]{1,0:T(8,128)(2,1)} %convolution_convert_fusion) | copy-start | bytes 3145732
  148.9 1.9 copy-start.1
  154.8 62.2 %copy-start.4 = (bf16[3072,128]{1,0:T(8,128)(2,1)S(1)}, bf16[3072,128]{1,0:T(8,128)(2,1)}, u32[]{:S(2)}) copy-start(bf16[3072,128]{1,0:T(8,128)(2,1)} %copy-done.3) | copy-start | bytes 2359300
  298.5 19.0 %all-to-all-start.5 = ((f32[32,1,1280]{2,1,0:T(1,128)}), f32[32,1,1280]{2,1,0:T(1,128)S(1)}, u32[]{:S(2)}, u32[]{:S(2)}) async-start(f32[32,1,1280]{2,1,0:T(1,128)} %broadcast_in_dim.8), calls=%async_computation.6 | async-start | bytes 327680 | tf_op jit(solution)/shard_map/all_to_all | solution.py:116
Sparse Core Ops, SparseCore 0:
  12.0 98.7 all-gather.1
  149.1 106.2 reduce-scatter.1

commit v5 on v1

--- a/solution.py
+++ b/solution.py
@@ -20,7 +20,7 @@
 def group_all_reduce(rows, groups):
     stacked, height, width = rows.shape
     pieces = rows.reshape(stacked, groups, height // groups, width).transpose(1, 0, 2, 3)
-    mine = jnp.sum(lax.all_to_all(pieces, "group", 0, 0, tiled=True), axis=0)
+    mine = jnp.sum(lax.all_to_all(pieces, "group", 0, 0, tiled=True).astype(jnp.float32), axis=0)
     spread = jnp.broadcast_to(mine[None], pieces.shape)
     gathered = lax.all_to_all(spread, "group", 0, 0, tiled=True)
     return gathered.transpose(1, 0, 2, 3).reshape(rows.shape)
@@ -101,8 +101,6 @@
     weight_rows = lax.psum_scatter(
         jnp.stack(up_parts + down_parts).astype(jnp.bfloat16), "row", scatter_dimension=1, tiled=True
     )
-    weight_sums = group_all_reduce(weight_rows.astype(jnp.float32), groups)
-    grad_up, grad_down = weight_sums[:layers], weight_sums[layers:]
     first_grad = (first_grad + back.astype(jnp.float32)).astype(jnp.bfloat16)
     owner_grad = lax.all_to_all(first_grad, "group", split_axis=1, concat_axis=0, tiled=True)
     proj_term = lax.dot_general(
@@ -111,6 +109,9 @@
     grad_proj = exchange_sum(proj_term, "row", lax.axis_size("row"))
     bias_all = jnp.stack(bias_terms)
     grad_bias = exchange_sum(bias_all, ("group", "row"), groups * lax.axis_size("row"))
+    weight_rows, grad_proj, grad_bias = lax.optimization_barrier((weight_rows, grad_proj, grad_bias))
+    weight_sums = group_all_reduce(weight_rows, groups)
+    grad_up, grad_down = weight_sums[:layers], weight_sums[layers:]
     return (logits, grad_down, grad_up, grad_bias, grad_proj)
 
 

time: 330 us -> 306 us (0.927)
  waiting for transfers between devices: 196 us -> 164 us
  blocking collectives: 0 us -> 25.4 us
  starting transfers between devices: 68.8 us -> 51.7 us
    reduce_scatter x1, waiting for transfers between devices: 33.2 us -> 0.01 us  [body(): lax.psum_scatter(jnp.stack(up_parts + down_parts).astype(jnp.bfloat16), '...]
    all_to_all x0 -> x2, blocking collectives: none -> 25.4 us  [the longest x1 13.4 us: group_all_reduce(): lax.all_to_all(pieces, 'group', 0, 0, tiled=True).astype(jnp.float32)]
    all_to_all x2, waiting for transfers between devices: 10.5 us -> 26.2 us  [exchange_sum(): mine = jnp.sum(lax.all_to_all(pieces, axis, 0, 0, tiled=True), axis=0)]
    all_to_all x2 -> x0, starting transfers between devices: 14.6 us -> none  [the longest x1 8.85 us: group_all_reduce(): mine = jnp.sum(lax.all_to_all(pieces, 'group', 0, 0, tiled=True), axis=0)]
    all_to_all x2 -> x0, waiting for transfers between devices: 12.9 us -> none  [the longest x1 7.9 us: group_all_reduce(): mine = jnp.sum(lax.all_to_all(pieces, 'group', 0, 0, tiled=True), axis=0)]
    all_to_all x2, starting transfers between devices: 17.1 us -> 13.7 us  [exchange_sum(): return lax.all_to_all(spread, axis, 0, 0, tiled=True).reshape(partial.shape)]
  transfers between devices with their start and end apart: 10 -> 8, of which waited for: 9 -> 7; matrix products, arithmetic and copies ran while one was open for 8% -> 8% of each run, Pallas kernels for 0% -> 0%
where the time goes in v5:
time: 306 us; the launch traced here: 305 us
  waiting for transfers between devices  164 us (54%)
  starting transfers between devices  51.7 us (17%)
  blocking collectives  25.4 us (8%)
  matrix products  23.1 us (8%)
  other arithmetic  16.4 us (5%)
  between operations  14.3 us (5%)
  local copies, waits for them, and re-layouts  10.5 us (3%)
    all_gather x1, waiting for transfers between devices, body(): lax.all_gather(jnp.concatenate([down_weight, up_weight], axis=0), 'row',...  38.7 us
    all_to_all x1, waiting for transfers between devices, body(): lax.all_to_all(projected, 'group', split_axis=0, concat_axis=1, tiled=True)  36.1 us
    all_to_all x1, waiting for transfers between devices, body(): lax.all_to_all(first_grad, 'group', split_axis=1, concat_axis=0, tiled=True)  36 us
    all_to_all x2, waiting for transfers between devices, exchange_sum(): return lax.all_to_all(spread, axis, 0, 0, tiled=True).reshape(partial.shape)  26.5 us
    all_to_all x2, waiting for transfers between devices, exchange_sum(): mine = jnp.sum(lax.all_to_all(pieces, axis, 0, 0, tiled=True), axis=0)  26.2 us
    all_to_all x2, starting transfers between devices, exchange_sum(): mine = jnp.sum(lax.all_to_all(pieces, axis, 0, 0, tiled=True), axis=0)  17.1 us
    all_to_all x2, starting transfers between devices, exchange_sum(): return lax.all_to_all(spread, axis, 0, 0, tiled=True).reshape(partial.shape)  13.7 us
    all_to_all x1, blocking collectives, group_all_reduce(): lax.all_to_all(pieces, 'group', 0, 0, tiled=True).astype(jnp.float32)  13.4 us
  transfers between devices with their start and end apart: 8, of which 7 were waited for; matrix products, arithmetic and copies ran while one was open for 8% of the time, Pallas kernels for 0%

profile of v5, /device:TPU:2, one launch (start us, length us, event | category | flops | bytes accessed | tf_op | source)
XLA Modules:
  0.0 305.0 jit_solution(14732220837217697801)
XLA Ops:
  10.9 8.9 %scatter_custom_fusion = bf16[3072,128]{1,0:T(8,128)(2,1)S(1)} fusion(s32[3072]{0:T(1024)S(1)} %bitcast.114, f32[3072,128]{1,0:T(8,128)} %param.11, f32[128]{0:T(128)S(1)} %get-tuple-element.20, f32[128]{0:T(128)S(1)} %get-tuple-element.19, bf16[]{:T(256)} %constant.0.clone.1), kind=kCustom, calls=%fused_computation.53 | custom fusion | flops 1179648 | bytes 2360322 | tf_op jit(solution)/shard_map/scatter | solution.py:49
  19.9 1.7 convolution_convert_fusion.4
  21.6 11.8 %all-to-all-start = ((bf16[16,192,256]{2,1,0:T(8,128)(2,1)}), bf16[16,192,256]{2,1,0:T(8,128)(2,1)S(1)}, u32[]{:S(2)}, u32[]{:S(2)}) async-start(bf16[16,192,256]{2,1,0:T(8,128)(2,1)} %bitcast.105), calls=%async_computation | async-start | bytes 3145728 | tf_op jit(solution)/shard_map/all_to_all | solution.py:53
  33.7 36.1 %all-to-all-done = bf16[16,192,256]{2,1,0:T(8,128)(2,1)S(1)} async-done(((bf16[16,192,256]{2,1,0:T(8,128)(2,1)}), bf16[16,192,256]{2,1,0:T(8,128)(2,1)S(1)}, u32[]{:S(2)}, u32[]{:S(2)}) %all-to-all-start) | async-done | bytes 1572896 | tf_op jit(solution)/shard_map/all_to_all | solution.py:53
  70.0 38.7 %all-gather.2.cloned.1.call-done = bf16[4,4096,128]{2,1,0:T(8,128)(2,1)} async-done(((bf16[4,128,128]{2,1,0:T(8,128)(2,1)}), bf16[4,4096,128]{2,1,0:T(8,128)(2,1)}) %all-gather.2.cloned.1.call-update) | async-done | bytes 4194320 | tf_op jit(solution)/shard_map/all_gather | solution.py:57
  108.7 1.8 convolution_convert_fusion.8
  110.5 3.7 %fusion.11 = (bf16[192,4096]{1,0:T(8,128)(2,1)S(1)}, f32[192,4096]{1,0:T(8,128)}) fusion(bf16[192,4096]{1,0:T(8,128)(2,1)S(1)} %bitcast.97, f32[4096]{0:T(1024)S(1)} %bitcast.112, bf16[192,128]{1,0:T(8,128)(2,1)S(1)} %convolution_convert_fusion.8, bf16[4,4096,128]{2,1,0:T(8,128)(2,1)} %all-gather.2.cloned.1.call-done), kind=kOutput, calls=%fused_computation.28 | convolution fusion | flops 205258752 | bytes 7405568 | tf_op jit(solution)/shard_map/dot_general | solution.py:65
  114.7 2.7 multiply_reduce_fusion
  120.5 2.5 convert_reduce_fusion.1
  125.2 2.2 pad_maximum_fusion
  127.4 1.9 copy-done.1
  129.3 4.0 %fusion.5 = bf16[192,4096]{1,0:T(8,128)(2,1)S(1)} fusion(f32[192,4096]{1,0:T(8,128)} %get-tuple-element.25, bf16[192,128]{1,0:T(8,128)(2,1)S(1)} %convolution_convert_fusion.5, f32[192,4096]{1,0:T(8,128)} %get-tuple-element.24, f32[192,4096]{1,0:T(8,128)S(1)} %copy-done.1, f32[192]{0:T(256)S(1)} %fusion.29, f32[4096]{0:T(1024)S(1)} %copy-done.5, ...), kind=kOutput, calls=%fused_computation.15 | convolution fusion | flops 209977344 | bytes 12124928 | tf_op jit(solution)/shard_map/dot_general | solution.py:95
  134.7 8.9 %all-to-all-start.1 = ((bf16[192,16,256]{2,0,1:T(8,128)(2,1)}), bf16[192,16,256]{2,0,1:T(8,128)(2,1)S(1)}, u32[]{:S(2)}, u32[]{:S(2)}) async-start(bf16[192,16,256]{2,0,1:T(8,128)(2,1)} %bitcast.104), calls=%async_computation.2 | async-start | bytes 3145728 | tf_op jit(solution)/shard_map/all_to_all | solution.py:105
  144.4 36.0 %all-to-all-done.1 = bf16[192,16,256]{2,0,1:T(8,128)(2,1)S(1)} async-done(((bf16[192,16,256]{2,0,1:T(8,128)(2,1)}), bf16[192,16,256]{2,0,1:T(8,128)(2,1)S(1)}, u32[]{:S(2)}, u32[]{:S(2)}) %all-to-all-start.1) | async-done | bytes 1572896 | tf_op jit(solution)/shard_map/all_to_all | solution.py:105
  180.4 12.7 %all-to-all-start.4 = ((f32[512,1,16]{2,1,0:T(1,128)}), f32[512,1,16]{2,1,0:T(1,128)S(1)}, u32[]{:S(2)}, u32[]{:S(2)}) async-start(f32[512,1,16]{2,1,0:T(1,128)} %bitcast.21), calls=%async_computation.5 | async-start | bytes 524288 | tf_op jit(solution)/shard_map/all_to_all | solution.py:15
  194.4 15.1 %all-to-all-done.4 = f32[512,1,16]{2,1,0:T(1,128)S(1)} async-done(((f32[512,1,16]{2,1,0:T(1,128)}), f32[512,1,16]{2,1,0:T(1,128)S(1)}, u32[]{:S(2)}, u32[]{:S(2)}) %all-to-all-start.4) | async-done | bytes 32800 | tf_op jit(solution)/shard_map/all_to_all | solution.py:15
  209.5 4.4 %all-to-all-start.2 = ((f32[32,1,1024]{2,1,0:T(1,128)}), f32[32,1,1024]{2,1,0:T(1,128)S(1)}, u32[]{:S(2)}, u32[]{:S(2)}) async-start(f32[32,1,1024]{2,1,0:T(1,128)} %all_to_all.70), calls=%async_computation.3 | async-start | bytes 262144 | tf_op jit(solution)/shard_map/all_to_all | solution.py:15
  214.5 11.1 %all-to-all-done.2 = f32[32,1,1024]{2,1,0:T(1,128)S(1)} async-done(((f32[32,1,1024]{2,1,0:T(1,128)}), f32[32,1,1024]{2,1,0:T(1,128)S(1)}, u32[]{:S(2)}, u32[]{:S(2)}) %all-to-all-start.2) | async-done | bytes 131104 | tf_op jit(solution)/shard_map/all_to_all | solution.py:15
  226.4 9.8 %all-to-all-start.5 = ((f32[512,1,16]{2,1,0:T(1,128)}), f32[512,1,16]{2,1,0:T(1,128)S(1)}, u32[]{:S(2)}, u32[]{:S(2)}) async-start(f32[512,1,16]{2,1,0:T(1,128)} %broadcast_in_dim.10), calls=%async_computation.6 | async-start | bytes 524288 | tf_op jit(solution)/shard_map/all_to_all | solution.py:17
  236.3 17.2 %all-to-all-done.5 = f32[512,1,16]{2,1,0:T(1,128)S(1)} async-done(((f32[512,1,16]{2,1,0:T(1,128)}), f32[512,1,16]{2,1,0:T(1,128)S(1)}, u32[]{:S(2)}, u32[]{:S(2)}) %all-to-all-start.5) | async-done | bytes 32800 | tf_op jit(solution)/shard_map/all_to_all | solution.py:17
  254.2 3.9 %all-to-all-start.3 = ((f32[32,1,1024]{2,1,0:T(1,128)}), f32[32,1,1024]{2,1,0:T(1,128)S(1)}, u32[]{:S(2)}, u32[]{:S(2)}) async-start(f32[32,1,1024]{2,1,0:T(1,128)} %broadcast_in_dim.9), calls=%async_computation.4 | async-start | bytes 262144 | tf_op jit(solution)/shard_map/all_to_all | solution.py:17
  260.7 9.3 %all-to-all-done.3 = f32[32,1,1024]{2,1,0:T(1,128)S(1)} async-done(((f32[32,1,1024]{2,1,0:T(1,128)}), f32[32,1,1024]{2,1,0:T(1,128)S(1)}, u32[]{:S(2)}, u32[]{:S(2)}) %all-to-all-start.3) | async-done | bytes 131104 | tf_op jit(solution)/shard_map/all_to_all | solution.py:17
  271.9 13.4 %all_to_all.79 = bf16[16,4,8,128]{3,2,1,0:T(8,128)(2,1)S(1)} all-to-all(bf16[16,4,8,128]{3,2,1,0:T(8,128)(2,1)S(1)} %copy_bitcast_fusion.2), channel_id=1, replica_groups=mesh['group'=16,'row'=32] {'group'}, dimensions={0} | all-to-all | bytes 262144 | tf_op jit(solution)/shard_map/all_to_all | solution.py:23
  285.3 12.1 %all_to_all.80 = f32[16,4,8,128]{3,2,1,0:T(8,128)S(1)} all-to-all(f32[16,4,8,128]{3,2,1,0:T(8,128)S(1)} %broadcast_in_dim.11), channel_id=1, replica_groups=mesh['group'=16,'row'=32] {'group'}, dimensions={0} | all-to-all | bytes 524288 | tf_op jit(solution)/shard_map/all_to_all | solution.py:25
  (59 shorter events, 20.9 us)
Async XLA Ops:
  7.2 12.7 %copy-start = (bf16[128,256]{1,0:T(8,128)(2,1)S(1)}, bf16[128,256]{1,0:T(8,128)(2,1)}, u32[]{:S(2)}) copy-start(bf16[128,256]{1,0:T(8,128)(2,1)} %param.15) | copy-start | bytes 196612
  7.2 101.5 %all-gather.2.cloned.1.call-start = ((), (), s32[]{:S(2)}) async-start(), calls=%async_computation.9 | async-start | bytes 4325376 | tf_op jit(solution)/shard_map/all_gather | solution.py:57
  19.8 50.0 %copy-start.2 = (bf16[3072,128]{1,0:T(8,128)(2,1)}, bf16[3072,128]{1,0:T(8,128)(2,1)S(1)}, u32[]{:S(2)}) copy-start(bf16[3072,128]{1,0:T(8,128)(2,1)S(1)} %scatter_custom_fusion) | copy-start | bytes 2359300
  19.8 13.8 %copy-start.5 = (f32[4096]{0:T(1024)S(1)}, f32[4096]{0:T(1024)}, u32[]{:S(2)}) copy-start(f32[4096]{0:T(1024)} %param.20) | copy-start | bytes 49156
  19.8 13.8 %copy-start.6 = (f32[2,4096]{1,0:T(2,128)S(1)}, f32[2,4096]{1,0:T(2,128)}, u32[]{:S(2)}) copy-start(f32[2,4096]{1,0:T(2,128)} %param.19) | copy-start | bytes 98308
  21.6 48.2 %all-to-all-start = ((bf16[16,192,256]{2,1,0:T(8,128)(2,1)}), bf16[16,192,256]{2,1,0:T(8,128)(2,1)S(1)}, u32[]{:S(2)}, u32[]{:S(2)}) async-start(bf16[16,192,256]{2,1,0:T(8,128)(2,1)} %bitcast.105), calls=%async_computation | async-start | bytes 3145728 | tf_op jit(solution)/shard_map/all_to_all | solution.py:53
  33.4 237.6 %reduce-scatter.2.cloned.1.call-start = ((), (), s32[]{:S(2)}) async-start(), calls=%async_computation.10 | async-start | bytes 4325376 | tf_op jit(solution)/shard_map/reduce_scatter | solution.py:101
  110.4 3.7 %copy-start.4 = (bf16[4,4096,128]{2,1,0:T(8,128)(2,1)S(1)}, bf16[4,4096,128]{2,1,0:T(8,128)(2,1)}, u32[]{:S(2)}) copy-start(bf16[4,4096,128]{2,1,0:T(8,128)(2,1)} %all-gather.2.cloned.1.call-done) | copy-start | bytes 12582916
  114.7 2.7 copy-start.8
  117.4 1.6 copy-start.7
  127.4 1.9 copy-start.1
  133.3 59.8 %copy-start.3 = (bf16[3072,128]{1,0:T(8,128)(2,1)S(1)}, bf16[3072,128]{1,0:T(8,128)(2,1)}, u32[]{:S(2)}) copy-start(bf16[3072,128]{1,0:T(8,128)(2,1)} %copy-done.2) | copy-start | bytes 2359300
  134.7 45.8 %all-to-all-start.1 = ((bf16[192,16,256]{2,0,1:T(8,128)(2,1)}), bf16[192,16,256]{2,0,1:T(8,128)(2,1)S(1)}, u32[]{:S(2)}, u32[]{:S(2)}) async-start(bf16[192,16,256]{2,0,1:T(8,128)(2,1)} %bitcast.104), calls=%async_computation.2 | async-start | bytes 3145728 | tf_op jit(solution)/shard_map/all_to_all | solution.py:105
  180.4 29.0 %all-to-all-start.4 = ((f32[512,1,16]{2,1,0:T(1,128)}), f32[512,1,16]{2,1,0:T(1,128)S(1)}, u32[]{:S(2)}, u32[]{:S(2)}) async-start(f32[512,1,16]{2,1,0:T(1,128)} %bitcast.21), calls=%async_computation.5 | async-start | bytes 524288 | tf_op jit(solution)/shard_map/all_to_all | solution.py:15
  209.5 16.1 %all-to-all-start.2 = ((f32[32,1,1024]{2,1,0:T(1,128)}), f32[32,1,1024]{2,1,0:T(1,128)S(1)}, u32[]{:S(2)}, u32[]{:S(2)}) async-start(f32[32,1,1024]{2,1,0:T(1,128)} %all_to_all.70), calls=%async_computation.3 | async-start | bytes 262144 | tf_op jit(solution)/shard_map/all_to_all | solution.py:15
  226.4 27.1 %all-to-all-start.5 = ((f32[512,1,16]{2,1,0:T(1,128)}), f32[512,1,16]{2,1,0:T(1,128)S(1)}, u32[]{:S(2)}, u32[]{:S(2)}) async-start(f32[512,1,16]{2,1,0:T(1,128)} %broadcast_in_dim.10), calls=%async_computation.6 | async-start | bytes 524288 | tf_op jit(solution)/shard_map/all_to_all | solution.py:17
  254.2 15.8 %all-to-all-start.3 = ((f32[32,1,1024]{2,1,0:T(1,128)}), f32[32,1,1024]{2,1,0:T(1,128)S(1)}, u32[]{:S(2)}, u32[]{:S(2)}) async-start(f32[32,1,1024]{2,1,0:T(1,128)} %broadcast_in_dim.9), calls=%async_computation.4 | async-start | bytes 262144 | tf_op jit(solution)/shard_map/all_to_all | solution.py:17
Sparse Core Ops, SparseCore 0:
  12.0 96.6 all-gather.1
  127.5 137.2 reduce-scatter.1

commit v6 on v5

--- a/solution.py
+++ b/solution.py
@@ -24,6 +24,20 @@
     spread = jnp.broadcast_to(mine[None], pieces.shape)
     gathered = lax.all_to_all(spread, "group", 0, 0, tiled=True)
     return gathered.transpose(1, 0, 2, 3).reshape(rows.shape)
+
+
+def doubling_gather(shard, axis):
+    count = lax.axis_size(axis)
+    me = lax.axis_index(axis)
+    held = shard[:, None]
+    step = 1
+    while step < count:
+        pairs = [(i, i ^ step) for i in range(count)]
+        other = lax.ppermute(held, axis, pairs)
+        upper = (me // step) % 2
+        held = jnp.where(upper == 1, jnp.concatenate([other, held], axis=1), jnp.concatenate([held, other], axis=1))
+        step *= 2
+    return held.reshape(shard.shape[0], count * shard.shape[1], *shard.shape[2:])
 
 
 def body(
@@ -54,9 +68,7 @@
     first_wide = first.astype(jnp.float32)
     crossed = first
     stored = []
-    weights_full = lax.all_gather(
-        jnp.concatenate([down_weight, up_weight], axis=0), "row", axis=1, tiled=True
-    )
+    weights_full = doubling_gather(jnp.concatenate([down_weight, up_weight], axis=0), "row")
     for layer_index in range(layers):
         down_full, up_full = weights_full[layer_index], weights_full[layers + layer_index]
         hidden = jnp.dot(crossed, down_full, preferred_element_type=jnp.float32).astype(

time: 306 us -> 358 us (1.17)
  waiting for transfers between devices: 164 us -> 189 us
  starting transfers between devices: 51.7 us -> 74 us
  other arithmetic: 16.4 us -> 22.3 us
    ppermute x0 -> x5, waiting for transfers between devices: none -> 94.9 us  [doubling_gather(): other = lax.ppermute(held, axis, pairs)]
    all_gather x1 -> x0, waiting for transfers between devices: 38.7 us -> none  [body(): lax.all_gather(jnp.concatenate([down_weight, up_weight], axis=0), 'row',...]
    all_to_all x1, waiting for transfers between devices: 36.1 us -> 5.56 us  [body(): lax.all_to_all(projected, 'group', split_axis=0, concat_axis=1, tiled=True)]
    ppermute x0 -> x5, starting transfers between devices: none -> 21.8 us  [doubling_gather(): other = lax.ppermute(held, axis, pairs)]
    select_n x0 -> x5, other arithmetic: none -> 7.3 us  [doubling_gather(): jnp.where(upper == 1, jnp.concatenate([other, held], axis=1), jnp.concate...]
  transfers between devices with their start and end apart: 8 -> 12, of which waited for: 7 -> 11; matrix products, arithmetic and copies ran while one was open for 8% -> 8% of each run, Pallas kernels for 0% -> 0%
where the time goes in v6:
time: 358 us; the launch traced here: 357 us
  waiting for transfers between devices  189 us (53%)
  starting transfers between devices  74 us (21%)
  blocking collectives  25.3 us (7%)
  other arithmetic  22.3 us (6%)
  matrix products  20.6 us (6%)
  between operations  14.5 us (4%)
  local copies, waits for them, and re-layouts  11 us (3%)
    ppermute x5, waiting for transfers between devices, doubling_gather(): other = lax.ppermute(held, axis, pairs)  94.9 us
    all_to_all x1, waiting for transfers between devices, body(): lax.all_to_all(first_grad, 'group', split_axis=1, concat_axis=0, tiled=True)  34.7 us
    all_to_all x2, waiting for transfers between devices, exchange_sum(): mine = jnp.sum(lax.all_to_all(pieces, axis, 0, 0, tiled=True), axis=0)  27.3 us
    all_to_all x2, waiting for transfers between devices, exchange_sum(): return lax.all_to_all(spread, axis, 0, 0, tiled=True).reshape(partial.shape)  26.4 us
    ppermute x5, starting transfers between devices, doubling_gather(): other = lax.ppermute(held, axis, pairs)  21.8 us
    all_to_all x2, starting transfers between devices, exchange_sum(): mine = jnp.sum(lax.all_to_all(pieces, axis, 0, 0, tiled=True), axis=0)  16.7 us
    all_to_all x2, starting transfers between devices, exchange_sum(): return lax.all_to_all(spread, axis, 0, 0, tiled=True).reshape(partial.shape)  13.3 us
    all_to_all x1, blocking collectives, group_all_reduce(): lax.all_to_all(pieces, 'group', 0, 0, tiled=True).astype(jnp.float32)  13 us
  transfers between devices with their start and end apart: 12, of which 11 were waited for; matrix products, arithmetic and copies ran while one was open for 8% of the time, Pallas kernels for 0%

profile of v6, /device:TPU:2, one launch (start us, length us, event | category | flops | bytes accessed | tf_op | source)
XLA Modules:
  0.0 356.7 jit_solution(10238520796879344072)
XLA Ops:
  16.3 5.3 %collective-permute-done.1 = bf16[4,2,128,128]{3,2,0,1:T(8,128)(2,1)S(1)} collective-permute-done((bf16[4,2,128,128]{3,2,0,1:T(8,128)(2,1)S(1)}, bf16[4,2,128,128]{3,2,0,1:T(8,128)(2,1)S(1)}, u32[]{:S(2)}, u32[]{:S(2)}) %collective-permute-start.1) | collective-permute-done | bytes 262176 | tf_op jit(solution)/shard_map/ppermute | solution.py:36
  21.7 4.5 %collective-permute-start.2 = (bf16[4,4,128,128]{3,2,0,1:T(8,128)(2,1)S(1)}, bf16[4,4,128,128]{3,2,0,1:T(8,128)(2,1)S(1)}, u32[]{:S(2)}, u32[]{:S(2)}) collective-permute-start(bf16[4,4,128,128]{3,2,0,1:T(8,128)(2,1)S(1)} %maximum_select_fusion.3), channel_id=1, source_target_pairs={{0,4},{1,5},{2,6},{3,7},{4,0},{5,1},{6,2},{7,3},{8,12},{9,13},{10,... | collective-permute-start | bytes 1572872 | tf_op jit(solution)/shard_map/ppermute | solution.py:36
  26.3 22.6 %collective-permute-done.2 = bf16[4,4,128,128]{3,2,0,1:T(8,128)(2,1)S(1)} collective-permute-done((bf16[4,4,128,128]{3,2,0,1:T(8,128)(2,1)S(1)}, bf16[4,4,128,128]{3,2,0,1:T(8,128)(2,1)S(1)}, u32[]{:S(2)}, u32[]{:S(2)}) %collective-permute-start.2) | collective-permute-done | bytes 524320 | tf_op jit(solution)/shard_map/ppermute | solution.py:36
  49.1 7.7 %collective-permute-start.3 = (bf16[4,8,128,128]{3,2,0,1:T(8,128)(2,1)S(1)}, bf16[4,8,128,128]{3,2,0,1:T(8,128)(2,1)}, u32[]{:S(2)}, u32[]{:S(2)}) collective-permute-start(bf16[4,8,128,128]{3,2,0,1:T(8,128)(2,1)S(1)} %maximum_select_fusion.2), channel_id=1, source_target_pairs={{0,8},{1,9},{2,10},{3,11},{4,12},{5,13},{6,14},{7,15},{8,0},{9,1},... | collective-permute-start | bytes 3145736 | tf_op jit(solution)/shard_map/ppermute | solution.py:36
  56.8 8.9 %scatter_custom_fusion = bf16[3072,128]{1,0:T(8,128)(2,1)S(1)} fusion(s32[3072]{0:T(1024)S(1)} %bitcast.113, f32[3072,128]{1,0:T(8,128)} %param.11, f32[128]{0:T(128)S(1)} %get-tuple-element.24, f32[128]{0:T(128)S(1)} %get-tuple-element.23, bf16[]{:T(256)} %constant.81.clone.1), kind=kCustom, calls=%fused_computation.52 | custom fusion | flops 1179648 | bytes 2360322 | tf_op jit(solution)/shard_map/scatter | solution.py:63
  67.5 11.8 %all-to-all-start = ((bf16[16,192,256]{2,1,0:T(8,128)(2,1)}), bf16[16,192,256]{2,1,0:T(8,128)(2,1)S(1)}, u32[]{:S(2)}, u32[]{:S(2)}) async-start(bf16[16,192,256]{2,1,0:T(8,128)(2,1)} %bitcast.6), calls=%async_computation | async-start | bytes 3145728 | tf_op jit(solution)/shard_map/all_to_all | solution.py:67
  79.4 23.7 %collective-permute-done.3 = bf16[4,8,128,128]{3,2,0,1:T(8,128)(2,1)} collective-permute-done((bf16[4,8,128,128]{3,2,0,1:T(8,128)(2,1)S(1)}, bf16[4,8,128,128]{3,2,0,1:T(8,128)(2,1)}, u32[]{:S(2)}, u32[]{:S(2)}) %collective-permute-start.3) | collective-permute-done | bytes 1048608 | tf_op jit(solution)/shard_map/ppermute | solution.py:36
  106.3 4.2 %collective-permute-start.4 = (bf16[4,16,128,128]{3,2,0,1:T(8,128)(2,1)}, bf16[4,16,128,128]{3,2,0,1:T(8,128)(2,1)}, u32[]{:S(2)}, u32[]{:S(2)}) collective-permute-start(bf16[4,16,128,128]{3,2,0,1:T(8,128)(2,1)} %maximum_select_fusion.1), channel_id=1, source_target_pairs={{0,16},{1,17},{2,18},{3,19},{4,20},{5,21},{6,22},{7,23},{8,24},{9,... | collective-permute-start | bytes 6291464 | tf_op jit(solution)/shard_map/ppermute | solution.py:36
  110.6 5.6 %all-to-all-done = bf16[16,192,256]{2,1,0:T(8,128)(2,1)S(1)} async-done(((bf16[16,192,256]{2,1,0:T(8,128)(2,1)}), bf16[16,192,256]{2,1,0:T(8,128)(2,1)S(1)}, u32[]{:S(2)}, u32[]{:S(2)}) %all-to-all-start) | async-done | bytes 1572896 | tf_op jit(solution)/shard_map/all_to_all | solution.py:67
  116.3 42.0 %collective-permute-done.4 = bf16[4,16,128,128]{3,2,0,1:T(8,128)(2,1)} collective-permute-done((bf16[4,16,128,128]{3,2,0,1:T(8,128)(2,1)}, bf16[4,16,128,128]{3,2,0,1:T(8,128)(2,1)}, u32[]{:S(2)}, u32[]{:S(2)}) %collective-permute-start.4) | collective-permute-done | bytes 2097184 | tf_op jit(solution)/shard_map/ppermute | solution.py:36
  158.3 3.8 %maximum_select_fusion = bf16[4,32,128,128]{3,2,0,1:T(8,128)(2,1)S(1)} fusion(bf16[4,16,128,128]{3,2,0,1:T(8,128)(2,1)} %maximum_select_fusion.1, bf16[4,16,128,128]{3,2,0,1:T(8,128)(2,1)} %collective-permute-done.4, pred[]{:T(512)S(6)} %eq.37), kind=kLoop, calls=%fused_computation.25 | loop fusion | flops 6291456 | bytes 8388609 | tf_op jit(solution)/shard_map/jit(_where)/select_n | solution.py:38
  180.8 4.0 %fusion.5 = bf16[192,4096]{1,0:T(8,128)(2,1)S(1)} fusion(f32[192,4096]{1,0:T(8,128)} %get-tuple-element.29, bf16[192,128]{1,0:T(8,128)(2,1)S(1)} %convolution_convert_fusion.5, bf16[4096,128]{1,0:T(8,128)(2,1)} %bitcast.96, f32[192,4096]{1,0:T(8,128)} %get-tuple-element.28, f32[192,4096]{1,0:T(8,128)S(1)} %copy-done.1, f32[192]{0:T(256)S(1)} %fusion.29, ...), kind=kOutput, calls=%fused_computation.15 | convolution fusion | flops 209977344 | bytes 12124928 | tf_op jit(solution)/shard_map/dot_general | solution.py:107
  186.1 10.3 %all-to-all-start.1 = ((bf16[192,16,256]{2,0,1:T(8,128)(2,1)}), bf16[192,16,256]{2,0,1:T(8,128)(2,1)S(1)}, u32[]{:S(2)}, u32[]{:S(2)}) async-start(bf16[192,16,256]{2,0,1:T(8,128)(2,1)} %bitcast.104), calls=%async_computation.2 | async-start | bytes 3145728 | tf_op jit(solution)/shard_map/all_to_all | solution.py:117
  197.4 34.7 %all-to-all-done.1 = bf16[192,16,256]{2,0,1:T(8,128)(2,1)S(1)} async-done(((bf16[192,16,256]{2,0,1:T(8,128)(2,1)}), bf16[192,16,256]{2,0,1:T(8,128)(2,1)S(1)}, u32[]{:S(2)}, u32[]{:S(2)}) %all-to-all-start.1) | async-done | bytes 1572896 | tf_op jit(solution)/shard_map/all_to_all | solution.py:117
  232.1 12.6 %all-to-all-start.4 = ((f32[512,1,16]{2,1,0:T(1,128)}), f32[512,1,16]{2,1,0:T(1,128)S(1)}, u32[]{:S(2)}, u32[]{:S(2)}) async-start(f32[512,1,16]{2,1,0:T(1,128)} %bitcast.22), calls=%async_computation.5 | async-start | bytes 524288 | tf_op jit(solution)/shard_map/all_to_all | solution.py:15
  245.9 15.2 %all-to-all-done.4 = f32[512,1,16]{2,1,0:T(1,128)S(1)} async-done(((f32[512,1,16]{2,1,0:T(1,128)}), f32[512,1,16]{2,1,0:T(1,128)S(1)}, u32[]{:S(2)}, u32[]{:S(2)}) %all-to-all-start.4) | async-done | bytes 32800 | tf_op jit(solution)/shard_map/all_to_all | solution.py:15
  261.1 4.2 %all-to-all-start.2 = ((f32[32,1,1024]{2,1,0:T(1,128)}), f32[32,1,1024]{2,1,0:T(1,128)S(1)}, u32[]{:S(2)}, u32[]{:S(2)}) async-start(f32[32,1,1024]{2,1,0:T(1,128)} %all_to_all.70), calls=%async_computation.3 | async-start | bytes 262144 | tf_op jit(solution)/shard_map/all_to_all | solution.py:15
  265.8 12.1 %all-to-all-done.2 = f32[32,1,1024]{2,1,0:T(1,128)S(1)} async-done(((f32[32,1,1024]{2,1,0:T(1,128)}), f32[32,1,1024]{2,1,0:T(1,128)S(1)}, u32[]{:S(2)}, u32[]{:S(2)}) %all-to-all-start.2) | async-done | bytes 131104 | tf_op jit(solution)/shard_map/all_to_all | solution.py:15
  278.8 9.1 %all-to-all-start.5 = ((f32[512,1,16]{2,1,0:T(1,128)}), f32[512,1,16]{2,1,0:T(1,128)S(1)}, u32[]{:S(2)}, u32[]{:S(2)}) async-start(f32[512,1,16]{2,1,0:T(1,128)} %broadcast_in_dim.13), calls=%async_computation.6 | async-start | bytes 524288 | tf_op jit(solution)/shard_map/all_to_all | solution.py:17
  288.0 16.7 %all-to-all-done.5 = f32[512,1,16]{2,1,0:T(1,128)S(1)} async-done(((f32[512,1,16]{2,1,0:T(1,128)}), f32[512,1,16]{2,1,0:T(1,128)S(1)}, u32[]{:S(2)}, u32[]{:S(2)}) %all-to-all-start.5) | async-done | bytes 32800 | tf_op jit(solution)/shard_map/all_to_all | solution.py:17
  305.4 4.1 %all-to-all-start.3 = ((f32[32,1,1024]{2,1,0:T(1,128)}), f32[32,1,1024]{2,1,0:T(1,128)S(1)}, u32[]{:S(2)}, u32[]{:S(2)}) async-start(f32[32,1,1024]{2,1,0:T(1,128)} %broadcast_in_dim.12), calls=%async_computation.4 | async-start | bytes 262144 | tf_op jit(solution)/shard_map/all_to_all | solution.py:17
  312.2 9.7 %all-to-all-done.3 = f32[32,1,1024]{2,1,0:T(1,128)S(1)} async-done(((f32[32,1,1024]{2,1,0:T(1,128)}), f32[32,1,1024]{2,1,0:T(1,128)S(1)}, u32[]{:S(2)}, u32[]{:S(2)}) %all-to-all-start.3) | async-done | bytes 131104 | tf_op jit(solution)/shard_map/all_to_all | solution.py:17
  323.8 13.0 %all_to_all.79 = bf16[16,4,8,128]{3,2,1,0:T(8,128)(2,1)S(1)} all-to-all(bf16[16,4,8,128]{3,2,1,0:T(8,128)(2,1)S(1)} %copy_bitcast_fusion.2), channel_id=1, replica_groups=mesh['group'=16,'row'=32] {'group'}, dimensions={0} | all-to-all | bytes 262144 | tf_op jit(solution)/shard_map/all_to_all | solution.py:23
  336.9 12.2 %all_to_all.80 = f32[16,4,8,128]{3,2,1,0:T(8,128)S(1)} all-to-all(f32[16,4,8,128]{3,2,1,0:T(8,128)S(1)} %broadcast_in_dim.14), channel_id=1, replica_groups=mesh['group'=16,'row'=32] {'group'}, dimensions={0} | all-to-all | bytes 524288 | tf_op jit(solution)/shard_map/all_to_all | solution.py:25
  (74 shorter events, 44.0 us)
Async XLA Ops:
  7.2 58.6 %copy-start = (bf16[128,256]{1,0:T(8,128)(2,1)S(1)}, bf16[128,256]{1,0:T(8,128)(2,1)}, u32[]{:S(2)}) copy-start(bf16[128,256]{1,0:T(8,128)(2,1)} %param.15) | copy-start | bytes 196612
  7.2 19.1 %copy-start.7 = (s32[1,3072]{1,0:T(1,128)S(1)}, s32[1,3072]{1,0:T(1,128)}, u32[]{:S(2)}) copy-start(s32[1,3072]{1,0:T(1,128)} %param.16) | copy-start | bytes 36868
  8.1 3.2 collective-permute-start
  11.4 10.3 %collective-permute-start.1 = (bf16[4,2,128,128]{3,2,0,1:T(8,128)(2,1)S(1)}, bf16[4,2,128,128]{3,2,0,1:T(8,128)(2,1)S(1)}, u32[]{:S(2)}, u32[]{:S(2)}) collective-permute-start(bf16[4,2,128,128]{3,2,0,1:T(8,128)(2,1)S(1)} %maximum_select_fusion.4), channel_id=1, source_target_pairs={{0,2},{1,3},{2,0},{3,1},{4,6},{5,7},{6,4},{7,5},{8,10},{9,11},{10,... | collective-permute-start | bytes 786440 | tf_op jit(solution)/shard_map/ppermute | solution.py:36
  21.7 27.2 %collective-permute-start.2 = (bf16[4,4,128,128]{3,2,0,1:T(8,128)(2,1)S(1)}, bf16[4,4,128,128]{3,2,0,1:T(8,128)(2,1)S(1)}, u32[]{:S(2)}, u32[]{:S(2)}) collective-permute-start(bf16[4,4,128,128]{3,2,0,1:T(8,128)(2,1)S(1)} %maximum_select_fusion.3), channel_id=1, source_target_pairs={{0,4},{1,5},{2,6},{3,7},{4,0},{5,1},{6,2},{7,3},{8,12},{9,13},{10,... | collective-permute-start | bytes 1572872 | tf_op jit(solution)/shard_map/ppermute | solution.py:36
  49.1 54.0 %collective-permute-start.3 = (bf16[4,8,128,128]{3,2,0,1:T(8,128)(2,1)S(1)}, bf16[4,8,128,128]{3,2,0,1:T(8,128)(2,1)}, u32[]{:S(2)}, u32[]{:S(2)}) collective-permute-start(bf16[4,8,128,128]{3,2,0,1:T(8,128)(2,1)S(1)} %maximum_select_fusion.2), channel_id=1, source_target_pairs={{0,8},{1,9},{2,10},{3,11},{4,12},{5,13},{6,14},{7,15},{8,0},{9,1},... | collective-permute-start | bytes 3145736 | tf_op jit(solution)/shard_map/ppermute | solution.py:36
  65.7 1.8 copy-start.3
  67.5 48.6 %all-to-all-start = ((bf16[16,192,256]{2,1,0:T(8,128)(2,1)}), bf16[16,192,256]{2,1,0:T(8,128)(2,1)S(1)}, u32[]{:S(2)}, u32[]{:S(2)}) async-start(bf16[16,192,256]{2,1,0:T(8,128)(2,1)} %bitcast.6), calls=%async_computation | async-start | bytes 3145728 | tf_op jit(solution)/shard_map/all_to_all | solution.py:67
  79.3 243.6 %reduce-scatter.2.cloned.1.call-start = ((), (), s32[]{:S(2)}) async-start(), calls=%async_computation.9 | async-start | bytes 4325376 | tf_op jit(solution)/shard_map/reduce_scatter | solution.py:113
  79.4 31.1 %copy-start.5 = (f32[4096]{0:T(1024)S(1)}, f32[4096]{0:T(1024)}, u32[]{:S(2)}) copy-start(f32[4096]{0:T(1024)} %param.20) | copy-start | bytes 49156
  79.4 31.2 %copy-start.6 = (f32[2,4096]{1,0:T(2,128)S(1)}, f32[2,4096]{1,0:T(2,128)}, u32[]{:S(2)}) copy-start(f32[2,4096]{1,0:T(2,128)} %param.19) | copy-start | bytes 98308
  106.3 52.0 %collective-permute-start.4 = (bf16[4,16,128,128]{3,2,0,1:T(8,128)(2,1)}, bf16[4,16,128,128]{3,2,0,1:T(8,128)(2,1)}, u32[]{:S(2)}, u32[]{:S(2)}) collective-permute-start(bf16[4,16,128,128]{3,2,0,1:T(8,128)(2,1)} %maximum_select_fusion.1), channel_id=1, source_target_pairs={{0,16},{1,17},{2,18},{3,19},{4,20},{5,21},{6,22},{7,23},{8,24},{9,... | collective-permute-start | bytes 6291464 | tf_op jit(solution)/shard_map/ppermute | solution.py:36
  162.7 3.0 copy-start.2
  166.3 2.7 copy-start.9
  168.9 0.9 copy-start.8
  178.9 1.9 copy-start.1
  186.1 58.5 %copy-start.4 = (bf16[3072,128]{1,0:T(8,128)(2,1)S(1)}, bf16[3072,128]{1,0:T(8,128)(2,1)}, u32[]{:S(2)}) copy-start(bf16[3072,128]{1,0:T(8,128)(2,1)} %copy-done.3) | copy-start | bytes 2359300
  186.1 45.9 %all-to-all-start.1 = ((bf16[192,16,256]{2,0,1:T(8,128)(2,1)}), bf16[192,16,256]{2,0,1:T(8,128)(2,1)S(1)}, u32[]{:S(2)}, u32[]{:S(2)}) async-start(bf16[192,16,256]{2,0,1:T(8,128)(2,1)} %bitcast.104), calls=%async_computation.2 | async-start | bytes 3145728 | tf_op jit(solution)/shard_map/all_to_all | solution.py:117
  232.1 29.0 %all-to-all-start.4 = ((f32[512,1,16]{2,1,0:T(1,128)}), f32[512,1,16]{2,1,0:T(1,128)S(1)}, u32[]{:S(2)}, u32[]{:S(2)}) async-start(f32[512,1,16]{2,1,0:T(1,128)} %bitcast.22), calls=%async_computation.5 | async-start | bytes 524288 | tf_op jit(solution)/shard_map/all_to_all | solution.py:15
  261.1 16.8 %all-to-all-start.2 = ((f32[32,1,1024]{2,1,0:T(1,128)}), f32[32,1,1024]{2,1,0:T(1,128)S(1)}, u32[]{:S(2)}, u32[]{:S(2)}) async-start(f32[32,1,1024]{2,1,0:T(1,128)} %all_to_all.70), calls=%async_computation.3 | async-start | bytes 262144 | tf_op jit(solution)/shard_map/all_to_all | solution.py:15
  278.8 25.9 %all-to-all-start.5 = ((f32[512,1,16]{2,1,0:T(1,128)}), f32[512,1,16]{2,1,0:T(1,128)S(1)}, u32[]{:S(2)}, u32[]{:S(2)}) async-start(f32[512,1,16]{2,1,0:T(1,128)} %broadcast_in_dim.13), calls=%async_computation.6 | async-start | bytes 524288 | tf_op jit(solution)/shard_map/all_to_all | solution.py:17
  305.4 16.4 %all-to-all-start.3 = ((f32[32,1,1024]{2,1,0:T(1,128)}), f32[32,1,1024]{2,1,0:T(1,128)S(1)}, u32[]{:S(2)}, u32[]{:S(2)}) async-start(f32[32,1,1024]{2,1,0:T(1,128)} %broadcast_in_dim.12), calls=%async_computation.4 | async-start | bytes 262144 | tf_op jit(solution)/shard_map/all_to_all | solution.py:17
Sparse Core Ops, SparseCore 0:
  179.0 138.9 reduce-scatter.1

commit v7 on v5

--- a/solution.py
+++ b/solution.py
@@ -106,9 +106,28 @@
     proj_term = lax.dot_general(
         ordered, owner_grad, (((0,), (0,)), ((), ())), preferred_element_type=jnp.float32
     )
-    grad_proj = exchange_sum(proj_term, "row", lax.axis_size("row"))
+    row_count_axis = lax.axis_size("row")
     bias_all = jnp.stack(bias_terms)
-    grad_bias = exchange_sum(bias_all, ("group", "row"), groups * lax.axis_size("row"))
+    proj_pieces = proj_term.reshape(row_count_axis, -1)
+    bias_pieces = bias_all.reshape(layers, row_count_axis, -1).transpose(1, 0, 2)
+    bias_pieces = bias_pieces.reshape(row_count_axis, -1)
+    split = proj_pieces.shape[1]
+    row_mine = jnp.sum(
+        lax.all_to_all(jnp.concatenate([proj_pieces, bias_pieces], axis=1), "row", 0, 0, tiled=True),
+        axis=0,
+    )
+    bias_chunk = exchange_sum(row_mine[split:], "group", groups)
+    last = jnp.concatenate([row_mine[:split], bias_chunk])
+    last_all = lax.all_to_all(
+        jnp.broadcast_to(last[None], (row_count_axis,) + last.shape), "row", 0, 0, tiled=True
+    )
+    grad_proj = last_all[:, :split].reshape(proj_term.shape)
+    grad_bias = (
+        last_all[:, split:]
+        .reshape(row_count_axis, layers, -1)
+        .transpose(1, 0, 2)
+        .reshape(bias_all.shape)
+    )
     weight_rows, grad_proj, grad_bias = lax.optimization_barrier((weight_rows, grad_proj, grad_bias))
     weight_sums = group_all_reduce(weight_rows, groups)
     grad_up, grad_down = weight_sums[:layers], weight_sums[layers:]

time: 306 us -> 300 us (0.980)
  blocking collectives: 25.4 us -> 75.9 us
  waiting for transfers between devices: 164 us -> 137 us
  starting transfers between devices: 51.7 us -> 25.6 us
    all_to_all x0 -> x3, blocking collectives: none -> 47.7 us  [the longest x1 18.4 us: body(): lax.all_to_all(jnp.concatenate([proj_pieces, bias_pieces], axis=1), 'row'...]
    all_to_all x2 -> x0, waiting for transfers between devices: 26.2 us -> none  [exchange_sum(): mine = jnp.sum(lax.all_to_all(pieces, axis, 0, 0, tiled=True), axis=0)]
    all_to_all x2 -> x1, waiting for transfers between devices: 26.5 us -> 7.05 us  [exchange_sum(): return lax.all_to_all(spread, axis, 0, 0, tiled=True).reshape(partial.shape)]
    reduce_scatter x1, waiting for transfers between devices: 0.01 us -> 18.4 us  [body(): lax.psum_scatter(jnp.stack(up_parts + down_parts).astype(jnp.bfloat16), '...]
    all_to_all x2 -> x0, starting transfers between devices: 17.1 us -> none  [exchange_sum(): mine = jnp.sum(lax.all_to_all(pieces, axis, 0, 0, tiled=True), axis=0)]
    all_to_all x2 -> x1, starting transfers between devices: 13.7 us -> 4.75 us  [exchange_sum(): return lax.all_to_all(spread, axis, 0, 0, tiled=True).reshape(partial.shape)]
  transfers between devices with their start and end apart: 8 -> 5, of which waited for: 7 -> 5; matrix products, arithmetic and copies ran while one was open for 8% -> 7% of each run, Pallas kernels for 0% -> 0%
where the time goes in v7:
time: 300 us; the launch traced here: 299 us
  waiting for transfers between devices  137 us (46%)
  blocking collectives  75.9 us (25%)
  starting transfers between devices  25.6 us (9%)
  matrix products  23.1 us (8%)
  other arithmetic  15 us (5%)
  between operations  14.4 us (5%)
  local copies, waits for them, and re-layouts  8.21 us (3%)
    all_gather x1, waiting for transfers between devices, body(): lax.all_gather(jnp.concatenate([down_weight, up_weight], axis=0), 'row',...  38.6 us
    all_to_all x1, waiting for transfers between devices, body(): lax.all_to_all(first_grad, 'group', split_axis=1, concat_axis=0, tiled=True)  36.9 us
    all_to_all x1, waiting for transfers between devices, body(): lax.all_to_all(projected, 'group', split_axis=0, concat_axis=1, tiled=True)  36.1 us
    all_to_all x1, blocking collectives, body(): lax.all_to_all(jnp.concatenate([proj_pieces, bias_pieces], axis=1), 'row'...  18.4 us
    reduce_scatter x1, waiting for transfers between devices, body(): lax.psum_scatter(jnp.stack(up_parts + down_parts).astype(jnp.bfloat16), '...  18.4 us
    all_to_all x1, blocking collectives, group_all_reduce(): lax.all_to_all(pieces, 'group', 0, 0, tiled=True).astype(jnp.float32)  16.1 us
    all_to_all x1, blocking collectives, body(): lax.all_to_all(jnp.broadcast_to(last[None], (row_count_axis,) + last.shap...  15.6 us
    all_to_all x1, blocking collectives, exchange_sum(): mine = jnp.sum(lax.all_to_all(pieces, axis, 0, 0, tiled=True), axis=0)  13.7 us
  transfers between devices with their start and end apart: 5, of which 5 were waited for; matrix products, arithmetic and copies ran while one was open for 7% of the time, Pallas kernels for 0%

profile of v7, /device:TPU:2, one launch (start us, length us, event | category | flops | bytes accessed | tf_op | source)
XLA Modules:
  0.0 299.3 jit_solution(15426145314764393287)
XLA Ops:
  7.2 1.5 pad_maximum_fusion.2
  8.8 1.4 fusion.19
  10.9 8.9 %scatter_custom_fusion = bf16[3072,128]{1,0:T(8,128)(2,1)S(1)} fusion(s32[3072]{0:T(1024)S(1)} %bitcast.126, f32[3072,128]{1,0:T(8,128)} %param.11, f32[128]{0:T(128)S(1)} %get-tuple-element.20, f32[128]{0:T(128)S(1)} %get-tuple-element.19, bf16[]{:T(256)} %constant.0.clone.1), kind=kCustom, calls=%fused_computation.53 | custom fusion | flops 1179648 | bytes 2360322 | tf_op jit(solution)/shard_map/scatter | solution.py:49
  19.9 1.8 convolution_convert_fusion.4
  21.6 11.8 %all-to-all-start = ((bf16[16,192,256]{2,1,0:T(8,128)(2,1)}), bf16[16,192,256]{2,1,0:T(8,128)(2,1)S(1)}, u32[]{:S(2)}, u32[]{:S(2)}) async-start(bf16[16,192,256]{2,1,0:T(8,128)(2,1)} %bitcast.113), calls=%async_computation | async-start | bytes 3145728 | tf_op jit(solution)/shard_map/all_to_all | solution.py:53
  33.7 36.1 %all-to-all-done = bf16[16,192,256]{2,1,0:T(8,128)(2,1)S(1)} async-done(((bf16[16,192,256]{2,1,0:T(8,128)(2,1)}), bf16[16,192,256]{2,1,0:T(8,128)(2,1)S(1)}, u32[]{:S(2)}, u32[]{:S(2)}) %all-to-all-start) | async-done | bytes 1572896 | tf_op jit(solution)/shard_map/all_to_all | solution.py:53
  70.0 38.6 %all-gather.2.cloned.1.call-done = bf16[4,4096,128]{2,1,0:T(8,128)(2,1)} async-done(((bf16[4,128,128]{2,1,0:T(8,128)(2,1)}), bf16[4,4096,128]{2,1,0:T(8,128)(2,1)}) %all-gather.2.cloned.1.call-update) | async-done | bytes 4194320 | tf_op jit(solution)/shard_map/all_gather | solution.py:57
  108.6 1.8 convolution_convert_fusion.8
  110.4 3.7 %fusion.11 = (bf16[192,4096]{1,0:T(8,128)(2,1)S(1)}, f32[192,4096]{1,0:T(8,128)}) fusion(bf16[192,4096]{1,0:T(8,128)(2,1)S(1)} %bitcast.105, f32[4096]{0:T(1024)S(1)} %bitcast.123, bf16[192,128]{1,0:T(8,128)(2,1)S(1)} %convolution_convert_fusion.8, bf16[4,4096,128]{2,1,0:T(8,128)(2,1)} %all-gather.2.cloned.1.call-done), kind=kOutput, calls=%fused_computation.28 | convolution fusion | flops 205258752 | bytes 7405568 | tf_op jit(solution)/shard_map/dot_general | solution.py:65
  114.7 2.7 multiply_reduce_fusion
  120.5 2.5 convert_reduce_fusion.1
  125.2 2.3 pad_maximum_fusion
  127.5 1.9 copy-done.1
  129.3 4.0 %fusion.5 = bf16[192,4096]{1,0:T(8,128)(2,1)S(1)} fusion(f32[192,4096]{1,0:T(8,128)} %get-tuple-element.25, bf16[192,128]{1,0:T(8,128)(2,1)S(1)} %convolution_convert_fusion.5, f32[192,4096]{1,0:T(8,128)} %get-tuple-element.24, f32[192,4096]{1,0:T(8,128)S(1)} %copy-done.1, f32[192]{0:T(256)S(1)} %fusion.29, f32[4096]{0:T(1024)S(1)} %copy-done.5, ...), kind=kOutput, calls=%fused_computation.15 | convolution fusion | flops 209977344 | bytes 12124928 | tf_op jit(solution)/shard_map/dot_general | solution.py:95
  134.7 8.9 %all-to-all-start.1 = ((bf16[192,16,256]{2,0,1:T(8,128)(2,1)}), bf16[192,16,256]{2,0,1:T(8,128)(2,1)S(1)}, u32[]{:S(2)}, u32[]{:S(2)}) async-start(bf16[192,16,256]{2,0,1:T(8,128)(2,1)} %bitcast.112), calls=%async_computation.2 | async-start | bytes 3145728 | tf_op jit(solution)/shard_map/all_to_all | solution.py:105
  143.6 36.9 %all-to-all-done.1 = bf16[192,16,256]{2,0,1:T(8,128)(2,1)S(1)} async-done(((bf16[192,16,256]{2,0,1:T(8,128)(2,1)}), bf16[192,16,256]{2,0,1:T(8,128)(2,1)S(1)}, u32[]{:S(2)}, u32[]{:S(2)}) %all-to-all-start.1) | async-done | bytes 1572896 | tf_op jit(solution)/shard_map/all_to_all | solution.py:105
  181.1 18.4 %all_to_all.81 = f32[32,1,1280]{2,1,0:T(1,128)S(1)} all-to-all(f32[32,1,1280]{2,1,0:T(1,128)S(1)} %all_to_all.64), channel_id=1, replica_groups=mesh['group'=16,'row'=32] {'row'}, dimensions={0} | all-to-all | bytes 327680 | tf_op jit(solution)/shard_map/all_to_all | solution.py:116
  199.8 13.7 %all_to_all.82 = f32[16,1,16]{2,1,0:T(1,128)S(1)} all-to-all(f32[16,1,16]{2,1,0:T(1,128)S(1)} %all_to_all.66), channel_id=1, replica_groups=mesh['group'=16,'row'=32] {'group'}, dimensions={0} | all-to-all | bytes 2048 | tf_op jit(solution)/shard_map/all_to_all | solution.py:15
  214.1 4.7 %all-to-all-start.4 = ((f32[16,1,16]{2,1,0:T(1,128)}), f32[16,1,16]{2,1,0:T(1,128)S(1)}, u32[]{:S(2)}, u32[]{:S(2)}) async-start(f32[16,1,16]{2,1,0:T(1,128)} %broadcast_in_dim.9), calls=%async_computation.5 | async-start | bytes 16384 | tf_op jit(solution)/shard_map/all_to_all | solution.py:17
  218.9 7.1 %all-to-all-done.4 = f32[16,1,16]{2,1,0:T(1,128)S(1)} async-done(((f32[16,1,16]{2,1,0:T(1,128)}), f32[16,1,16]{2,1,0:T(1,128)S(1)}, u32[]{:S(2)}, u32[]{:S(2)}) %all-to-all-start.4) | async-done | bytes 1056 | tf_op jit(solution)/shard_map/all_to_all | solution.py:17
  227.3 15.6 %all_to_all.83 = f32[32,1,1280]{2,1,0:T(1,128)S(1)} all-to-all(f32[32,1,1280]{2,1,0:T(1,128)S(1)} %broadcast_in_dim.10), channel_id=1, replica_groups=mesh['group'=16,'row'=32] {'row'}, dimensions={0} | all-to-all | bytes 327680 | tf_op jit(solution)/shard_map/all_to_all | solution.py:121
  244.2 18.4 %reduce-scatter.2.cloned.1.call-done = bf16[4,128,128]{2,1,0:T(8,128)(2,1)} async-done(((bf16[4,4096,128]{2,1,0:T(8,128)(2,1)}), bf16[4,128,128]{2,1,0:T(8,128)(2,1)}) %reduce-scatter.2.cloned.1.call-update) | async-done | bytes 131088 | tf_op jit(solution)/shard_map/reduce_scatter | solution.py:101
  263.5 16.1 %all_to_all.84 = bf16[16,4,8,128]{3,2,1,0:T(8,128)(2,1)S(1)} all-to-all(bf16[16,4,8,128]{3,2,1,0:T(8,128)(2,1)S(1)} %copy_bitcast_fusion.3), channel_id=1, replica_groups=mesh['group'=16,'row'=32] {'group'}, dimensions={0} | all-to-all | bytes 262144 | tf_op jit(solution)/shard_map/all_to_all | solution.py:23
  279.7 12.1 %all_to_all.85 = f32[16,4,8,128]{3,2,1,0:T(8,128)S(1)} all-to-all(f32[16,4,8,128]{3,2,1,0:T(8,128)S(1)} %broadcast_in_dim.11), channel_id=1, replica_groups=mesh['group'=16,'row'=32] {'group'}, dimensions={0} | all-to-all | bytes 524288 | tf_op jit(solution)/shard_map/all_to_all | solution.py:25
  (65 shorter events, 14.2 us)
Async XLA Ops:
  7.2 12.7 %copy-start = (bf16[128,256]{1,0:T(8,128)(2,1)S(1)}, bf16[128,256]{1,0:T(8,128)(2,1)}, u32[]{:S(2)}) copy-start(bf16[128,256]{1,0:T(8,128)(2,1)} %param.15) | copy-start | bytes 196612
  7.2 101.5 %all-gather.2.cloned.1.call-start = ((), (), s32[]{:S(2)}) async-start(), calls=%async_computation.9 | async-start | bytes 4325376 | tf_op jit(solution)/shard_map/all_gather | solution.py:57
  19.8 50.0 %copy-start.2 = (bf16[3072,128]{1,0:T(8,128)(2,1)}, bf16[3072,128]{1,0:T(8,128)(2,1)S(1)}, u32[]{:S(2)}) copy-start(bf16[3072,128]{1,0:T(8,128)(2,1)S(1)} %scatter_custom_fusion) | copy-start | bytes 2359300
  19.8 13.8 %copy-start.5 = (f32[4096]{0:T(1024)S(1)}, f32[4096]{0:T(1024)}, u32[]{:S(2)}) copy-start(f32[4096]{0:T(1024)} %param.20) | copy-start | bytes 49156
  19.8 13.8 %copy-start.6 = (f32[2,4096]{1,0:T(2,128)S(1)}, f32[2,4096]{1,0:T(2,128)}, u32[]{:S(2)}) copy-start(f32[2,4096]{1,0:T(2,128)} %param.19) | copy-start | bytes 98308
  21.6 48.2 %all-to-all-start = ((bf16[16,192,256]{2,1,0:T(8,128)(2,1)}), bf16[16,192,256]{2,1,0:T(8,128)(2,1)S(1)}, u32[]{:S(2)}, u32[]{:S(2)}) async-start(bf16[16,192,256]{2,1,0:T(8,128)(2,1)} %bitcast.113), calls=%async_computation | async-start | bytes 3145728 | tf_op jit(solution)/shard_map/all_to_all | solution.py:53
  33.4 229.2 %reduce-scatter.2.cloned.1.call-start = ((), (), s32[]{:S(2)}) async-start(), calls=%async_computation.10 | async-start | bytes 4325376 | tf_op jit(solution)/shard_map/reduce_scatter | solution.py:101
  110.4 3.7 %copy-start.4 = (bf16[4,4096,128]{2,1,0:T(8,128)(2,1)S(1)}, bf16[4,4096,128]{2,1,0:T(8,128)(2,1)}, u32[]{:S(2)}) copy-start(bf16[4,4096,128]{2,1,0:T(8,128)(2,1)} %all-gather.2.cloned.1.call-done) | copy-start | bytes 12582916
  114.7 2.7 copy-start.8
  117.4 1.6 copy-start.7
  127.4 1.9 copy-start.1
  133.3 47.1 %copy-start.3 = (bf16[3072,128]{1,0:T(8,128)(2,1)S(1)}, bf16[3072,128]{1,0:T(8,128)(2,1)}, u32[]{:S(2)}) copy-start(bf16[3072,128]{1,0:T(8,128)(2,1)} %copy-done.2) | copy-start | bytes 2359300
  134.7 45.8 %all-to-all-start.1 = ((bf16[192,16,256]{2,0,1:T(8,128)(2,1)}), bf16[192,16,256]{2,0,1:T(8,128)(2,1)S(1)}, u32[]{:S(2)}, u32[]{:S(2)}) async-start(bf16[192,16,256]{2,0,1:T(8,128)(2,1)} %bitcast.112), calls=%async_computation.2 | async-start | bytes 3145728 | tf_op jit(solution)/shard_map/all_to_all | solution.py:105
  214.1 11.8 %all-to-all-start.4 = ((f32[16,1,16]{2,1,0:T(1,128)}), f32[16,1,16]{2,1,0:T(1,128)S(1)}, u32[]{:S(2)}, u32[]{:S(2)}) async-start(f32[16,1,16]{2,1,0:T(1,128)} %broadcast_in_dim.9), calls=%async_computation.5 | async-start | bytes 16384 | tf_op jit(solution)/shard_map/all_to_all | solution.py:17
Sparse Core Ops, SparseCore 0:
  12.0 96.5 all-gather.1
  127.6 134.9 reduce-scatter.1

commit v8 on v7

--- a/solution.py
+++ b/solution.py
@@ -15,15 +15,6 @@
     mine = jnp.sum(lax.all_to_all(pieces, axis, 0, 0, tiled=True), axis=0)
     spread = jnp.broadcast_to(mine[None], pieces.shape)
     return lax.all_to_all(spread, axis, 0, 0, tiled=True).reshape(partial.shape)
-
-
-def group_all_reduce(rows, groups):
-    stacked, height, width = rows.shape
-    pieces = rows.reshape(stacked, groups, height // groups, width).transpose(1, 0, 2, 3)
-    mine = jnp.sum(lax.all_to_all(pieces, "group", 0, 0, tiled=True).astype(jnp.float32), axis=0)
-    spread = jnp.broadcast_to(mine[None], pieces.shape)
-    gathered = lax.all_to_all(spread, "group", 0, 0, tiled=True)
-    return gathered.transpose(1, 0, 2, 3).reshape(rows.shape)
 
 
 def body(
@@ -98,8 +89,16 @@
         back = (back_wide + through).astype(jnp.bfloat16)
         up_parts[layer_index] = up_term
         down_parts[layer_index] = down_term
-    weight_rows = lax.psum_scatter(
-        jnp.stack(up_parts + down_parts).astype(jnp.bfloat16), "row", scatter_dimension=1, tiled=True
+    row_total = lax.axis_size("row")
+    width = first.shape[1]
+    rank = up_parts[0].shape[1]
+    block_rows = width // row_total
+    piece = block_rows // groups
+    slabs = jnp.stack(up_parts + down_parts).astype(jnp.bfloat16)
+    count = slabs.shape[0]
+    slabs = slabs.reshape(count, row_total, groups, piece, rank).transpose(0, 2, 1, 3, 4)
+    group_part = lax.psum_scatter(
+        slabs.reshape(count, width, rank), "group", scatter_dimension=1, tiled=True
     )
     first_grad = (first_grad + back.astype(jnp.float32)).astype(jnp.bfloat16)
     owner_grad = lax.all_to_all(first_grad, "group", split_axis=1, concat_axis=0, tiled=True)
@@ -128,9 +127,13 @@
         .transpose(1, 0, 2)
         .reshape(bias_all.shape)
     )
-    weight_rows, grad_proj, grad_bias = lax.optimization_barrier((weight_rows, grad_proj, grad_bias))
-    weight_sums = group_all_reduce(weight_rows, groups)
-    grad_up, grad_down = weight_sums[:layers], weight_sums[layers:]
+    group_part, grad_proj, grad_bias = lax.optimization_barrier((group_part, grad_proj, grad_bias))
+    row_pieces = group_part.reshape(count, row_total, piece, rank).transpose(1, 0, 2, 3)
+    mine = jnp.sum(lax.all_to_all(row_pieces, "row", 0, 0, tiled=True).astype(jnp.float32), axis=0)
+    spread = jnp.broadcast_to(mine[None], (groups,) + mine.shape)
+    gathered = lax.all_to_all(spread, "group", 0, 0, tiled=True)
+    blocks = gathered.transpose(1, 0, 2, 3).reshape(count, block_rows, rank)
+    grad_up, grad_down = blocks[:layers], blocks[layers:]
     return (logits, grad_down, grad_up, grad_bias, grad_proj)
 
 

time: 300 us -> 306 us (1.020)
  local copies, waits for them, and re-layouts: 8.21 us -> 17.1 us
  waiting for transfers between devices: 137 us -> 131 us
    reduce_scatter x1, waiting for transfers between devices: 18.4 us -> 0.01 us  [body(): lax.psum_scatter(slabs.reshape(count, width, rank), 'group', scatter_dime...]
    all_to_all x1, waiting for transfers between devices: 36.9 us -> 52.1 us  [body(): lax.all_to_all(first_grad, 'group', split_axis=1, concat_axis=0, tiled=True)]
    dot_general x0 -> x2, local copies, waits for them, and re-layouts: none -> 5.65 us  [the longest x1 3.15 us: body(): lax.dot_general(mix_grad, hidden, (((0,), (0,)), ((), ())), preferred_ele...]
    transpose x1 -> x2, local copies, waits for them, and re-layouts: 0.93 us -> 4.11 us  [the longest x1 3.12 us: body(): slabs.reshape(count, row_total, groups, piece, rank)]
  transfers between devices with their start and end apart: 5 -> 5, of which waited for: 5 -> 4; matrix products, arithmetic and copies ran while one was open for 7% -> 8% of each run, Pallas kernels for 0% -> 0%
where the time goes in v8:
time: 306 us; the launch traced here: 305 us
  waiting for transfers between devices  131 us (43%)
  blocking collectives  77.4 us (25%)
  starting transfers between devices  25.6 us (8%)
  matrix products  23.8 us (8%)
  local copies, waits for them, and re-layouts  17.1 us (6%)
  other arithmetic  15.6 us (5%)
  between operations  14.4 us (5%)
    all_to_all x1, waiting for transfers between devices, body(): lax.all_to_all(first_grad, 'group', split_axis=1, concat_axis=0, tiled=True)  52.1 us
    all_to_all x1, waiting for transfers between devices, body(): lax.all_to_all(projected, 'group', split_axis=0, concat_axis=1, tiled=True)  36.1 us
    all_gather x1, waiting for transfers between devices, body(): lax.all_gather(jnp.concatenate([down_weight, up_weight], axis=0), 'row',...  36.1 us
    all_to_all x1, blocking collectives, body(): lax.all_to_all(jnp.concatenate([proj_pieces, bias_pieces], axis=1), 'row'...  18.3 us
    all_to_all x1, blocking collectives, body(): lax.all_to_all(row_pieces, 'row', 0, 0, tiled=True).astype(jnp.float32)  17.7 us
    all_to_all x1, blocking collectives, body(): lax.all_to_all(jnp.broadcast_to(last[None], (row_count_axis,) + last.shap...  15.6 us
    all_to_all x1, blocking collectives, exchange_sum(): mine = jnp.sum(lax.all_to_all(pieces, axis, 0, 0, tiled=True), axis=0)  12.9 us
    all_to_all x1, blocking collectives, body(): gathered = lax.all_to_all(spread, 'group', 0, 0, tiled=True)  12.9 us
  transfers between devices with their start and end apart: 5, of which 4 were waited for; matrix products, arithmetic and copies ran while one was open for 8% of the time, Pallas kernels for 0%

profile of v8, /device:TPU:2, one launch (start us, length us, event | category | flops | bytes accessed | tf_op | source)
XLA Modules:
  0.0 305.4 jit_solution(2044302068018439409)
XLA Ops:
  10.9 8.9 %scatter_custom_fusion = bf16[3072,128]{1,0:T(8,128)(2,1)S(1)} fusion(s32[3072]{0:T(1024)S(1)} %bitcast.145, f32[3072,128]{1,0:T(8,128)} %param.11, f32[128]{0:T(128)S(1)} %get-tuple-element.21, f32[128]{0:T(128)S(1)} %get-tuple-element.20, bf16[]{:T(256)} %constant.0.clone.1), kind=kCustom, calls=%fused_computation.50 | custom fusion | flops 1179648 | bytes 2360322 | tf_op jit(solution)/shard_map/scatter | solution.py:40
  21.6 11.8 %all-to-all-start = ((bf16[16,192,256]{2,1,0:T(8,128)(2,1)}), bf16[16,192,256]{2,1,0:T(8,128)(2,1)S(1)}, u32[]{:S(2)}, u32[]{:S(2)}) async-start(bf16[16,192,256]{2,1,0:T(8,128)(2,1)} %bitcast.130), calls=%async_computation | async-start | bytes 3145728 | tf_op jit(solution)/shard_map/all_to_all | solution.py:44
  33.7 36.1 %all-to-all-done = bf16[16,192,256]{2,1,0:T(8,128)(2,1)S(1)} async-done(((bf16[16,192,256]{2,1,0:T(8,128)(2,1)}), bf16[16,192,256]{2,1,0:T(8,128)(2,1)S(1)}, u32[]{:S(2)}, u32[]{:S(2)}) %all-to-all-start) | async-done | bytes 1572896 | tf_op jit(solution)/shard_map/all_to_all | solution.py:44
  70.0 2.5 copy.55
  72.5 36.1 %all-gather.2.cloned.1.call-done = bf16[4,4096,128]{2,1,0:T(8,128)(2,1)} async-done(((bf16[4,128,128]{2,1,0:T(8,128)(2,1)}), bf16[4,4096,128]{2,1,0:T(8,128)(2,1)}) %all-gather.2.cloned.1.call-update) | async-done | bytes 4194320 | tf_op jit(solution)/shard_map/all_gather | solution.py:48
  108.6 1.8 convolution_convert_fusion.8
  110.4 3.7 %fusion.7 = (bf16[192,4096]{1,0:T(8,128)(2,1)S(1)}, f32[192,4096]{1,0:T(8,128)}) fusion(bf16[192,4096]{1,0:T(8,128)(2,1)S(1)} %bitcast.121, f32[4096]{0:T(1024)S(1)} %bitcast.142, bf16[192,128]{1,0:T(8,128)(2,1)S(1)} %convolution_convert_fusion.8, bf16[4,4096,128]{2,1,0:T(8,128)(2,1)} %all-gather.2.cloned.1.call-done), kind=kOutput, calls=%fused_computation.22 | convolution fusion | flops 205258752 | bytes 7405568 | tf_op jit(solution)/shard_map/dot_general | solution.py:56
  114.7 2.7 multiply_reduce_fusion
  120.3 2.3 convert_reduce_fusion.1
  122.5 1.8 convolution_convert_fusion.1
  124.3 3.1 %copy.54 = bf16[4096,192]{1,0:T(8,128)(2,1)S(1)} copy(bf16[4096,192]{0,1:T(8,128)(2,1)} %get-tuple-element.15) | data formatting | bytes 3145728 | tf_op jit(solution)/shard_map/dot_general | solution.py:76
  128.2 2.3 convolution_convert_fusion.5
  131.9 3.1 %copy.56 = bf16[4,16,32,8,128]{4,3,2,1,0:T(8,128)(2,1)} copy(bf16[4,16,32,8,128]{4,3,1,2,0:T(8,128)(2,1)S(1)} %maximum_bitcast_fusion) | data formatting | bytes 8388608 | tf_op jit(solution)/shard_map/transpose | solution.py:99
  135.0 1.9 copy-done.2
  136.9 4.0 %fusion.5 = bf16[192,4096]{1,0:T(8,128)(2,1)S(1)} fusion(f32[192,4096]{1,0:T(8,128)S(1)} %copy-done.2, bf16[192,128]{1,0:T(8,128)(2,1)S(1)} %convolution_convert_fusion.5, f32[192,4096]{1,0:T(8,128)} %get-tuple-element.25, f32[192,4096]{1,0:T(8,128)} %get-tuple-element.23, f32[192]{0:T(256)S(1)} %fusion.27, f32[4096]{0:T(1024)S(1)} %copy-done.9, ...), kind=kOutput, calls=%fused_computation.15 | convolution fusion | flops 209977344 | bytes 12124928 | tf_op jit(solution)/shard_map/dot_general | solution.py:86
  142.2 8.9 %all-to-all-start.1 = ((bf16[192,16,256]{2,0,1:T(8,128)(2,1)}), bf16[192,16,256]{2,0,1:T(8,128)(2,1)S(1)}, u32[]{:S(2)}, u32[]{:S(2)}) async-start(bf16[192,16,256]{2,0,1:T(8,128)(2,1)} %bitcast.129), calls=%async_computation.2 | async-start | bytes 3145728 | tf_op jit(solution)/shard_map/all_to_all | solution.py:104
  151.1 52.1 %all-to-all-done.1 = bf16[192,16,256]{2,0,1:T(8,128)(2,1)S(1)} async-done(((bf16[192,16,256]{2,0,1:T(8,128)(2,1)}), bf16[192,16,256]{2,0,1:T(8,128)(2,1)S(1)}, u32[]{:S(2)}, u32[]{:S(2)}) %all-to-all-start.1) | async-done | bytes 1572896 | tf_op jit(solution)/shard_map/all_to_all | solution.py:104
  203.9 18.3 %all_to_all.81 = f32[32,1,1280]{2,1,0:T(1,128)S(1)} all-to-all(f32[32,1,1280]{2,1,0:T(1,128)S(1)} %all_to_all.64), channel_id=1, replica_groups=mesh['group'=16,'row'=32] {'row'}, dimensions={0} | all-to-all | bytes 327680 | tf_op jit(solution)/shard_map/all_to_all | solution.py:115
  222.4 12.9 %all_to_all.82 = f32[16,1,16]{2,1,0:T(1,128)S(1)} all-to-all(f32[16,1,16]{2,1,0:T(1,128)S(1)} %all_to_all.66), channel_id=1, replica_groups=mesh['group'=16,'row'=32] {'group'}, dimensions={0} | all-to-all | bytes 2048 | tf_op jit(solution)/shard_map/all_to_all | solution.py:15
  236.0 4.8 %all-to-all-start.4 = ((f32[16,1,16]{2,1,0:T(1,128)}), f32[16,1,16]{2,1,0:T(1,128)S(1)}, u32[]{:S(2)}, u32[]{:S(2)}) async-start(f32[16,1,16]{2,1,0:T(1,128)} %broadcast_in_dim.9), calls=%async_computation.5 | async-start | bytes 16384 | tf_op jit(solution)/shard_map/all_to_all | solution.py:17
  240.7 7.1 %all-to-all-done.4 = f32[16,1,16]{2,1,0:T(1,128)S(1)} async-done(((f32[16,1,16]{2,1,0:T(1,128)}), f32[16,1,16]{2,1,0:T(1,128)S(1)}, u32[]{:S(2)}, u32[]{:S(2)}) %all-to-all-start.4) | async-done | bytes 1056 | tf_op jit(solution)/shard_map/all_to_all | solution.py:17
  249.1 15.6 %all_to_all.83 = f32[32,1,1280]{2,1,0:T(1,128)S(1)} all-to-all(f32[32,1,1280]{2,1,0:T(1,128)S(1)} %broadcast_in_dim.10), channel_id=1, replica_groups=mesh['group'=16,'row'=32] {'row'}, dimensions={0} | all-to-all | bytes 327680 | tf_op jit(solution)/shard_map/all_to_all | solution.py:120
  267.1 17.7 %all_to_all.84 = bf16[32,4,8,128]{3,2,1,0:T(8,128)(2,1)S(1)} all-to-all(bf16[32,4,8,128]{3,2,1,0:T(8,128)(2,1)S(1)} %copy_bitcast_fusion.2), channel_id=1, replica_groups=mesh['group'=16,'row'=32] {'row'}, dimensions={0} | all-to-all | bytes 524288 | tf_op jit(solution)/shard_map/all_to_all | solution.py:132
  284.9 12.9 %all_to_all.85 = f32[16,4,8,128]{3,2,1,0:T(8,128)S(1)} all-to-all(f32[16,4,8,128]{3,2,1,0:T(8,128)S(1)} %broadcast_in_dim.11), channel_id=1, replica_groups=mesh['group'=16,'row'=32] {'group'}, dimensions={0} | all-to-all | bytes 524288 | tf_op jit(solution)/shard_map/all_to_all | solution.py:134
  (77 shorter events, 18.6 us)
Async XLA Ops:
  7.2 12.7 %copy-start = (bf16[128,256]{1,0:T(8,128)(2,1)S(1)}, bf16[128,256]{1,0:T(8,128)(2,1)}, u32[]{:S(2)}) copy-start(bf16[128,256]{1,0:T(8,128)(2,1)} %param.15) | copy-start | bytes 196612
  7.2 101.5 %all-gather.2.cloned.1.call-start = ((), (), s32[]{:S(2)}) async-start(), calls=%async_computation.9 | async-start | bytes 4325376 | tf_op jit(solution)/shard_map/all_gather | solution.py:48
  19.8 50.0 %copy-start.4 = (bf16[3072,128]{1,0:T(8,128)(2,1)}, bf16[3072,128]{1,0:T(8,128)(2,1)S(1)}, u32[]{:S(2)}) copy-start(bf16[3072,128]{1,0:T(8,128)(2,1)S(1)} %scatter_custom_fusion) | copy-start | bytes 2359300
  19.8 13.8 %copy-start.9 = (f32[4096]{0:T(1024)S(1)}, f32[4096]{0:T(1024)}, u32[]{:S(2)}) copy-start(f32[4096]{0:T(1024)} %param.20) | copy-start | bytes 49156
  19.8 13.8 %copy-start.10 = (f32[2,4096]{1,0:T(2,128)S(1)}, f32[2,4096]{1,0:T(2,128)}, u32[]{:S(2)}) copy-start(f32[2,4096]{1,0:T(2,128)} %param.19) | copy-start | bytes 98308
  21.6 48.2 %all-to-all-start = ((bf16[16,192,256]{2,1,0:T(8,128)(2,1)}), bf16[16,192,256]{2,1,0:T(8,128)(2,1)S(1)}, u32[]{:S(2)}, u32[]{:S(2)}) async-start(bf16[16,192,256]{2,1,0:T(8,128)(2,1)} %bitcast.130), calls=%async_computation | async-start | bytes 3145728 | tf_op jit(solution)/shard_map/all_to_all | solution.py:44
  33.4 232.7 %reduce-scatter.2.cloned.1.call-start = ((), (), s32[]{:S(2)}) async-start(), calls=%async_computation.10 | async-start | bytes 4456448 | tf_op jit(solution)/shard_map/reduce_scatter | solution.py:100
  110.4 3.7 %copy-start.7 = (bf16[4,4096,128]{2,1,0:T(8,128)(2,1)S(1)}, bf16[4,4096,128]{2,1,0:T(8,128)(2,1)}, u32[]{:S(2)}) copy-start(bf16[4,4096,128]{2,1,0:T(8,128)(2,1)} %all-gather.2.cloned.1.call-done) | copy-start | bytes 12582916
  114.7 2.7 copy-start.12
  117.4 0.9 copy-start.11
  120.3 2.3 copy-start.1
  122.5 1.8 copy-start.6
  127.5 3.1 %copy-start.3 = (bf16[4096,192]{1,0:T(8,128)(2,1)S(1)}, bf16[4096,192]{1,0:T(8,128)(2,1)}, u32[]{:S(2)}) copy-start(bf16[4096,192]{1,0:T(8,128)(2,1)} %copy.55) | copy-start | bytes 4718596
  128.2 3.1 %copy-start.8 = (bf16[4096,128]{1,0:T(8,128)(2,1)S(1)}, bf16[4096,128]{1,0:T(8,128)(2,1)}, u32[]{:S(2)}) copy-start(bf16[4096,128]{1,0:T(8,128)(2,1)} %convolution_convert_fusion.1) | copy-start | bytes 3145732
  135.0 1.9 copy-start.2
  140.9 62.4 %copy-start.5 = (bf16[3072,128]{1,0:T(8,128)(2,1)S(1)}, bf16[3072,128]{1,0:T(8,128)(2,1)}, u32[]{:S(2)}) copy-start(bf16[3072,128]{1,0:T(8,128)(2,1)} %copy-done.4) | copy-start | bytes 2359300
  142.2 61.1 %all-to-all-start.1 = ((bf16[192,16,256]{2,0,1:T(8,128)(2,1)}), bf16[192,16,256]{2,0,1:T(8,128)(2,1)S(1)}, u32[]{:S(2)}, u32[]{:S(2)}) async-start(bf16[192,16,256]{2,0,1:T(8,128)(2,1)} %bitcast.129), calls=%async_computation.2 | async-start | bytes 3145728 | tf_op jit(solution)/shard_map/all_to_all | solution.py:104
  236.0 11.8 %all-to-all-start.4 = ((f32[16,1,16]{2,1,0:T(1,128)}), f32[16,1,16]{2,1,0:T(1,128)S(1)}, u32[]{:S(2)}, u32[]{:S(2)}) async-start(f32[16,1,16]{2,1,0:T(1,128)} %broadcast_in_dim.9), calls=%async_computation.5 | async-start | bytes 16384 | tf_op jit(solution)/shard_map/all_to_all | solution.py:17
Sparse Core Ops, SparseCore 0:
  12.0 96.5 all-gather.1
  135.1 107.1 reduce-scatter.1

commit v9 on v7

--- a/solution.py
+++ b/solution.py
@@ -85,7 +85,7 @@
         up_term = lax.dot_general(
             mix_grad, hidden, (((0,), (0,)), ((), ())), preferred_element_type=jnp.float32
         )
-        bias_terms[layer_index] = jnp.sum(mix_grad.astype(jnp.float32), axis=0)
+        bias_terms[layer_index] = mix_grad
         hidden_grad = jnp.dot(mix_grad, up_full, preferred_element_type=jnp.float32).astype(
             jnp.bfloat16
         )
@@ -98,9 +98,10 @@
         back = (back_wide + through).astype(jnp.bfloat16)
         up_parts[layer_index] = up_term
         down_parts[layer_index] = down_term
-    weight_rows = lax.psum_scatter(
-        jnp.stack(up_parts + down_parts).astype(jnp.bfloat16), "row", scatter_dimension=1, tiled=True
-    )
+    slab = jnp.stack(up_parts + down_parts).astype(jnp.bfloat16)
+    slab, bias_terms = lax.optimization_barrier((slab, bias_terms))
+    bias_terms = [jnp.sum(mix_grad.astype(jnp.float32), axis=0) for mix_grad in bias_terms]
+    weight_rows = lax.psum_scatter(slab, "row", scatter_dimension=1, tiled=True)
     first_grad = (first_grad + back.astype(jnp.float32)).astype(jnp.bfloat16)
     owner_grad = lax.all_to_all(first_grad, "group", split_axis=1, concat_axis=0, tiled=True)
     proj_term = lax.dot_general(

time: 300 us -> 300 us (level)
  the two profiles are of different devices: /device:TPU:2 before, /device:TPU:64 now
where the time goes in v9:
time: 300 us; the launch traced here: 299 us
  waiting for transfers between devices  139 us (46%)
  blocking collectives  74.9 us (25%)
  matrix products  25.6 us (9%)
  starting transfers between devices  23.6 us (8%)
  other arithmetic  15.4 us (5%)
  between operations  14.4 us (5%)
  local copies, waits for them, and re-layouts  6.34 us (2%)
    all_gather x1, waiting for transfers between devices, body(): lax.all_gather(jnp.concatenate([down_weight, up_weight], axis=0), 'row',...  38.5 us
    all_to_all x1, waiting for transfers between devices, body(): lax.all_to_all(first_grad, 'group', split_axis=1, concat_axis=0, tiled=True)  37.6 us
    all_to_all x1, waiting for transfers between devices, body(): lax.all_to_all(projected, 'group', split_axis=0, concat_axis=1, tiled=True)  37.3 us
    all_to_all x1, blocking collectives, body(): lax.all_to_all(jnp.concatenate([proj_pieces, bias_pieces], axis=1), 'row'...  19.3 us
    reduce_scatter x1, waiting for transfers between devices, body(): weight_rows = lax.psum_scatter(slab, 'row', scatter_dimension=1, tiled=True)  18.5 us
    all_to_all x1, blocking collectives, body(): lax.all_to_all(jnp.broadcast_to(last[None], (row_count_axis,) + last.shap...  15.6 us
    all_to_all x1, blocking collectives, group_all_reduce(): lax.all_to_all(pieces, 'group', 0, 0, tiled=True).astype(jnp.float32)  15.4 us
    all_to_all x1, blocking collectives, group_all_reduce(): gathered = lax.all_to_all(spread, 'group', 0, 0, tiled=True)  12.7 us
  transfers between devices with their start and end apart: 5, of which 5 were waited for; matrix products, arithmetic and copies ran while one was open for 8% of the time, Pallas kernels for 0%

profile of v9, /device:TPU:64, one launch (start us, length us, event | category | flops | bytes accessed | tf_op | source)
XLA Modules:
  0.0 299.4 jit_solution(4828361209377360769)
XLA Ops:
  7.2 1.5 pad_maximum_fusion.2
  8.8 1.4 fusion.17
  10.9 8.9 %scatter_custom_fusion = bf16[3072,128]{1,0:T(8,128)(2,1)S(1)} fusion(s32[3072]{0:T(1024)S(1)} %bitcast.123, f32[3072,128]{1,0:T(8,128)} %param.11, f32[128]{0:T(128)S(1)} %get-tuple-element.24, f32[128]{0:T(128)S(1)} %get-tuple-element.23, bf16[]{:T(256)} %constant.0.clone.1), kind=kCustom, calls=%fused_computation.52 | custom fusion | flops 1179648 | bytes 2360322 | tf_op jit(solution)/shard_map/scatter | solution.py:49
  19.9 1.7 convolution_convert_fusion.4
  21.6 10.9 %all-to-all-start = ((bf16[16,192,256]{2,1,0:T(8,128)(2,1)}), bf16[16,192,256]{2,1,0:T(8,128)(2,1)S(1)}, u32[]{:S(2)}, u32[]{:S(2)}) async-start(bf16[16,192,256]{2,1,0:T(8,128)(2,1)} %bitcast.6), calls=%async_computation | async-start | bytes 3145728 | tf_op jit(solution)/shard_map/all_to_all | solution.py:53
  32.8 37.3 %all-to-all-done = bf16[16,192,256]{2,1,0:T(8,128)(2,1)S(1)} async-done(((bf16[16,192,256]{2,1,0:T(8,128)(2,1)}), bf16[16,192,256]{2,1,0:T(8,128)(2,1)S(1)}, u32[]{:S(2)}, u32[]{:S(2)}) %all-to-all-start) | async-done | bytes 1572896 | tf_op jit(solution)/shard_map/all_to_all | solution.py:53
  70.3 38.5 %all-gather.2.cloned.1.call-done = bf16[4,4096,128]{2,1,0:T(8,128)(2,1)} async-done(((bf16[4,128,128]{2,1,0:T(8,128)(2,1)}), bf16[4,4096,128]{2,1,0:T(8,128)(2,1)}) %all-gather.2.cloned.1.call-update) | async-done | bytes 4194320 | tf_op jit(solution)/shard_map/all_gather | solution.py:57
  108.8 1.8 convolution_convert_fusion.8
  110.6 3.8 %fusion.11 = (bf16[192,4096]{1,0:T(8,128)(2,1)S(1)}, f32[192,4096]{1,0:T(8,128)}) fusion(bf16[192,4096]{1,0:T(8,128)(2,1)S(1)} %bitcast.104, f32[4096]{0:T(1024)S(1)} %bitcast.118, bf16[192,128]{1,0:T(8,128)(2,1)S(1)} %convolution_convert_fusion.8, bf16[4,4096,128]{2,1,0:T(8,128)(2,1)} %all-gather.2.cloned.1.call-done), kind=kOutput, calls=%fused_computation.28 | convolution fusion | flops 205258752 | bytes 7405568 | tf_op jit(solution)/shard_map/dot_general | solution.py:65
  115.0 2.7 multiply_reduce_fusion
  119.9 2.5 fusion.15
  125.3 2.2 pad_maximum_fusion
  127.5 4.9 %fusion.5 = bf16[192,4096]{1,0:T(8,128)(2,1)S(1)} fusion(f32[192,4096]{1,0:T(8,128)} %get-tuple-element.29, bf16[192,128]{1,0:T(8,128)(2,1)S(1)} %convolution_convert_fusion.5, f32[192,4096]{1,0:T(8,128)} %get-tuple-element.28, f32[192,4096]{1,0:T(8,128)} %get-tuple-element.26, f32[192]{0:T(256)S(1)} %fusion.26, f32[4096]{0:T(1024)S(1)} %copy-done.5, ...), kind=kOutput, calls=%fused_computation.15 | convolution fusion | flops 209977344 | bytes 12124928 | tf_op jit(solution)/shard_map/dot_general | solution.py:95
  133.8 7.8 %all-to-all-start.1 = ((bf16[192,16,256]{2,0,1:T(8,128)(2,1)}), bf16[192,16,256]{2,0,1:T(8,128)(2,1)}, u32[]{:S(2)}, u32[]{:S(2)}) async-start(bf16[192,16,256]{2,0,1:T(8,128)(2,1)} %bitcast.109), calls=%async_computation.2 | async-start | bytes 3145728 | tf_op jit(solution)/shard_map/all_to_all | solution.py:106
  142.1 37.6 %all-to-all-done.1 = bf16[192,16,256]{2,0,1:T(8,128)(2,1)} async-done(((bf16[192,16,256]{2,0,1:T(8,128)(2,1)}), bf16[192,16,256]{2,0,1:T(8,128)(2,1)}, u32[]{:S(2)}, u32[]{:S(2)}) %all-to-all-start.1) | async-done | bytes 1572896 | tf_op jit(solution)/shard_map/all_to_all | solution.py:106
  179.7 2.1 fusion.29
  182.0 19.3 %all_to_all.81 = f32[32,1,1280]{2,1,0:T(1,128)S(1)} all-to-all(f32[32,1,1280]{2,1,0:T(1,128)S(1)} %all_to_all.64), channel_id=1, replica_groups=mesh['group'=16,'row'=32] {'row'}, dimensions={0} | all-to-all | bytes 327680 | tf_op jit(solution)/shard_map/all_to_all | solution.py:117
  201.5 11.9 %all_to_all.82 = f32[16,1,16]{2,1,0:T(1,128)S(1)} all-to-all(f32[16,1,16]{2,1,0:T(1,128)S(1)} %all_to_all.66), channel_id=1, replica_groups=mesh['group'=16,'row'=32] {'group'}, dimensions={0} | all-to-all | bytes 2048 | tf_op jit(solution)/shard_map/all_to_all | solution.py:15
  214.0 4.7 %all-to-all-start.4 = ((f32[16,1,16]{2,1,0:T(1,128)}), f32[16,1,16]{2,1,0:T(1,128)S(1)}, u32[]{:S(2)}, u32[]{:S(2)}) async-start(f32[16,1,16]{2,1,0:T(1,128)} %broadcast_in_dim.9), calls=%async_computation.5 | async-start | bytes 16384 | tf_op jit(solution)/shard_map/all_to_all | solution.py:17
  218.7 7.1 %all-to-all-done.4 = f32[16,1,16]{2,1,0:T(1,128)S(1)} async-done(((f32[16,1,16]{2,1,0:T(1,128)}), f32[16,1,16]{2,1,0:T(1,128)S(1)}, u32[]{:S(2)}, u32[]{:S(2)}) %all-to-all-start.4) | async-done | bytes 1056 | tf_op jit(solution)/shard_map/all_to_all | solution.py:17
  227.2 15.6 %all_to_all.83 = f32[32,1,1280]{2,1,0:T(1,128)S(1)} all-to-all(f32[32,1,1280]{2,1,0:T(1,128)S(1)} %broadcast_in_dim.10), channel_id=1, replica_groups=mesh['group'=16,'row'=32] {'row'}, dimensions={0} | all-to-all | bytes 327680 | tf_op jit(solution)/shard_map/all_to_all | solution.py:122
  244.2 18.5 %reduce-scatter.2.cloned.1.call-done = bf16[4,128,128]{2,1,0:T(8,128)(2,1)} async-done(((bf16[4,4096,128]{2,1,0:T(8,128)(2,1)}), bf16[4,128,128]{2,1,0:T(8,128)(2,1)}) %reduce-scatter.2.cloned.1.call-update) | async-done | bytes 131088 | tf_op jit(solution)/shard_map/reduce_scatter | solution.py:104
  263.7 15.4 %all_to_all.84 = bf16[16,4,8,128]{3,2,1,0:T(8,128)(2,1)S(1)} all-to-all(bf16[16,4,8,128]{3,2,1,0:T(8,128)(2,1)S(1)} %copy_bitcast_fusion.3), channel_id=1, replica_groups=mesh['group'=16,'row'=32] {'group'}, dimensions={0} | all-to-all | bytes 262144 | tf_op jit(solution)/shard_map/all_to_all | solution.py:23
  279.2 12.7 %all_to_all.85 = f32[16,4,8,128]{3,2,1,0:T(8,128)S(1)} all-to-all(f32[16,4,8,128]{3,2,1,0:T(8,128)S(1)} %broadcast_in_dim.11), channel_id=1, replica_groups=mesh['group'=16,'row'=32] {'group'}, dimensions={0} | all-to-all | bytes 524288 | tf_op jit(solution)/shard_map/all_to_all | solution.py:25
  (65 shorter events, 14.1 us)
Async XLA Ops:
  7.2 12.7 %copy-start = (bf16[128,256]{1,0:T(8,128)(2,1)S(1)}, bf16[128,256]{1,0:T(8,128)(2,1)}, u32[]{:S(2)}) copy-start(bf16[128,256]{1,0:T(8,128)(2,1)} %param.15) | copy-start | bytes 196612
  7.2 101.7 %all-gather.2.cloned.1.call-start = ((), (), s32[]{:S(2)}) async-start(), calls=%async_computation.9 | async-start | bytes 4325376 | tf_op jit(solution)/shard_map/all_gather | solution.py:57
  19.8 1.8 copy-start.3
  19.8 12.9 %copy-start.5 = (f32[4096]{0:T(1024)S(1)}, f32[4096]{0:T(1024)}, u32[]{:S(2)}) copy-start(f32[4096]{0:T(1024)} %param.20) | copy-start | bytes 49156
  19.8 12.9 %copy-start.6 = (f32[2,4096]{1,0:T(2,128)S(1)}, f32[2,4096]{1,0:T(2,128)}, u32[]{:S(2)}) copy-start(f32[2,4096]{1,0:T(2,128)} %param.19) | copy-start | bytes 98308
  21.6 48.5 %all-to-all-start = ((bf16[16,192,256]{2,1,0:T(8,128)(2,1)}), bf16[16,192,256]{2,1,0:T(8,128)(2,1)S(1)}, u32[]{:S(2)}, u32[]{:S(2)}) async-start(bf16[16,192,256]{2,1,0:T(8,128)(2,1)} %bitcast.6), calls=%async_computation | async-start | bytes 3145728 | tf_op jit(solution)/shard_map/all_to_all | solution.py:53
  32.5 230.2 %reduce-scatter.2.cloned.1.call-start = ((), (), s32[]{:S(2)}) async-start(), calls=%async_computation.10 | async-start | bytes 4325376 | tf_op jit(solution)/shard_map/reduce_scatter | solution.py:104
  110.6 3.8 %copy-start.4 = (bf16[4,4096,128]{2,1,0:T(8,128)(2,1)S(1)}, bf16[4,4096,128]{2,1,0:T(8,128)(2,1)}, u32[]{:S(2)}) copy-start(bf16[4,4096,128]{2,1,0:T(8,128)(2,1)} %all-gather.2.cloned.1.call-done) | copy-start | bytes 12582916
  115.0 2.7 copy-start.8
  117.7 0.8 copy-start.7
  122.4 2.1 copy-start.1
  132.4 9.1 %copy-start.2 = (bf16[192,4096]{1,0:T(8,128)(2,1)S(1)}, bf16[192,4096]{1,0:T(8,128)(2,1)}, u32[]{:S(2)}) copy-start(bf16[192,4096]{1,0:T(8,128)(2,1)} %copy-done.1) | copy-start | bytes 4718596
  133.8 45.9 %all-to-all-start.1 = ((bf16[192,16,256]{2,0,1:T(8,128)(2,1)}), bf16[192,16,256]{2,0,1:T(8,128)(2,1)}, u32[]{:S(2)}, u32[]{:S(2)}) async-start(bf16[192,16,256]{2,0,1:T(8,128)(2,1)} %bitcast.109), calls=%async_computation.2 | async-start | bytes 3145728 | tf_op jit(solution)/shard_map/all_to_all | solution.py:106
  214.0 11.8 %all-to-all-start.4 = ((f32[16,1,16]{2,1,0:T(1,128)}), f32[16,1,16]{2,1,0:T(1,128)S(1)}, u32[]{:S(2)}, u32[]{:S(2)}) async-start(f32[16,1,16]{2,1,0:T(1,128)} %broadcast_in_dim.9), calls=%async_computation.5 | async-start | bytes 16384 | tf_op jit(solution)/shard_map/all_to_all | solution.py:17
Sparse Core Ops, SparseCore 0:
  12.0 96.7 all-gather.1
  127.7 135.0 reduce-scatter.1

commit v10 on v9

--- a/solution.py
+++ b/solution.py
@@ -21,8 +21,8 @@
     stacked, height, width = rows.shape
     pieces = rows.reshape(stacked, groups, height // groups, width).transpose(1, 0, 2, 3)
     mine = jnp.sum(lax.all_to_all(pieces, "group", 0, 0, tiled=True).astype(jnp.float32), axis=0)
-    spread = jnp.broadcast_to(mine[None], pieces.shape)
-    gathered = lax.all_to_all(spread, "group", 0, 0, tiled=True)
+    spread = jnp.broadcast_to(mine.astype(jnp.bfloat16)[None], pieces.shape)
+    gathered = lax.all_to_all(spread, "group", 0, 0, tiled=True).astype(jnp.float32)
     return gathered.transpose(1, 0, 2, 3).reshape(rows.shape)
 
 

time: 300 us -> 300 us (level)
  the two profiles are of different devices: /device:TPU:64 before, /device:TPU:2 now
where the time goes in v10:
time: 300 us; the launch traced here: 299 us
  waiting for transfers between devices  136 us (45%)
  blocking collectives  76 us (25%)
  starting transfers between devices  25.6 us (9%)
  matrix products  25.6 us (9%)
  other arithmetic  15.4 us (5%)
  between operations  14.4 us (5%)
  local copies, waits for them, and re-layouts  6.32 us (2%)
    all_gather x1, waiting for transfers between devices, body(): lax.all_gather(jnp.concatenate([down_weight, up_weight], axis=0), 'row',...  38.7 us
    all_to_all x1, waiting for transfers between devices, body(): lax.all_to_all(first_grad, 'group', split_axis=1, concat_axis=0, tiled=True)  36.5 us
    all_to_all x1, waiting for transfers between devices, body(): lax.all_to_all(projected, 'group', split_axis=0, concat_axis=1, tiled=True)  36.1 us
    all_to_all x1, blocking collectives, body(): lax.all_to_all(jnp.concatenate([proj_pieces, bias_pieces], axis=1), 'row'...  18.6 us
    reduce_scatter x1, waiting for transfers between devices, body(): weight_rows = lax.psum_scatter(slab, 'row', scatter_dimension=1, tiled=True)  17.1 us
    all_to_all x1, blocking collectives, group_all_reduce(): lax.all_to_all(pieces, 'group', 0, 0, tiled=True).astype(jnp.float32)  16.1 us
    all_to_all x1, blocking collectives, body(): lax.all_to_all(jnp.broadcast_to(last[None], (row_count_axis,) + last.shap...  16 us
    all_to_all x1, blocking collectives, exchange_sum(): mine = jnp.sum(lax.all_to_all(pieces, axis, 0, 0, tiled=True), axis=0)  13.7 us
  transfers between devices with their start and end apart: 5, of which 5 were waited for; matrix products, arithmetic and copies ran while one was open for 8% of the time, Pallas kernels for 0%

profile of v10, /device:TPU:2, one launch (start us, length us, event | category | flops | bytes accessed | tf_op | source)
XLA Modules:
  0.0 298.8 jit_solution(5511135230182900880)
XLA Ops:
  7.2 1.5 pad_maximum_fusion.2
  8.8 1.4 fusion.17
  10.9 8.9 %scatter_custom_fusion = bf16[3072,128]{1,0:T(8,128)(2,1)S(1)} fusion(s32[3072]{0:T(1024)S(1)} %bitcast.121, f32[3072,128]{1,0:T(8,128)} %param.11, f32[128]{0:T(128)S(1)} %get-tuple-element.24, f32[128]{0:T(128)S(1)} %get-tuple-element.23, bf16[]{:T(256)} %constant.1.clone.1), kind=kCustom, calls=%fused_computation.52 | custom fusion | flops 1179648 | bytes 2360322 | tf_op jit(solution)/shard_map/scatter | solution.py:49
  19.9 1.7 convolution_convert_fusion.4
  21.6 11.8 %all-to-all-start = ((bf16[16,192,256]{2,1,0:T(8,128)(2,1)}), bf16[16,192,256]{2,1,0:T(8,128)(2,1)S(1)}, u32[]{:S(2)}, u32[]{:S(2)}) async-start(bf16[16,192,256]{2,1,0:T(8,128)(2,1)} %bitcast.6), calls=%async_computation | async-start | bytes 3145728 | tf_op jit(solution)/shard_map/all_to_all | solution.py:53
  33.7 36.1 %all-to-all-done = bf16[16,192,256]{2,1,0:T(8,128)(2,1)S(1)} async-done(((bf16[16,192,256]{2,1,0:T(8,128)(2,1)}), bf16[16,192,256]{2,1,0:T(8,128)(2,1)S(1)}, u32[]{:S(2)}, u32[]{:S(2)}) %all-to-all-start) | async-done | bytes 1572896 | tf_op jit(solution)/shard_map/all_to_all | solution.py:53
  70.0 38.7 %all-gather.2.cloned.1.call-done = bf16[4,4096,128]{2,1,0:T(8,128)(2,1)} async-done(((bf16[4,128,128]{2,1,0:T(8,128)(2,1)}), bf16[4,4096,128]{2,1,0:T(8,128)(2,1)}) %all-gather.2.cloned.1.call-update) | async-done | bytes 4194320 | tf_op jit(solution)/shard_map/all_gather | solution.py:57
  108.6 1.8 convolution_convert_fusion.8
  110.4 3.8 %fusion.11 = (bf16[192,4096]{1,0:T(8,128)(2,1)S(1)}, f32[192,4096]{1,0:T(8,128)}) fusion(bf16[192,4096]{1,0:T(8,128)(2,1)S(1)} %bitcast.103, f32[4096]{0:T(1024)S(1)} %bitcast.116, bf16[192,128]{1,0:T(8,128)(2,1)S(1)} %convolution_convert_fusion.8, bf16[4,4096,128]{2,1,0:T(8,128)(2,1)} %all-gather.2.cloned.1.call-done), kind=kOutput, calls=%fused_computation.28 | convolution fusion | flops 205258752 | bytes 7405568 | tf_op jit(solution)/shard_map/dot_general | solution.py:65
  114.8 2.7 multiply_reduce_fusion
  119.7 2.5 fusion.15
  125.1 2.2 pad_maximum_fusion
  127.3 4.9 %fusion.5 = bf16[192,4096]{1,0:T(8,128)(2,1)S(1)} fusion(f32[192,4096]{1,0:T(8,128)} %get-tuple-element.29, bf16[192,128]{1,0:T(8,128)(2,1)S(1)} %convolution_convert_fusion.5, f32[192,4096]{1,0:T(8,128)} %get-tuple-element.28, f32[192,4096]{1,0:T(8,128)} %get-tuple-element.26, f32[192]{0:T(256)S(1)} %fusion.26, f32[4096]{0:T(1024)S(1)} %copy-done.5, ...), kind=kOutput, calls=%fused_computation.15 | convolution fusion | flops 209977344 | bytes 12124928 | tf_op jit(solution)/shard_map/dot_general | solution.py:95
  133.6 8.9 %all-to-all-start.1 = ((bf16[192,16,256]{2,0,1:T(8,128)(2,1)}), bf16[192,16,256]{2,0,1:T(8,128)(2,1)}, u32[]{:S(2)}, u32[]{:S(2)}) async-start(bf16[192,16,256]{2,0,1:T(8,128)(2,1)} %bitcast.108), calls=%async_computation.2 | async-start | bytes 3145728 | tf_op jit(solution)/shard_map/all_to_all | solution.py:106
  143.0 36.5 %all-to-all-done.1 = bf16[192,16,256]{2,0,1:T(8,128)(2,1)} async-done(((bf16[192,16,256]{2,0,1:T(8,128)(2,1)}), bf16[192,16,256]{2,0,1:T(8,128)(2,1)}, u32[]{:S(2)}, u32[]{:S(2)}) %all-to-all-start.1) | async-done | bytes 1572896 | tf_op jit(solution)/shard_map/all_to_all | solution.py:106
  179.5 2.1 fusion.29
  181.8 18.6 %all_to_all.81 = f32[32,1,1280]{2,1,0:T(1,128)S(1)} all-to-all(f32[32,1,1280]{2,1,0:T(1,128)S(1)} %all_to_all.64), channel_id=1, replica_groups=mesh['group'=16,'row'=32] {'row'}, dimensions={0} | all-to-all | bytes 327680 | tf_op jit(solution)/shard_map/all_to_all | solution.py:117
  200.6 13.7 %all_to_all.82 = f32[16,1,16]{2,1,0:T(1,128)S(1)} all-to-all(f32[16,1,16]{2,1,0:T(1,128)S(1)} %all_to_all.66), channel_id=1, replica_groups=mesh['group'=16,'row'=32] {'group'}, dimensions={0} | all-to-all | bytes 2048 | tf_op jit(solution)/shard_map/all_to_all | solution.py:15
  214.9 4.7 %all-to-all-start.4 = ((f32[16,1,16]{2,1,0:T(1,128)}), f32[16,1,16]{2,1,0:T(1,128)S(1)}, u32[]{:S(2)}, u32[]{:S(2)}) async-start(f32[16,1,16]{2,1,0:T(1,128)} %broadcast_in_dim.9), calls=%async_computation.5 | async-start | bytes 16384 | tf_op jit(solution)/shard_map/all_to_all | solution.py:17
  219.7 7.1 %all-to-all-done.4 = f32[16,1,16]{2,1,0:T(1,128)S(1)} async-done(((f32[16,1,16]{2,1,0:T(1,128)}), f32[16,1,16]{2,1,0:T(1,128)S(1)}, u32[]{:S(2)}, u32[]{:S(2)}) %all-to-all-start.4) | async-done | bytes 1056 | tf_op jit(solution)/shard_map/all_to_all | solution.py:17
  228.1 16.0 %all_to_all.83 = f32[32,1,1280]{2,1,0:T(1,128)S(1)} all-to-all(f32[32,1,1280]{2,1,0:T(1,128)S(1)} %broadcast_in_dim.10), channel_id=1, replica_groups=mesh['group'=16,'row'=32] {'row'}, dimensions={0} | all-to-all | bytes 327680 | tf_op jit(solution)/shard_map/all_to_all | solution.py:122
  245.4 17.1 %reduce-scatter.2.cloned.1.call-done = bf16[4,128,128]{2,1,0:T(8,128)(2,1)} async-done(((bf16[4,4096,128]{2,1,0:T(8,128)(2,1)}), bf16[4,128,128]{2,1,0:T(8,128)(2,1)}) %reduce-scatter.2.cloned.1.call-update) | async-done | bytes 131088 | tf_op jit(solution)/shard_map/reduce_scatter | solution.py:104
  263.4 16.1 %all_to_all.84 = bf16[16,4,8,128]{3,2,1,0:T(8,128)(2,1)S(1)} all-to-all(bf16[16,4,8,128]{3,2,1,0:T(8,128)(2,1)S(1)} %copy_bitcast_fusion.2), channel_id=1, replica_groups=mesh['group'=16,'row'=32] {'group'}, dimensions={0} | all-to-all | bytes 262144 | tf_op jit(solution)/shard_map/all_to_all | solution.py:23
  279.6 11.6 %all_to_all.85 = bf16[16,4,8,128]{3,2,1,0:T(8,128)(2,1)S(1)} all-to-all(bf16[16,4,8,128]{3,2,1,0:T(8,128)(2,1)S(1)} %broadcast_in_dim.11), channel_id=1, replica_groups=mesh['group'=16,'row'=32] {'group'}, dimensions={0} | all-to-all | bytes 262144 | tf_op jit(solution)/shard_map/all_to_all | solution.py:25
  (65 shorter events, 14.1 us)
Async XLA Ops:
  7.2 12.7 %copy-start = (bf16[128,256]{1,0:T(8,128)(2,1)S(1)}, bf16[128,256]{1,0:T(8,128)(2,1)}, u32[]{:S(2)}) copy-start(bf16[128,256]{1,0:T(8,128)(2,1)} %param.15) | copy-start | bytes 196612
  7.2 101.5 %all-gather.2.cloned.1.call-start = ((), (), s32[]{:S(2)}) async-start(), calls=%async_computation.9 | async-start | bytes 4325376 | tf_op jit(solution)/shard_map/all_gather | solution.py:57
  19.8 1.8 copy-start.3
  19.8 13.8 %copy-start.5 = (f32[4096]{0:T(1024)S(1)}, f32[4096]{0:T(1024)}, u32[]{:S(2)}) copy-start(f32[4096]{0:T(1024)} %param.20) | copy-start | bytes 49156
  19.8 13.8 %copy-start.6 = (f32[2,4096]{1,0:T(2,128)S(1)}, f32[2,4096]{1,0:T(2,128)}, u32[]{:S(2)}) copy-start(f32[2,4096]{1,0:T(2,128)} %param.19) | copy-start | bytes 98308
  21.6 48.2 %all-to-all-start = ((bf16[16,192,256]{2,1,0:T(8,128)(2,1)}), bf16[16,192,256]{2,1,0:T(8,128)(2,1)S(1)}, u32[]{:S(2)}, u32[]{:S(2)}) async-start(bf16[16,192,256]{2,1,0:T(8,128)(2,1)} %bitcast.6), calls=%async_computation | async-start | bytes 3145728 | tf_op jit(solution)/shard_map/all_to_all | solution.py:53
  33.4 229.1 %reduce-scatter.2.cloned.1.call-start = ((), (), s32[]{:S(2)}) async-start(), calls=%async_computation.10 | async-start | bytes 4325376 | tf_op jit(solution)/shard_map/reduce_scatter | solution.py:104
  110.4 3.8 %copy-start.4 = (bf16[4,4096,128]{2,1,0:T(8,128)(2,1)S(1)}, bf16[4,4096,128]{2,1,0:T(8,128)(2,1)}, u32[]{:S(2)}) copy-start(bf16[4,4096,128]{2,1,0:T(8,128)(2,1)} %all-gather.2.cloned.1.call-done) | copy-start | bytes 12582916
  114.8 2.7 copy-start.8
  117.5 0.8 copy-start.7
  122.2 2.1 copy-start.1
  132.3 10.2 %copy-start.2 = (bf16[192,4096]{1,0:T(8,128)(2,1)S(1)}, bf16[192,4096]{1,0:T(8,128)(2,1)}, u32[]{:S(2)}) copy-start(bf16[192,4096]{1,0:T(8,128)(2,1)} %copy-done.1) | copy-start | bytes 4718596
  133.6 45.9 %all-to-all-start.1 = ((bf16[192,16,256]{2,0,1:T(8,128)(2,1)}), bf16[192,16,256]{2,0,1:T(8,128)(2,1)}, u32[]{:S(2)}, u32[]{:S(2)}) async-start(bf16[192,16,256]{2,0,1:T(8,128)(2,1)} %bitcast.108), calls=%async_computation.2 | async-start | bytes 3145728 | tf_op jit(solution)/shard_map/all_to_all | solution.py:106
  214.9 11.8 %all-to-all-start.4 = ((f32[16,1,16]{2,1,0:T(1,128)}), f32[16,1,16]{2,1,0:T(1,128)S(1)}, u32[]{:S(2)}, u32[]{:S(2)}) async-start(f32[16,1,16]{2,1,0:T(1,128)} %broadcast_in_dim.9), calls=%async_computation.5 | async-start | bytes 16384 | tf_op jit(solution)/shard_map/all_to_all | solution.py:17
Sparse Core Ops, SparseCore 0:
  12.0 96.6 all-gather.1
  127.5 135.0 reduce-scatter.1
